TPU v7x, 128 devices: a whole 4x4x4 slice. The times are simulated.
128 devices in a mesh: req: 32 (over y, z, core), hid: 4 (over x).
Axes of the slice: x: 4, y: 4, z: 4, core: 2. Of those that a mesh axis runs over, the one named last changes fastest.
Arguments:
- hidden_in: bfloat16 [32, 512, 1536], P('req', 'hid'), may hold values from -6 to 6
- queries: bfloat16 [32, 512, 1536], P('req', 'hid'), may hold values from -4 to 4
- cache_keys: bfloat16 [32, 4096, 256], P('req', 'hid'), may hold values from -6 to 6
- cache_values: bfloat16 [32, 4096, 256], P('req', 'hid'), may hold values from -6 to 6
- lengths: int32 [32], P('req'), may hold values from 256 to 4096, as said below
- routes: int32 [32, 512, 4], P('req'), may hold values from 0 to 31, all different within a row; in each aligned block of 128 rows (0 to 127, 128 to 255, ..., all dimensions but the last counted through in order) at most 32 rows name the same one
- attn_gain: float32 [1536], replicated, may hold values from 0.25 to 1.75
- key_proj: bfloat16 [1536, 256], replicated, may hold values from -0.15625 to 0.15625
- value_proj: bfloat16 [1536, 256], replicated, may hold values from -0.15625 to 0.15625
- out_proj: bfloat16 [1536, 1536], replicated, may hold values from -0.15625 to 0.15625
- moe_gain: float32 [1536], replicated, may hold values from 0.25 to 1.75
- router: bfloat16 [1536, 32], replicated, may hold values from -0.3125 to 0.3125
- gate_up: bfloat16 [32, 2, 1536, 768], P('req', None, None, 'hid'), may hold values from -0.15625 to 0.15625
- down_proj: bfloat16 [32, 768, 1536], P('req', 'hid'), may hold values from -0.21875 to 0.21875
Outputs:
- layer_out: bfloat16 [32, 512, 1536], P('req', 'hid')
- new_keys: bfloat16 [32, 512, 256], P('req', 'hid')
- new_values: bfloat16 [32, 512, 256], P('req', 'hid')
Inputs may be any that keep to these rules, and one draw needn't show every extreme that they name: `routes`: each row names 4 different experts; within each aligned block of 128 tokens (the tokens of one device) no expert is named by more than 32 tokens, and in some block one expert is named by exactly 32. `lengths`: some request holds exactly 4096 cached positions and some other exactly 256.
All inputs are finite; a program needn't handle non-finite values.
Results may differ from a plain program's by a relative error of at most 0.015.
Values may be sent and summed in bfloat16 or wider, within the bound.
No kernel may reach another device: no remote copies, remote signals or barrier semaphores. Data moves between devices by JAX's collectives and lax.ppermute only.
A program may use at most 128 MiB of HBM per device.

v0:
```python
import jax
import jax.numpy as jnp
from jax import lax
from jax.sharding import PartitionSpec as P
from jax.experimental import pallas as pl
from jax.experimental.pallas import tpu as pltpu
import functools

QH = 12
KVH = 2
HD = 128


EPS = 1e-06
MASKED_SCORE = -1e30
KEY_BLOCK = 512


def normalize(row_data, gain_vector):
    row_data = row_data.astype(jnp.float32)
    return (
        row_data
        * lax.rsqrt(jnp.mean(row_data * row_data, axis=-1, keepdims=True) + EPS)
        * gain_vector
    )


def absorb(state_now, grouped, key_rows, value_rows, visible):
    row_max, totals, accumulated = state_now
    scores = jnp.einsum(
        "tgsd,kgd->gstk", grouped, key_rows.reshape(-1, KVH, HD), preferred_element_type=jnp.float32
    ) * HD ** (-0.5)
    scores = jnp.where(visible, scores, MASKED_SCORE)
    new_max = jnp.maximum(row_max, jnp.max(scores, axis=-1))
    weights = jnp.where(visible, jnp.exp(scores - new_max[..., None]), 0.0)
    rescale = jnp.exp(row_max - new_max)
    totals = totals * rescale + jnp.sum(weights, axis=-1)
    accumulated = accumulated * rescale[..., None] + jnp.einsum(
        "gstk,kgd->gstd",
        weights.astype(jnp.bfloat16),
        value_rows.reshape(-1, KVH, HD),
        preferred_element_type=jnp.float32,
    )
    return (new_max, totals, accumulated)


def cache_block(state_now, grouped, key_rows, value_rows, first_pos, length):
    positions = first_pos + jnp.arange(key_rows.shape[0], dtype=jnp.int32)
    visible = (positions < length)[None, :]
    return lax.cond(
        first_pos < length,
        lambda current: absorb(current, grouped, key_rows, value_rows, visible),
        lambda current: current,
        state_now,
    )


def span_block(state_now, grouped, key_rows, value_rows, first_pos, query_pos):
    positions = first_pos + jnp.arange(key_rows.shape[0], dtype=jnp.int32)
    visible = positions[None, :] <= query_pos[:, None]
    return lax.cond(
        first_pos <= query_pos[-1],
        lambda current: absorb(current, grouped, key_rows, value_rows, visible),
        lambda current: current,
        state_now,
    )


def block_size(extent):
    return max(min(KEY_BLOCK, extent), extent // 8)


def empty_state(query_count):
    group_size = QH // KVH
    return (
        jnp.full((KVH, group_size, query_count), MASKED_SCORE, jnp.float32),
        jnp.zeros((KVH, group_size, query_count), jnp.float32),
        jnp.zeros((KVH, group_size, query_count, HD), jnp.float32),
    )


def attention_kernel(token_count, scalars, q_ref, k_ref, v_ref, o_ref, m_ref, l_ref, acc_ref):
    length = scalars[0]
    hid_index = scalars[1]
    parts, part_rows, _ = k_ref.shape
    rows = q_ref.shape[1]
    cache_rows = part_rows - token_count
    q = q_ref[0]
    m_ref[...] = jnp.full(m_ref.shape, MASKED_SCORE, jnp.float32)
    l_ref[...] = jnp.zeros(l_ref.shape, jnp.float32)
    acc_ref[...] = jnp.zeros(acc_ref.shape, jnp.float32)
    blocks = []
    for part in range(parts):
        for first in range(0, cache_rows, KEY_BLOCK):
            blocks.append((part, first, min(KEY_BLOCK, cache_rows - first), True))
        blocks.append((part, cache_rows, token_count, False))

    def live(part, first, is_cache):
        if is_cache:
            return part * cache_rows + first < length
        return part <= hid_index

    def visible(part, first, size, is_cache):
        if is_cache:
            pos = part * cache_rows + first + lax.broadcasted_iota(jnp.int32, (1, size), 1)
            return pos < length
        key_pos = part * token_count + lax.broadcasted_iota(jnp.int32, (1, size), 1)
        row_ids = lax.broadcasted_iota(jnp.int32, (rows, 1), 0)
        return key_pos <= hid_index * token_count + row_ids % token_count

    def scores(part, first, size):
        k = k_ref[part, pl.ds(first, size), :]
        raw = lax.dot_general(q, k, (((1,), (1,)), ((), ())), preferred_element_type=jnp.float32)
        return raw * HD ** (-0.5)

    for part, first, size, is_cache in blocks:

        @pl.when(live(part, first, is_cache))
        def _():
            s = jnp.where(visible(part, first, size, is_cache), scores(part, first, size), MASKED_SCORE)
            m_ref[...] = jnp.maximum(m_ref[...], jnp.max(s, axis=-1, keepdims=True))

    for part, first, size, is_cache in blocks:

        @pl.when(live(part, first, is_cache))
        def _():
            s = scores(part, first, size)
            w = jnp.where(visible(part, first, size, is_cache), jnp.exp(s - m_ref[...]), 0.0)
            l_ref[...] += jnp.sum(w, axis=-1, keepdims=True)
            v = v_ref[part, pl.ds(first, size), :]
            acc_ref[...] += jnp.dot(w.astype(jnp.bfloat16), v, preferred_element_type=jnp.float32)

    o_ref[0] = (acc_ref[...] / l_ref[...]).astype(o_ref.dtype)


def attention(grouped, all_keys, all_values, length, hid_index, token_count, interpret=False):
    groups, rows, head = grouped.shape
    parts, part_rows, _ = all_keys.shape
    scalars = jnp.stack([length, hid_index]).astype(jnp.int32)
    kv_spec = pl.BlockSpec((parts, part_rows, head), lambda g, s: (0, 0, g))
    row_spec = pl.BlockSpec((1, rows, head), lambda g, s: (g, 0, 0))
    return pl.pallas_call(
        functools.partial(attention_kernel, token_count),
        out_shape=jax.ShapeDtypeStruct((groups, rows, head), jnp.bfloat16),
        grid_spec=pltpu.PrefetchScalarGridSpec(
            num_scalar_prefetch=1,
            grid=(groups,),
            in_specs=[row_spec, kv_spec, kv_spec],
            out_specs=row_spec,
            scratch_shapes=[
                pltpu.VMEM((rows, 1), jnp.float32),
                pltpu.VMEM((rows, 1), jnp.float32),
                pltpu.VMEM((rows, head), jnp.float32),
            ],
        ),
        interpret=interpret,
    )(scalars, grouped, all_keys, all_values)


def expert_activation(row_data, gate_weights):
    gate_out = jnp.dot(row_data, gate_weights[0], preferred_element_type=jnp.float32)
    up_out = jnp.dot(row_data, gate_weights[1], preferred_element_type=jnp.float32)
    return (jnp.maximum(gate_out, 0.0) * up_out).astype(jnp.bfloat16)


def body(
    hidden_in,
    queries,
    cache_keys,
    cache_values,
    lengths,
    routes,
    attn_gain,
    key_proj,
    value_proj,
    out_proj,
    moe_gain,
    router,
    gate_up,
    down_proj,
):
    own_count = hidden_in.shape[1]
    model_width = hidden_in.shape[2]
    hid_index = lax.axis_index("hid")
    hid_count = lax.axis_size("hid")
    group_size = QH // KVH
    normed = normalize(hidden_in[0], attn_gain).astype(jnp.bfloat16)
    new_keys = jnp.dot(normed, key_proj, preferred_element_type=jnp.float32).astype(jnp.bfloat16)
    new_values = jnp.dot(normed, value_proj, preferred_element_type=jnp.float32).astype(jnp.bfloat16)
    length = lengths[0]
    cache_local = cache_keys.shape[1]
    all_keys = lax.all_gather(jnp.concatenate([cache_keys[0], new_keys], axis=0), "hid", axis=0)
    all_values = lax.all_gather(jnp.concatenate([cache_values[0], new_values], axis=0), "hid", axis=0)
    all_weights = lax.all_gather(
        jnp.concatenate([gate_up[0], down_proj[0].T[None]], axis=0), "hid", axis=0
    )
    grouped = (
        queries[0]
        .reshape(own_count, KVH, group_size, HD)
        .transpose(1, 2, 0, 3)
        .reshape(KVH, group_size * own_count, HD)
    )
    attended = (
        attention(grouped, all_keys, all_values, length, hid_index, own_count)
        .reshape(KVH, group_size, own_count, HD)
        .transpose(2, 0, 1, 3)
        .reshape(own_count, QH * HD)
    )
    mid_stream = (
        hidden_in[0].astype(jnp.float32)
        + jnp.dot(attended, out_proj, preferred_element_type=jnp.float32)
    ).astype(jnp.bfloat16)
    moe_in = normalize(mid_stream, moe_gain).astype(jnp.bfloat16)
    logits = jnp.dot(moe_in, router, preferred_element_type=jnp.float32)
    expert_count = router.shape[1]
    top_count = routes.shape[2]
    capacity = 2 * own_count * top_count // expert_count
    own_routes = lax.dynamic_slice_in_dim(routes[0], hid_index * own_count, own_count, axis=0)
    flat_routes = own_routes.reshape(-1)
    onehot = (flat_routes[:, None] == jnp.arange(expert_count, dtype=jnp.int32)[None, :]).astype(
        jnp.int32
    )
    slot_ids = jnp.sum((jnp.cumsum(onehot, axis=0) - 1) * onehot, axis=-1)
    targets = flat_routes * capacity + slot_ids
    slot_count = expert_count * capacity
    pick = targets[None, :] == jnp.arange(slot_count, dtype=jnp.int32)[:, None]
    pick_rows = jnp.any(pick.reshape(slot_count, own_count, top_count), axis=-1).astype(jnp.bfloat16)
    send_rows = jnp.dot(pick_rows, moe_in, preferred_element_type=jnp.float32).astype(jnp.bfloat16)
    grouped_rows = lax.all_to_all(
        send_rows.reshape(expert_count, capacity, model_width), "req", 0, 0, tiled=True
    )
    flat_rows = grouped_rows.reshape(-1, model_width)
    gate_out = jnp.einsum(
        "nd,hdf->hnf", flat_rows, all_weights[:, 0], preferred_element_type=jnp.float32
    )
    up_out = jnp.einsum(
        "nd,hdf->hnf", flat_rows, all_weights[:, 1], preferred_element_type=jnp.float32
    )
    activation = (jnp.maximum(gate_out, 0.0) * up_out).astype(jnp.bfloat16)
    partials = jnp.einsum(
        "hnf,hdf->hnd", activation, all_weights[:, 2], preferred_element_type=jnp.float32
    ).astype(jnp.bfloat16)
    expert_out = jnp.sum(partials.astype(jnp.float32), axis=0).astype(jnp.bfloat16)
    returned = lax.all_to_all(
        expert_out.reshape(-1, capacity, model_width), "req", 0, 0, tiled=True
    )
    fetched = jnp.dot(
        pick.T.astype(jnp.bfloat16),
        returned.reshape(slot_count, model_width),
        preferred_element_type=jnp.float32,
    ).reshape(own_count, top_count, model_width)
    picked = jnp.take_along_axis(logits, own_routes, axis=1)
    gate_values = jax.nn.sigmoid(picked)
    weights = gate_values / jnp.sum(gate_values, axis=1, keepdims=True)
    moe_out = jnp.sum(weights[..., None] * fetched, axis=1)
    final_rows = (mid_stream.astype(jnp.float32) + moe_out).astype(jnp.bfloat16)
    return (final_rows[None], new_keys[None], new_values[None])


def solution(mesh):
    in_specs = (
        P("req", "hid", None),
        P("req", "hid", None),
        P("req", "hid", None),
        P("req", "hid", None),
        P("req"),
        P("req", None, None),
        P(),
        P(),
        P(),
        P(),
        P(),
        P(),
        P("req", None, None, "hid"),
        P("req", "hid", None),
    )
    out_specs = (P("req", "hid", None), P("req", "hid", None), P("req", "hid", None))
    return jax.shard_map(body, mesh=mesh, in_specs=in_specs, out_specs=out_specs, check_vma=False)
```

profile of v0, /device:TPU:1, one launch (start us, length us, event | category | flops | bytes accessed | tf_op | source)
XLA Modules:
  0.0 234.6 jit_solution(12992392398622482169)
XLA Ops:
  7.3 1.3 fusion.13
  8.6 1.4 convolution_convert_fusion.3
  10.0 1.9 pad_maximum_fusion.1
  12.0 1.4 convolution_convert_fusion.2
  13.5 0.6 copy-done.8
  14.1 0.8 pad_maximum_fusion.2
  15.1 1.5 pad_maximum_fusion
  16.6 0.7 fusion.24
  17.3 0.1 copy.74
  18.3 1.2 reduce-window.6
  19.4 0.2 slice_reduce_fusion
  19.8 0.1 reduce_sum.63
  20.0 0.2 copy.69
  20.2 0.9 copy.70
  21.2 0.7 pad_add_fusion.scalars
  21.8 0.4 fusion.7
  22.2 25.9 %all-gather.7.cloned.1.call-done = bf16[4608,256]{1,0:T(8,128)(2,1)} async-done(((bf16[1152,256]{1,0:T(8,128)(2,1)}), bf16[4608,256]{1,0:T(8,128)(2,1)}) %all-gather.7.cloned.1.call-update) | async-done | bytes 2359312 | tf_op jit(solution)/shard_map/all_gather | solution.py:192
  48.1 34.7 %all-gather.9.cloned.1.call-done = bf16[4608,256]{1,0:T(8,128)(2,1)} async-done(((bf16[1152,256]{1,0:T(8,128)(2,1)}), bf16[4608,256]{1,0:T(8,128)(2,1)}) %all-gather.9.cloned.1.call-update) | async-done | bytes 2359312 | tf_op jit(solution)/shard_map/all_gather | solution.py:193
  82.8 7.6 %shard_map.157 = bf16[2,768,128]{2,1,0:T(8,128)(2,1)} custom-call(s32[2]{0:T(128)} %pad_add_fusion.scalars, bf16[2,768,128]{2,1,0:T(8,128)(2,1)} %bitcast.108, bf16[4,1152,256]{2,1,0:T(8,128)(2,1)} %bitcast.106, bf16[4,1152,256]{2,1,0:T(8,128)(2,1)} %bitcast.107), custom_call_target="tpu_custom_call" | custom-call | tf_op jit(solution)/shard_map/pallas_call | solution.py:142
  90.3 1.2 copy.71
  91.5 3.4 %multiply_reduce_fusion = (f32[128]{0:T(128)S(1)}, f32[128,1536]{1,0:T(8,128)S(1)}) fusion(bf16[128,1536]{0,1:T(8,128)(2,1)S(1)} %bitcast.110, bf16[1536,1536]{1,0:T(8,128)(2,1)} %param.23, bf16[1,128,1536]{2,1,0:T(8,128)(2,1)S(1)} %copy-done.1), kind=kOutput, calls=%fused_computation.31 | convolution fusion | flops 605159296 | bytes 6291968 | tf_op jit(solution)/shard_map/dot_general | solution.py:211
  95.0 1.1 convolution_convert_fusion.1
  96.0 63.0 %all_to_all.10 = bf16[32,32,1536]{2,1,0:T(8,128)(2,1)} all-to-all(bf16[32,32,1536]{2,1,0:T(8,128)(2,1)S(1)} %bitcast.102), channel_id=1, replica_groups=mesh['req'=32,'hid'=4] {'req'}, dimensions={0} | all-to-all | bytes 6291456 | tf_op jit(solution)/shard_map/all_to_all | solution.py:229
  159.1 6.9 %fusion.3 = f32[4,192,1024]{2,1,0:T(8,128)} fusion(bf16[1024,1536,1]{1,0,2:T(8,128)(2,1)} %bitcast.104, bf16[4,3,1536,192]{2,3,1,0:T(8,128)(2,1)} %bitcast.118), kind=kOutput, calls=%fused_computation.11 | convolution fusion | flops 2415919104 | bytes 8650752 | tf_op jit(solution)/shard_map/nd,hdf->hnf/dot_general | solution.py:236
  166.0 12.0 %fusion = bf16[1024,1536]{1,0:T(8,128)(2,1)} fusion(bf16[4,3,1536,192]{2,3,1,0:T(8,128)(2,1)} %bitcast.119, f32[4,192,1024]{2,1,0:T(8,128)} %fusion.3, bf16[1024,1536,1]{1,0,2:T(8,128)(2,1)} %bitcast.105), kind=kOutput, calls=%fused_computation.5 | convolution fusion | flops 4845207552 | bytes 14155776 | tf_op jit(solution)/shard_map/hnf,hdf->hnd/dot_general | solution.py:240
  177.9 5.6 %all-to-all-start.1 = ((bf16[32,32,1536]{2,1,0:T(8,128)(2,1)}), bf16[32,32,1536]{2,1,0:T(8,128)(2,1)}, u32[]{:S(2)}, u32[]{:S(2)}) async-start(bf16[32,32,1536]{2,1,0:T(8,128)(2,1)} %bitcast.103), calls=%async_computation.1 | async-start | bytes 6291456 | tf_op jit(solution)/shard_map/all_to_all | solution.py:244
  183.6 0.1 copy.72
  183.8 0.3 fusion.27
  184.1 3.8 %gather_fusion = f32[512]{0:T(512)S(1)} fusion(f32[128,32]{0,1:T(8,128)S(1)} %fusion.27, s32[512]{0:T(512)S(1)} %reshape.190), kind=kCustom, calls=%fused_computation | custom fusion | bytes 8192 | tf_op jit(solution)/shard_map/jit(take_along_axis)/gather | solution.py:252
  188.1 35.3 %all-to-all-done.1 = bf16[32,32,1536]{2,1,0:T(8,128)(2,1)} async-done(((bf16[32,32,1536]{2,1,0:T(8,128)(2,1)}), bf16[32,32,1536]{2,1,0:T(8,128)(2,1)}, u32[]{:S(2)}, u32[]{:S(2)}) %all-to-all-start.1) | async-done | bytes 3145760 | tf_op jit(solution)/shard_map/all_to_all | solution.py:244
  223.4 3.8 %fusion.8 = f32[128,1536]{1,0:T(8,128)S(1)} fusion(bf16[1024,1536,1]{1,0,2:T(8,128)(2,1)} %bitcast.31, f32[128,4]{0,1:T(4,128)S(1)} %multiply_divide_fusion, s32[128,4]{0,1:T(4,128)S(1)} %fusion.25), kind=kOutput, calls=%fused_computation.19 | convolution fusion | flops 1612513280 | bytes 3936256 | tf_op jit(solution)/shard_map/dot_general | solution.py:247
  227.2 0.9 fusion.16
  (43 shorter events, 1.0 us)
Async XLA Ops:
  7.2 1.4 copy-start
  7.2 4.8 %copy-start.1 = (bf16[1,128,1536]{2,1,0:T(8,128)(2,1)S(1)}, bf16[1,128,1536]{2,1,0:T(8,128)(2,1)}, u32[]{:S(2)}) copy-start(bf16[1,128,1536]{2,1,0:T(8,128)(2,1)} %param.14) | copy-start | bytes 1179652
  7.2 4.8 %copy-start.10 = (f32[1536]{0:T(1024)S(1)}, f32[1536]{0:T(1024)}, u32[]{:S(2)}) copy-start(f32[1536]{0:T(1024)} %param.20) | copy-start | bytes 18436
  7.2 6.9 %copy-start.4 = (bf16[1,1024,256]{2,1,0:T(8,128)(2,1)S(1)}, bf16[1,1024,256]{2,1,0:T(8,128)(2,1)}, u32[]{:S(2)}) copy-start(bf16[1,1024,256]{2,1,0:T(8,128)(2,1)} %param.17) | copy-start | bytes 1572868
  7.2 40.8 %all-gather.7.cloned.1.call-start = ((), (), s32[]{:S(2)}) async-start(), calls=%async_computation.2 | async-start | bytes 2949120 | tf_op jit(solution)/shard_map/all_gather | solution.py:192
  8.5 6.5 %copy-start.2 = (bf16[1,2,1536,192]{2,3,1,0:T(8,128)(2,1)S(1)}, bf16[1,2,1536,192]{2,3,1,0:T(8,128)(2,1)}, u32[]{:S(2)}) copy-start(bf16[1,2,1536,192]{2,3,1,0:T(8,128)(2,1)} %param.26) | copy-start | bytes 3538948
  8.6 6.5 %copy-start.3 = (bf16[1,192,1536]{2,1,0:T(8,128)(2,1)S(1)}, bf16[1,192,1536]{2,1,0:T(8,128)(2,1)}, u32[]{:S(2)}) copy-start(bf16[1,192,1536]{2,1,0:T(8,128)(2,1)} %param.27) | copy-start | bytes 1769476
  10.0 6.5 %copy-start.7 = (bf16[128,256]{1,0:T(8,128)(2,1)}, bf16[128,256]{1,0:T(8,128)(2,1)S(1)}, u32[]{:S(2)}) copy-start(bf16[128,256]{1,0:T(8,128)(2,1)S(1)} %convolution_convert_fusion.3) | copy-start | bytes 196612
  12.0 70.8 %all-gather.9.cloned.1.call-start = ((), (), s32[]{:S(2)}) async-start(), calls=%async_computation.3 | async-start | bytes 2949120 | tf_op jit(solution)/shard_map/all_gather | solution.py:193
  13.5 0.6 copy-start.8
  15.0 5.0 %copy-start.5 = (bf16[1,128,1536]{2,1,0:T(8,128)(2,1)S(1)}, bf16[1,128,1536]{2,1,0:T(8,128)(2,1)}, u32[]{:S(2)}) copy-start(bf16[1,128,1536]{2,1,0:T(8,128)(2,1)} %param.15) | copy-start | bytes 1179652
  15.0 144.1 %all-gather.11.cloned.1.call-start = ((), (), s32[]{:S(2)}) async-start(), calls=%async_computation.4 | async-start | bytes 8847360 | tf_op jit(solution)/shard_map/all_gather | solution.py:194
  91.5 3.4 %copy-start.9 = (f32[1536]{0:T(1024)S(1)}, f32[1536]{0:T(1024)}, u32[]{:S(2)}) copy-start(f32[1536]{0:T(1024)} %param.24) | copy-start | bytes 18436
  177.9 5.9 %copy-start.6 = (bf16[1536,32]{0,1:T(8,128)(2,1)S(1)}, bf16[1536,32]{0,1:T(8,128)(2,1)}, u32[]{:S(2)}) copy-start(bf16[1536,32]{0,1:T(8,128)(2,1)} %param.25) | copy-start | bytes 294916
  177.9 45.4 %all-to-all-start.1 = ((bf16[32,32,1536]{2,1,0:T(8,128)(2,1)}), bf16[32,32,1536]{2,1,0:T(8,128)(2,1)}, u32[]{:S(2)}, u32[]{:S(2)}) async-start(bf16[32,32,1536]{2,1,0:T(8,128)(2,1)} %bitcast.103), calls=%async_computation.1 | async-start | bytes 6291456 | tf_op jit(solution)/shard_map/all_to_all | solution.py:244
Sparse Core Ops, SparseCore 0:
  12.1 35.9 all-gather.6
  49.7 32.9 all-gather.8
  84.4 72.2 all-gather.10
where the time goes:
time: 235 us
  waiting for transfers between devices  95.9 us (41%)
  blocking collectives  63 us (27%)
  matrix products  30.3 us (13%)
  between operations  14.7 us (6%)
  other arithmetic  9.45 us (4%)
  local copies, waits for them, and re-layouts  7.95 us (3%)
  Pallas kernels  7.57 us (3%)
  starting transfers between devices  5.76 us (2%)
    all_to_all x1, blocking collectives, body(): lax.all_to_all(send_rows.reshape(expert_count, capacity, model_width), 'r...  63 us
    all_to_all x1, waiting for transfers between devices, body(): lax.all_to_all(expert_out.reshape(-1, capacity, model_width), 'req', 0, 0...  35.3 us
    all_gather x1, waiting for transfers between devices, body(): lax.all_gather(jnp.concatenate([cache_values[0], new_values], axis=0), 'h...  34.7 us
    all_gather x1, waiting for transfers between devices, body(): lax.all_gather(jnp.concatenate([cache_keys[0], new_keys], axis=0), 'hid',...  25.9 us
    dot_general x1, matrix products, body(): jnp.einsum('hnf,hdf->hnd', activation, all_weights[:, 2], preferred_eleme...  12 us
    pallas_call x1, Pallas kernels, attention(): pl.pallas_call(functools.partial(attention_kernel, token_count), out_shap...  7.57 us
    dot_general x1, matrix products, body(): jnp.einsum('nd,hdf->hnf', flat_rows, all_weights[:, 1], preferred_element...  6.86 us
    all_to_all x1, starting transfers between devices, body(): lax.all_to_all(expert_out.reshape(-1, capacity, model_width), 'req', 0, 0...  5.63 us
  transfers between devices with their start and end apart: 4, of which 3 were waited for; matrix products, arithmetic and copies ran while one was open for 8% of the time, Pallas kernels for 3%

commit v1 on v0

--- a/solution.py
+++ b/solution.py
@@ -79,7 +79,7 @@
     )
 
 
-def attention_kernel(token_count, scalars, q_ref, k_ref, v_ref, o_ref, m_ref, l_ref, acc_ref):
+def attention_kernel(token_count, scalars, q_ref, k_ref, v_ref, o_ref, m_ref, l_ref, acc_ref, s_ref):
     length = scalars[0]
     hid_index = scalars[1]
     parts, part_rows, _ = k_ref.shape
@@ -108,24 +108,21 @@
         row_ids = lax.broadcasted_iota(jnp.int32, (rows, 1), 0)
         return key_pos <= hid_index * token_count + row_ids % token_count
 
-    def scores(part, first, size):
-        k = k_ref[part, pl.ds(first, size), :]
-        raw = lax.dot_general(q, k, (((1,), (1,)), ((), ())), preferred_element_type=jnp.float32)
-        return raw * HD ** (-0.5)
-
     for part, first, size, is_cache in blocks:
 
         @pl.when(live(part, first, is_cache))
         def _():
-            s = jnp.where(visible(part, first, size, is_cache), scores(part, first, size), MASKED_SCORE)
+            k = k_ref[part, pl.ds(first, size), :]
+            raw = lax.dot_general(q, k, (((1,), (1,)), ((), ())), preferred_element_type=jnp.float32)
+            s = jnp.where(visible(part, first, size, is_cache), raw * HD ** (-0.5), MASKED_SCORE)
+            s_ref[:, pl.ds(part * part_rows + first, size)] = s
             m_ref[...] = jnp.maximum(m_ref[...], jnp.max(s, axis=-1, keepdims=True))
 
     for part, first, size, is_cache in blocks:
 
         @pl.when(live(part, first, is_cache))
         def _():
-            s = scores(part, first, size)
-            w = jnp.where(visible(part, first, size, is_cache), jnp.exp(s - m_ref[...]), 0.0)
+            w = jnp.exp(s_ref[:, pl.ds(part * part_rows + first, size)] - m_ref[...])
             l_ref[...] += jnp.sum(w, axis=-1, keepdims=True)
             v = v_ref[part, pl.ds(first, size), :]
             acc_ref[...] += jnp.dot(w.astype(jnp.bfloat16), v, preferred_element_type=jnp.float32)
@@ -133,11 +130,12 @@
     o_ref[0] = (acc_ref[...] / l_ref[...]).astype(o_ref.dtype)
 
 
-def attention(grouped, all_keys, all_values, length, hid_index, token_count, interpret=False):
+def attention(grouped, all_kv, length, hid_index, token_count, interpret=False):
     groups, rows, head = grouped.shape
-    parts, part_rows, _ = all_keys.shape
+    parts, part_rows, _ = all_kv.shape
     scalars = jnp.stack([length, hid_index]).astype(jnp.int32)
-    kv_spec = pl.BlockSpec((parts, part_rows, head), lambda g, s: (0, 0, g))
+    k_spec = pl.BlockSpec((parts, part_rows, head), lambda g, s: (0, 0, g))
+    v_spec = pl.BlockSpec((parts, part_rows, head), lambda g, s: (0, 0, groups + g))
     row_spec = pl.BlockSpec((1, rows, head), lambda g, s: (g, 0, 0))
     return pl.pallas_call(
         functools.partial(attention_kernel, token_count),
@@ -145,16 +143,17 @@
         grid_spec=pltpu.PrefetchScalarGridSpec(
             num_scalar_prefetch=1,
             grid=(groups,),
-            in_specs=[row_spec, kv_spec, kv_spec],
+            in_specs=[row_spec, k_spec, v_spec],
             out_specs=row_spec,
             scratch_shapes=[
                 pltpu.VMEM((rows, 1), jnp.float32),
                 pltpu.VMEM((rows, 1), jnp.float32),
                 pltpu.VMEM((rows, head), jnp.float32),
+                pltpu.VMEM((rows, parts * part_rows), jnp.float32),
             ],
         ),
         interpret=interpret,
-    )(scalars, grouped, all_keys, all_values)
+    )(scalars, grouped, all_kv, all_kv)
 
 
 def expert_activation(row_data, gate_weights):
@@ -189,8 +188,17 @@
     new_values = jnp.dot(normed, value_proj, preferred_element_type=jnp.float32).astype(jnp.bfloat16)
     length = lengths[0]
     cache_local = cache_keys.shape[1]
-    all_keys = lax.all_gather(jnp.concatenate([cache_keys[0], new_keys], axis=0), "hid", axis=0)
-    all_values = lax.all_gather(jnp.concatenate([cache_values[0], new_values], axis=0), "hid", axis=0)
+    all_kv = lax.all_gather(
+        jnp.concatenate(
+            [
+                jnp.concatenate([cache_keys[0], new_keys], axis=0),
+                jnp.concatenate([cache_values[0], new_values], axis=0),
+            ],
+            axis=1,
+        ),
+        "hid",
+        axis=0,
+    )
     all_weights = lax.all_gather(
         jnp.concatenate([gate_up[0], down_proj[0].T[None]], axis=0), "hid", axis=0
     )
@@ -201,7 +209,7 @@
         .reshape(KVH, group_size * own_count, HD)
     )
     attended = (
-        attention(grouped, all_keys, all_values, length, hid_index, own_count)
+        attention(grouped, all_kv, length, hid_index, own_count)
         .reshape(KVH, group_size, own_count, HD)
         .transpose(2, 0, 1, 3)
         .reshape(own_count, QH * HD)

time: 235 us -> 221 us (0.940)
  waiting for transfers between devices: 95.9 us -> 84.8 us
  blocking collectives: 63 us -> 58 us
  starting transfers between devices: 5.76 us -> 8.13 us
    all_gather x2 -> x1, waiting for transfers between devices: 60.6 us -> 48.5 us  [body(): lax.all_gather(jnp.concatenate([jnp.concatenate([cache_keys[0], new_keys]...]
    all_to_all x1, blocking collectives: 63 us -> 58 us  [body(): lax.all_to_all(send_rows.reshape(expert_count, capacity, model_width), 'r...]
    all_to_all x1, starting transfers between devices: 5.63 us -> 8.05 us  [body(): lax.all_to_all(expert_out.reshape(-1, capacity, model_width), 'req', 0, 0...]
  transfers between devices with their start and end apart: 4 -> 3, of which waited for: 3 -> 3; matrix products, arithmetic and copies ran while one was open for 8% -> 8% of each run, Pallas kernels for 3% -> 4%
where the time goes in v1:
time: 221 us
  waiting for transfers between devices  84.8 us (38%)
  blocking collectives  58 us (26%)
  matrix products  30.8 us (14%)
  between operations  14.9 us (7%)
  Pallas kernels  9.18 us (4%)
  starting transfers between devices  8.13 us (4%)
  other arithmetic  7.82 us (4%)
  local copies, waits for them, and re-layouts  7.32 us (3%)
    all_to_all x1, blocking collectives, body(): lax.all_to_all(send_rows.reshape(expert_count, capacity, model_width), 'r...  58 us
    all_gather x1, waiting for transfers between devices, body(): lax.all_gather(jnp.concatenate([jnp.concatenate([cache_keys[0], new_keys]...  48.5 us
    all_to_all x1, waiting for transfers between devices, body(): lax.all_to_all(expert_out.reshape(-1, capacity, model_width), 'req', 0, 0...  35.3 us
    dot_general x1, matrix products, body(): jnp.einsum('hnf,hdf->hnd', activation, all_weights[:, 2], preferred_eleme...  12 us
    pallas_call x1, Pallas kernels, attention(): pl.pallas_call(functools.partial(attention_kernel, token_count), out_shap...  9.18 us
    all_to_all x1, starting transfers between devices, body(): lax.all_to_all(expert_out.reshape(-1, capacity, model_width), 'req', 0, 0...  8.05 us
    dot_general x1, matrix products, body(): jnp.einsum('nd,hdf->hnf', flat_rows, all_weights[:, 1], preferred_element...  6.86 us
  transfers between devices with their start and end apart: 3, of which 3 were waited for; matrix products, arithmetic and copies ran while one was open for 8% of the time, Pallas kernels for 4%

profile of v1, /device:TPU:1, one launch (start us, length us, event | category | flops | bytes accessed | tf_op | source)
XLA Modules:
  0.0 221.0 jit_solution(7229022054149853566)
XLA Ops:
  7.2 1.3 fusion.13
  8.6 1.4 convolution_convert_fusion.2
  10.0 1.6 convolution_convert_fusion.3
  11.7 1.1 maximum_maximum_fusion
  12.9 1.5 pad_maximum_fusion
  14.4 0.7 fusion.24
  15.1 0.1 copy.74
  15.3 0.1 reshape.183
  16.1 1.2 reduce-window.6
  17.2 0.2 slice_reduce_fusion
  17.5 0.1 fusion.20
  17.6 0.1 reduce_sum.63
  17.8 0.2 copy.69
  18.1 0.9 copy.70
  19.0 0.7 pad_add_fusion.scalars
  19.6 0.4 fusion.7
  20.0 48.5 %all-gather.5.cloned.1.call-done = bf16[4608,512]{1,0:T(8,128)(2,1)} async-done(((bf16[1152,512]{1,0:T(8,128)(2,1)}), bf16[4608,512]{1,0:T(8,128)(2,1)}) %all-gather.5.cloned.1.call-update) | async-done | bytes 4718608 | tf_op jit(solution)/shard_map/all_gather | solution.py:191
  68.5 9.2 %shard_map.157 = bf16[2,768,128]{2,1,0:T(8,128)(2,1)} custom-call(s32[2]{0:T(128)} %pad_add_fusion.scalars, bf16[2,768,128]{2,1,0:T(8,128)(2,1)} %bitcast.107, bf16[4,1152,512]{2,1,0:T(8,128)(2,1)} %bitcast.101, bf16[4,1152,512]{2,1,0:T(8,128)(2,1)} %bitcast.102), custom_call_target="tpu_custom_call" | custom-call | tf_op jit(solution)/shard_map/pallas_call | solution.py:140
  77.7 1.2 copy.71
  78.9 3.8 %multiply_reduce_fusion = (f32[128]{0:T(128)S(1)}, f32[128,1536]{1,0:T(8,128)S(1)}) fusion(bf16[128,1536]{0,1:T(8,128)(2,1)S(1)} %bitcast.109, bf16[1536,1536]{1,0:T(8,128)(2,1)} %param.23, bf16[1,128,1536]{2,1,0:T(8,128)(2,1)S(1)} %copy-done.1), kind=kOutput, calls=%fused_computation.32 | convolution fusion | flops 605159296 | bytes 6291968 | tf_op jit(solution)/shard_map/dot_general | solution.py:219
  82.8 1.1 convolution_convert_fusion.1
  83.8 58.0 %all_to_all.10 = bf16[32,32,1536]{2,1,0:T(8,128)(2,1)} all-to-all(bf16[32,32,1536]{2,1,0:T(8,128)(2,1)S(1)} %bitcast.103), channel_id=1, replica_groups=mesh['req'=32,'hid'=4] {'req'}, dimensions={0} | all-to-all | bytes 6291456 | tf_op jit(solution)/shard_map/all_to_all | solution.py:237
  141.8 1.0 all-gather.7.cloned.1.call-done
  142.8 6.9 %fusion.3 = f32[4,192,1024]{2,1,0:T(8,128)} fusion(bf16[1024,1536,1]{1,0,2:T(8,128)(2,1)} %bitcast.105, bf16[4,3,1536,192]{2,3,1,0:T(8,128)(2,1)} %bitcast.117), kind=kOutput, calls=%fused_computation.11 | convolution fusion | flops 2415919104 | bytes 8650752 | tf_op jit(solution)/shard_map/nd,hdf->hnf/dot_general | solution.py:244
  149.6 12.0 %fusion = bf16[1024,1536]{1,0:T(8,128)(2,1)} fusion(bf16[4,3,1536,192]{2,3,1,0:T(8,128)(2,1)} %bitcast.118, f32[4,192,1024]{2,1,0:T(8,128)} %fusion.3, bf16[1024,1536,1]{1,0,2:T(8,128)(2,1)} %bitcast.106), kind=kOutput, calls=%fused_computation.5 | convolution fusion | flops 4845207552 | bytes 14155776 | tf_op jit(solution)/shard_map/hnf,hdf->hnd/dot_general | solution.py:248
  161.6 8.1 %all-to-all-start.1 = ((bf16[32,32,1536]{2,1,0:T(8,128)(2,1)}), bf16[32,32,1536]{2,1,0:T(8,128)(2,1)}, u32[]{:S(2)}, u32[]{:S(2)}) async-start(bf16[32,32,1536]{2,1,0:T(8,128)(2,1)} %bitcast.104), calls=%async_computation.1 | async-start | bytes 6291456 | tf_op jit(solution)/shard_map/all_to_all | solution.py:252
  169.7 0.1 copy.72
  169.9 0.3 fusion.27
  170.2 3.8 %gather_fusion = f32[512]{0:T(512)S(1)} fusion(f32[128,32]{0,1:T(8,128)S(1)} %fusion.27, s32[512]{0:T(512)S(1)} %reshape.190), kind=kCustom, calls=%fused_computation | custom fusion | bytes 8192 | tf_op jit(solution)/shard_map/jit(take_along_axis)/gather | solution.py:260
  174.2 35.3 %all-to-all-done.1 = bf16[32,32,1536]{2,1,0:T(8,128)(2,1)} async-done(((bf16[32,32,1536]{2,1,0:T(8,128)(2,1)}), bf16[32,32,1536]{2,1,0:T(8,128)(2,1)}, u32[]{:S(2)}, u32[]{:S(2)}) %all-to-all-start.1) | async-done | bytes 3145760 | tf_op jit(solution)/shard_map/all_to_all | solution.py:252
  209.5 3.8 %fusion.8 = f32[128,1536]{1,0:T(8,128)S(1)} fusion(bf16[1024,1536,1]{1,0,2:T(8,128)(2,1)} %bitcast.30, f32[128,4]{0,1:T(4,128)S(1)} %multiply_divide_fusion, s32[128,4]{0,1:T(4,128)S(1)} %fusion.25), kind=kOutput, calls=%fused_computation.19 | convolution fusion | flops 1612513280 | bytes 3936256 | tf_op jit(solution)/shard_map/dot_general | solution.py:255
  213.3 0.9 fusion.16
  (39 shorter events, 0.7 us)
Async XLA Ops:
  7.2 1.4 copy-start
  7.2 4.5 %copy-start.4 = (bf16[1,1024,256]{2,1,0:T(8,128)(2,1)S(1)}, bf16[1,1024,256]{2,1,0:T(8,128)(2,1)}, u32[]{:S(2)}) copy-start(bf16[1,1024,256]{2,1,0:T(8,128)(2,1)} %param.17) | copy-start | bytes 1572868
  7.2 61.3 %all-gather.5.cloned.1.call-start = ((), (), s32[]{:S(2)}) async-start(), calls=%async_computation.2 | async-start | bytes 5898240 | tf_op jit(solution)/shard_map/all_gather | solution.py:191
  7.2 4.4 %copy-start.5 = (bf16[1,1024,256]{2,1,0:T(8,128)(2,1)S(1)}, bf16[1,1024,256]{2,1,0:T(8,128)(2,1)}, u32[]{:S(2)}) copy-start(bf16[1,1024,256]{2,1,0:T(8,128)(2,1)} %param.16) | copy-start | bytes 1572868
  8.5 4.3 %copy-start.2 = (bf16[1,2,1536,192]{2,3,1,0:T(8,128)(2,1)S(1)}, bf16[1,2,1536,192]{2,3,1,0:T(8,128)(2,1)}, u32[]{:S(2)}) copy-start(bf16[1,2,1536,192]{2,3,1,0:T(8,128)(2,1)} %param.26) | copy-start | bytes 3538948
  8.6 4.3 %copy-start.3 = (bf16[1,192,1536]{2,1,0:T(8,128)(2,1)S(1)}, bf16[1,192,1536]{2,1,0:T(8,128)(2,1)}, u32[]{:S(2)}) copy-start(bf16[1,192,1536]{2,1,0:T(8,128)(2,1)} %param.27) | copy-start | bytes 1769476
  10.0 4.3 %copy-start.8 = (bf16[128,256]{1,0:T(8,128)(2,1)}, bf16[128,256]{1,0:T(8,128)(2,1)S(1)}, u32[]{:S(2)}) copy-start(bf16[128,256]{1,0:T(8,128)(2,1)S(1)} %convolution_convert_fusion.2) | copy-start | bytes 196612
  11.6 2.7 %copy-start.9 = (bf16[128,256]{1,0:T(8,128)(2,1)}, bf16[128,256]{1,0:T(8,128)(2,1)S(1)}, u32[]{:S(2)}) copy-start(bf16[128,256]{1,0:T(8,128)(2,1)S(1)} %convolution_convert_fusion.3) | copy-start | bytes 196612
  12.8 5.0 %copy-start.6 = (bf16[1,128,1536]{2,1,0:T(8,128)(2,1)S(1)}, bf16[1,128,1536]{2,1,0:T(8,128)(2,1)}, u32[]{:S(2)}) copy-start(bf16[1,128,1536]{2,1,0:T(8,128)(2,1)} %param.15) | copy-start | bytes 1179652
  12.8 130.0 %all-gather.7.cloned.1.call-start = ((), (), s32[]{:S(2)}) async-start(), calls=%async_computation.3 | async-start | bytes 8847360 | tf_op jit(solution)/shard_map/all_gather | solution.py:202
  68.5 10.4 %copy-start.1 = (bf16[1,128,1536]{2,1,0:T(8,128)(2,1)S(1)}, bf16[1,128,1536]{2,1,0:T(8,128)(2,1)}, u32[]{:S(2)}) copy-start(bf16[1,128,1536]{2,1,0:T(8,128)(2,1)} %param.14) | copy-start | bytes 1179652
  78.9 3.8 %copy-start.10 = (f32[1536]{0:T(1024)S(1)}, f32[1536]{0:T(1024)}, u32[]{:S(2)}) copy-start(f32[1536]{0:T(1024)} %param.24) | copy-start | bytes 18436
  161.6 8.3 %copy-start.7 = (bf16[1536,32]{0,1:T(8,128)(2,1)S(1)}, bf16[1536,32]{0,1:T(8,128)(2,1)}, u32[]{:S(2)}) copy-start(bf16[1536,32]{0,1:T(8,128)(2,1)} %param.25) | copy-start | bytes 294916
  161.6 47.9 %all-to-all-start.1 = ((bf16[32,32,1536]{2,1,0:T(8,128)(2,1)}), bf16[32,32,1536]{2,1,0:T(8,128)(2,1)}, u32[]{:S(2)}, u32[]{:S(2)}) async-start(bf16[32,32,1536]{2,1,0:T(8,128)(2,1)} %bitcast.104), calls=%async_computation.1 | async-start | bytes 6291456 | tf_op jit(solution)/shard_map/all_to_all | solution.py:252
Sparse Core Ops, SparseCore 0:
  12.9 55.5 all-gather.4
  70.2 72.5 all-gather.6

commit v2 on v1

--- a/solution.py
+++ b/solution.py
@@ -95,10 +95,15 @@
             blocks.append((part, first, min(KEY_BLOCK, cache_rows - first), True))
         blocks.append((part, cache_rows, token_count, False))
 
-    def live(part, first, is_cache):
+    def live(part, first, size, is_cache):
         if is_cache:
             return part * cache_rows + first < length
         return part <= hid_index
+
+    def whole(part, first, size, is_cache):
+        if is_cache:
+            return part * cache_rows + first + size <= length
+        return part < hid_index
 
     def visible(part, first, size, is_cache):
         if is_cache:
@@ -108,19 +113,25 @@
         row_ids = lax.broadcasted_iota(jnp.int32, (rows, 1), 0)
         return key_pos <= hid_index * token_count + row_ids % token_count
 
+    def first_pass(part, first, size, is_cache, masked):
+        k = k_ref[part, pl.ds(first, size), :]
+        raw = lax.dot_general(q, k, (((1,), (1,)), ((), ())), preferred_element_type=jnp.float32)
+        s = raw * HD ** (-0.5)
+        if masked:
+            s = jnp.where(visible(part, first, size, is_cache), s, MASKED_SCORE)
+        s_ref[:, pl.ds(part * part_rows + first, size)] = s
+        m_ref[...] = jnp.maximum(m_ref[...], jnp.max(s, axis=-1, keepdims=True))
+
     for part, first, size, is_cache in blocks:
-
-        @pl.when(live(part, first, is_cache))
-        def _():
-            k = k_ref[part, pl.ds(first, size), :]
-            raw = lax.dot_general(q, k, (((1,), (1,)), ((), ())), preferred_element_type=jnp.float32)
-            s = jnp.where(visible(part, first, size, is_cache), raw * HD ** (-0.5), MASKED_SCORE)
-            s_ref[:, pl.ds(part * part_rows + first, size)] = s
-            m_ref[...] = jnp.maximum(m_ref[...], jnp.max(s, axis=-1, keepdims=True))
+        is_whole = whole(part, first, size, is_cache)
+        pl.when(is_whole)(functools.partial(first_pass, part, first, size, is_cache, False))
+        pl.when(jnp.logical_and(live(part, first, size, is_cache), jnp.logical_not(is_whole)))(
+            functools.partial(first_pass, part, first, size, is_cache, True)
+        )
 
     for part, first, size, is_cache in blocks:
 
-        @pl.when(live(part, first, is_cache))
+        @pl.when(live(part, first, size, is_cache))
         def _():
             w = jnp.exp(s_ref[:, pl.ds(part * part_rows + first, size)] - m_ref[...])
             l_ref[...] += jnp.sum(w, axis=-1, keepdims=True)

time: 221 us -> 221 us (level)
  Pallas kernels: 9.18 us -> 11.4 us
    pallas_call x1, Pallas kernels: 9.18 us -> 11.4 us  [attention(): pl.pallas_call(functools.partial(attention_kernel, token_count), out_shap...]
  transfers between devices with their start and end apart: 3 -> 3, of which waited for: 3 -> 3; matrix products, arithmetic and copies ran while one was open for 8% -> 8% of each run, Pallas kernels for 4% -> 5%
where the time goes in v2:
time: 221 us
  waiting for transfers between devices  84.3 us (38%)
  blocking collectives  56.2 us (25%)
  matrix products  30.7 us (14%)
  between operations  14.9 us (7%)
  Pallas kernels  11.4 us (5%)
  starting transfers between devices  8.18 us (4%)
  other arithmetic  7.82 us (4%)
  local copies, waits for them, and re-layouts  7.37 us (3%)
    all_to_all x1, blocking collectives, body(): lax.all_to_all(send_rows.reshape(expert_count, capacity, model_width), 'r...  56.2 us
    all_gather x1, waiting for transfers between devices, body(): lax.all_gather(jnp.concatenate([jnp.concatenate([cache_keys[0], new_keys]...  48.5 us
    all_to_all x1, waiting for transfers between devices, body(): lax.all_to_all(expert_out.reshape(-1, capacity, model_width), 'req', 0, 0...  35.3 us
    dot_general x1, matrix products, body(): jnp.einsum('hnf,hdf->hnd', activation, all_weights[:, 2], preferred_eleme...  12 us
    pallas_call x1, Pallas kernels, attention(): pl.pallas_call(functools.partial(attention_kernel, token_count), out_shap...  11.4 us
    all_to_all x1, starting transfers between devices, body(): lax.all_to_all(expert_out.reshape(-1, capacity, model_width), 'req', 0, 0...  8.1 us
    dot_general x1, matrix products, body(): jnp.einsum('nd,hdf->hnf', flat_rows, all_weights[:, 1], preferred_element...  6.86 us
  transfers between devices with their start and end apart: 3, of which 3 were waited for; matrix products, arithmetic and copies ran while one was open for 8% of the time, Pallas kernels for 5%

profile of v2, /device:TPU:1, one launch (start us, length us, event | category | flops | bytes accessed | tf_op | source)
XLA Modules:
  0.0 221.0 jit_solution(8668512977169663076)
XLA Ops:
  7.2 1.3 fusion.13
  8.6 1.4 convolution_convert_fusion.2
  10.0 1.6 convolution_convert_fusion.3
  11.7 1.1 maximum_maximum_fusion
  12.9 1.5 pad_maximum_fusion
  14.4 0.7 fusion.24
  15.1 0.1 copy.74
  15.3 0.1 reshape.183
  16.1 1.2 reduce-window.6
  17.2 0.2 slice_reduce_fusion
  17.5 0.1 fusion.20
  17.6 0.1 reduce_sum.63
  17.8 0.2 copy.69
  18.1 0.9 copy.70
  19.0 0.7 pad_add_fusion.scalars
  19.6 0.4 fusion.7
  20.0 48.5 %all-gather.5.cloned.1.call-done = bf16[4608,512]{1,0:T(8,128)(2,1)} async-done(((bf16[1152,512]{1,0:T(8,128)(2,1)}), bf16[4608,512]{1,0:T(8,128)(2,1)}) %all-gather.5.cloned.1.call-update) | async-done | bytes 4718608 | tf_op jit(solution)/shard_map/all_gather | solution.py:202
  68.5 11.4 %shard_map.157 = bf16[2,768,128]{2,1,0:T(8,128)(2,1)} custom-call(s32[2]{0:T(128)} %pad_add_fusion.scalars, bf16[2,768,128]{2,1,0:T(8,128)(2,1)} %bitcast.107, bf16[4,1152,512]{2,1,0:T(8,128)(2,1)} %bitcast.101, bf16[4,1152,512]{2,1,0:T(8,128)(2,1)} %bitcast.102), custom_call_target="tpu_custom_call" | custom-call | tf_op jit(solution)/shard_map/pallas_call | solution.py:151
  79.9 1.3 copy.71
  81.2 3.7 %multiply_reduce_fusion = (f32[128]{0:T(128)S(1)}, f32[128,1536]{1,0:T(8,128)S(1)}) fusion(bf16[128,1536]{0,1:T(8,128)(2,1)S(1)} %bitcast.109, bf16[1536,1536]{1,0:T(8,128)(2,1)} %param.23, bf16[1,128,1536]{2,1,0:T(8,128)(2,1)S(1)} %copy-done.1), kind=kOutput, calls=%fused_computation.32 | convolution fusion | flops 605159296 | bytes 6291968 | tf_op jit(solution)/shard_map/dot_general | solution.py:230
  85.0 1.0 convolution_convert_fusion.1
  86.0 56.2 %all_to_all.10 = bf16[32,32,1536]{2,1,0:T(8,128)(2,1)} all-to-all(bf16[32,32,1536]{2,1,0:T(8,128)(2,1)S(1)} %bitcast.103), channel_id=1, replica_groups=mesh['req'=32,'hid'=4] {'req'}, dimensions={0} | all-to-all | bytes 6291456 | tf_op jit(solution)/shard_map/all_to_all | solution.py:248
  142.3 0.5 all-gather.7.cloned.1.call-done
  142.7 6.9 %fusion.3 = f32[4,192,1024]{2,1,0:T(8,128)} fusion(bf16[1024,1536,1]{1,0,2:T(8,128)(2,1)} %bitcast.105, bf16[4,3,1536,192]{2,3,1,0:T(8,128)(2,1)} %bitcast.117), kind=kOutput, calls=%fused_computation.11 | convolution fusion | flops 2415919104 | bytes 8650752 | tf_op jit(solution)/shard_map/nd,hdf->hnf/dot_general | solution.py:255
  149.6 12.0 %fusion = bf16[1024,1536]{1,0:T(8,128)(2,1)} fusion(bf16[4,3,1536,192]{2,3,1,0:T(8,128)(2,1)} %bitcast.118, f32[4,192,1024]{2,1,0:T(8,128)} %fusion.3, bf16[1024,1536,1]{1,0,2:T(8,128)(2,1)} %bitcast.106), kind=kOutput, calls=%fused_computation.5 | convolution fusion | flops 4845207552 | bytes 14155776 | tf_op jit(solution)/shard_map/hnf,hdf->hnd/dot_general | solution.py:259
  161.6 8.1 %all-to-all-start.1 = ((bf16[32,32,1536]{2,1,0:T(8,128)(2,1)}), bf16[32,32,1536]{2,1,0:T(8,128)(2,1)}, u32[]{:S(2)}, u32[]{:S(2)}) async-start(bf16[32,32,1536]{2,1,0:T(8,128)(2,1)} %bitcast.104), calls=%async_computation.1 | async-start | bytes 6291456 | tf_op jit(solution)/shard_map/all_to_all | solution.py:263
  169.7 0.1 copy.72
  169.9 0.3 fusion.27
  170.2 3.8 %gather_fusion = f32[512]{0:T(512)S(1)} fusion(f32[128,32]{0,1:T(8,128)S(1)} %fusion.27, s32[512]{0:T(512)S(1)} %reshape.190), kind=kCustom, calls=%fused_computation | custom fusion | bytes 8192 | tf_op jit(solution)/shard_map/jit(take_along_axis)/gather | solution.py:271
  174.2 35.3 %all-to-all-done.1 = bf16[32,32,1536]{2,1,0:T(8,128)(2,1)} async-done(((bf16[32,32,1536]{2,1,0:T(8,128)(2,1)}), bf16[32,32,1536]{2,1,0:T(8,128)(2,1)}, u32[]{:S(2)}, u32[]{:S(2)}) %all-to-all-start.1) | async-done | bytes 3145760 | tf_op jit(solution)/shard_map/all_to_all | solution.py:263
  209.5 3.8 %fusion.8 = f32[128,1536]{1,0:T(8,128)S(1)} fusion(bf16[1024,1536,1]{1,0,2:T(8,128)(2,1)} %bitcast.30, f32[128,4]{0,1:T(4,128)S(1)} %multiply_divide_fusion, s32[128,4]{0,1:T(4,128)S(1)} %fusion.25), kind=kOutput, calls=%fused_computation.19 | convolution fusion | flops 1612513280 | bytes 3936256 | tf_op jit(solution)/shard_map/dot_general | solution.py:266
  213.3 0.9 fusion.16
  (39 shorter events, 0.7 us)
Async XLA Ops:
  7.2 1.4 copy-start
  7.2 4.5 %copy-start.4 = (bf16[1,1024,256]{2,1,0:T(8,128)(2,1)S(1)}, bf16[1,1024,256]{2,1,0:T(8,128)(2,1)}, u32[]{:S(2)}) copy-start(bf16[1,1024,256]{2,1,0:T(8,128)(2,1)} %param.17) | copy-start | bytes 1572868
  7.2 61.3 %all-gather.5.cloned.1.call-start = ((), (), s32[]{:S(2)}) async-start(), calls=%async_computation.2 | async-start | bytes 5898240 | tf_op jit(solution)/shard_map/all_gather | solution.py:202
  7.2 4.4 %copy-start.5 = (bf16[1,1024,256]{2,1,0:T(8,128)(2,1)S(1)}, bf16[1,1024,256]{2,1,0:T(8,128)(2,1)}, u32[]{:S(2)}) copy-start(bf16[1,1024,256]{2,1,0:T(8,128)(2,1)} %param.16) | copy-start | bytes 1572868
  8.5 4.3 %copy-start.2 = (bf16[1,2,1536,192]{2,3,1,0:T(8,128)(2,1)S(1)}, bf16[1,2,1536,192]{2,3,1,0:T(8,128)(2,1)}, u32[]{:S(2)}) copy-start(bf16[1,2,1536,192]{2,3,1,0:T(8,128)(2,1)} %param.26) | copy-start | bytes 3538948
  8.6 4.3 %copy-start.3 = (bf16[1,192,1536]{2,1,0:T(8,128)(2,1)S(1)}, bf16[1,192,1536]{2,1,0:T(8,128)(2,1)}, u32[]{:S(2)}) copy-start(bf16[1,192,1536]{2,1,0:T(8,128)(2,1)} %param.27) | copy-start | bytes 1769476
  10.0 4.3 %copy-start.8 = (bf16[128,256]{1,0:T(8,128)(2,1)}, bf16[128,256]{1,0:T(8,128)(2,1)S(1)}, u32[]{:S(2)}) copy-start(bf16[128,256]{1,0:T(8,128)(2,1)S(1)} %convolution_convert_fusion.2) | copy-start | bytes 196612
  11.6 2.7 %copy-start.9 = (bf16[128,256]{1,0:T(8,128)(2,1)}, bf16[128,256]{1,0:T(8,128)(2,1)S(1)}, u32[]{:S(2)}) copy-start(bf16[128,256]{1,0:T(8,128)(2,1)S(1)} %convolution_convert_fusion.3) | copy-start | bytes 196612
  12.8 5.0 %copy-start.6 = (bf16[1,128,1536]{2,1,0:T(8,128)(2,1)S(1)}, bf16[1,128,1536]{2,1,0:T(8,128)(2,1)}, u32[]{:S(2)}) copy-start(bf16[1,128,1536]{2,1,0:T(8,128)(2,1)} %param.15) | copy-start | bytes 1179652
  12.8 129.9 %all-gather.7.cloned.1.call-start = ((), (), s32[]{:S(2)}) async-start(), calls=%async_computation.3 | async-start | bytes 8847360 | tf_op jit(solution)/shard_map/all_gather | solution.py:213
  68.5 12.7 %copy-start.1 = (bf16[1,128,1536]{2,1,0:T(8,128)(2,1)S(1)}, bf16[1,128,1536]{2,1,0:T(8,128)(2,1)}, u32[]{:S(2)}) copy-start(bf16[1,128,1536]{2,1,0:T(8,128)(2,1)} %param.14) | copy-start | bytes 1179652
  81.2 3.7 %copy-start.10 = (f32[1536]{0:T(1024)S(1)}, f32[1536]{0:T(1024)}, u32[]{:S(2)}) copy-start(f32[1536]{0:T(1024)} %param.24) | copy-start | bytes 18436
  161.6 8.3 %copy-start.7 = (bf16[1536,32]{0,1:T(8,128)(2,1)S(1)}, bf16[1536,32]{0,1:T(8,128)(2,1)}, u32[]{:S(2)}) copy-start(bf16[1536,32]{0,1:T(8,128)(2,1)} %param.25) | copy-start | bytes 294916
  161.6 47.9 %all-to-all-start.1 = ((bf16[32,32,1536]{2,1,0:T(8,128)(2,1)}), bf16[32,32,1536]{2,1,0:T(8,128)(2,1)}, u32[]{:S(2)}, u32[]{:S(2)}) async-start(bf16[32,32,1536]{2,1,0:T(8,128)(2,1)} %bitcast.104), calls=%async_computation.1 | async-start | bytes 6291456 | tf_op jit(solution)/shard_map/all_to_all | solution.py:263
Sparse Core Ops, SparseCore 0:
  12.9 55.5 all-gather.4
  70.2 72.4 all-gather.6

commit v3 on v2

--- a/solution.py
+++ b/solution.py
@@ -245,29 +245,37 @@
     pick = targets[None, :] == jnp.arange(slot_count, dtype=jnp.int32)[:, None]
     pick_rows = jnp.any(pick.reshape(slot_count, own_count, top_count), axis=-1).astype(jnp.bfloat16)
     send_rows = jnp.dot(pick_rows, moe_in, preferred_element_type=jnp.float32).astype(jnp.bfloat16)
-    grouped_rows = lax.all_to_all(
-        send_rows.reshape(expert_count, capacity, model_width), "req", 0, 0, tiled=True
-    )
-    flat_rows = grouped_rows.reshape(-1, model_width)
-    gate_out = jnp.einsum(
-        "nd,hdf->hnf", flat_rows, all_weights[:, 0], preferred_element_type=jnp.float32
-    )
-    up_out = jnp.einsum(
-        "nd,hdf->hnf", flat_rows, all_weights[:, 1], preferred_element_type=jnp.float32
-    )
-    activation = (jnp.maximum(gate_out, 0.0) * up_out).astype(jnp.bfloat16)
-    partials = jnp.einsum(
-        "hnf,hdf->hnd", activation, all_weights[:, 2], preferred_element_type=jnp.float32
-    ).astype(jnp.bfloat16)
-    expert_out = jnp.sum(partials.astype(jnp.float32), axis=0).astype(jnp.bfloat16)
-    returned = lax.all_to_all(
-        expert_out.reshape(-1, capacity, model_width), "req", 0, 0, tiled=True
-    )
-    fetched = jnp.dot(
-        pick.T.astype(jnp.bfloat16),
-        returned.reshape(slot_count, model_width),
-        preferred_element_type=jnp.float32,
-    ).reshape(own_count, top_count, model_width)
+    chunk_count = 2
+    chunk = capacity // chunk_count
+    send_rows = send_rows.reshape(expert_count, capacity, model_width)
+    pick_slots = pick.T.astype(jnp.bfloat16).reshape(own_count * top_count, expert_count, capacity)
+    fetched = None
+    for index in range(chunk_count):
+        grouped_rows = lax.all_to_all(
+            send_rows[:, index * chunk : (index + 1) * chunk], "req", 0, 0, tiled=True
+        )
+        flat_rows = grouped_rows.reshape(-1, model_width)
+        gate_out = jnp.einsum(
+            "nd,hdf->hnf", flat_rows, all_weights[:, 0], preferred_element_type=jnp.float32
+        )
+        up_out = jnp.einsum(
+            "nd,hdf->hnf", flat_rows, all_weights[:, 1], preferred_element_type=jnp.float32
+        )
+        activation = (jnp.maximum(gate_out, 0.0) * up_out).astype(jnp.bfloat16)
+        partials = jnp.einsum(
+            "hnf,hdf->hnd", activation, all_weights[:, 2], preferred_element_type=jnp.float32
+        ).astype(jnp.bfloat16)
+        expert_out = jnp.sum(partials.astype(jnp.float32), axis=0).astype(jnp.bfloat16)
+        returned = lax.all_to_all(
+            expert_out.reshape(-1, chunk, model_width), "req", 0, 0, tiled=True
+        )
+        part = jnp.dot(
+            pick_slots[:, :, index * chunk : (index + 1) * chunk].reshape(own_count * top_count, -1),
+            returned.reshape(-1, model_width),
+            preferred_element_type=jnp.float32,
+        )
+        fetched = part if fetched is None else fetched + part
+    fetched = fetched.reshape(own_count, top_count, model_width)
     picked = jnp.take_along_axis(logits, own_routes, axis=1)
     gate_values = jax.nn.sigmoid(picked)
     weights = gate_values / jnp.sum(gate_values, axis=1, keepdims=True)

time: 221 us -> 236 us (1.068)
  blocking collectives: 56.2 us -> 35.6 us
  matrix products: 30.7 us -> 40.6 us
  starting transfers between devices: 8.18 us -> 16.5 us
  local copies, waits for them, and re-layouts: 7.37 us -> 15.5 us
  other arithmetic: 7.82 us -> 12.1 us
  waiting for transfers between devices: 84.3 us -> 87.1 us
    all_to_all x1, blocking collectives: 56.2 us -> 35.6 us  [body(): lax.all_to_all(send_rows[:, index * chunk:(index + 1) * chunk], 'req', 0,...]
    all_gather x1, waiting for transfers between devices: 0.45 us -> 14.2 us  [body(): lax.all_gather(jnp.concatenate([gate_up[0], down_proj[0].T[None]], axis=0...]
    all_to_all x1 -> x3, waiting for transfers between devices: 35.3 us -> 24.9 us  [the longest x2 24.9 us: body(): lax.all_to_all(expert_out.reshape(-1, chunk, model_width), 'req', 0, 0, t...]
    all_to_all x1 -> x3, starting transfers between devices: 8.1 us -> 16.5 us  [the longest x2 12.7 us: body(): lax.all_to_all(expert_out.reshape(-1, chunk, model_width), 'req', 0, 0, t...]
    dot_general x2 -> x4, matrix products: 10.6 us -> 18.1 us  [the longest x2 9.53 us: body(): jnp.einsum('nd,hdf->hnf', flat_rows, all_weights[:, 0], preferred_element...]
    reshape x0 -> x1, local copies, waits for them, and re-layouts: none -> 4.82 us  [body(): fetched = fetched.reshape(own_count, top_count, model_width)]
    reduce_sum x0 -> x1, other arithmetic: none -> 4.18 us  [body(): moe_out = jnp.sum(weights[..., None] * fetched, axis=1)]
    dot_general x1 -> x2, matrix products: 12 us -> 15.9 us  [body(): jnp.einsum('hnf,hdf->hnd', activation, all_weights[:, 2], preferred_eleme...]
  transfers between devices with their start and end apart: 3 -> 5, of which waited for: 3 -> 4; matrix products, arithmetic and copies ran while one was open for 8% -> 20% of each run, Pallas kernels for 5% -> 6%
where the time goes in v3:
time: 236 us
  waiting for transfers between devices  87.1 us (37%)
  matrix products  40.6 us (17%)
  blocking collectives  35.6 us (15%)
  starting transfers between devices  16.5 us (7%)
  local copies, waits for them, and re-layouts  15.5 us (7%)
  between operations  15 us (6%)
  Pallas kernels  13.3 us (6%)
  other arithmetic  12.1 us (5%)
    all_gather x1, waiting for transfers between devices, body(): lax.all_gather(jnp.concatenate([jnp.concatenate([cache_keys[0], new_keys]...  47.9 us
    all_to_all x1, blocking collectives, body(): lax.all_to_all(send_rows[:, index * chunk:(index + 1) * chunk], 'req', 0,...  35.6 us
    all_to_all x2, waiting for transfers between devices, body(): lax.all_to_all(expert_out.reshape(-1, chunk, model_width), 'req', 0, 0, t...  24.9 us
    dot_general x2, matrix products, body(): jnp.einsum('hnf,hdf->hnd', activation, all_weights[:, 2], preferred_eleme...  15.9 us
    all_gather x1, waiting for transfers between devices, body(): lax.all_gather(jnp.concatenate([gate_up[0], down_proj[0].T[None]], axis=0...  14.2 us
    pallas_call x1, Pallas kernels, attention(): pl.pallas_call(functools.partial(attention_kernel, token_count), out_shap...  13.3 us
    all_to_all x2, starting transfers between devices, body(): lax.all_to_all(expert_out.reshape(-1, chunk, model_width), 'req', 0, 0, t...  12.7 us
    dot_general x2, matrix products, body(): jnp.einsum('nd,hdf->hnf', flat_rows, all_weights[:, 0], preferred_element...  9.53 us
  transfers between devices with their start and end apart: 5, of which 4 were waited for; matrix products, arithmetic and copies ran while one was open for 20% of the time, Pallas kernels for 6%

profile of v3, /device:TPU:1, one launch (start us, length us, event | category | flops | bytes accessed | tf_op | source)
XLA Modules:
  0.0 235.7 jit_solution(3127175586682488462)
XLA Ops:
  7.3 1.3 fusion.16
  8.6 1.3 convolution_convert_fusion.1
  10.3 1.1 maximum_maximum_fusion
  12.2 1.5 pad_maximum_fusion
  13.7 0.7 fusion.29
  14.8 1.2 reduce-window.6
  17.4 0.9 copy.70
  18.3 0.7 pad_add_fusion.scalars
  19.3 47.9 %all-gather.5.cloned.1.call-done = bf16[4608,512]{1,0:T(8,128)(2,1)} async-done(((bf16[1152,512]{1,0:T(8,128)(2,1)}), bf16[4608,512]{1,0:T(8,128)(2,1)}) %all-gather.5.cloned.1.call-update) | async-done | bytes 4718608 | tf_op jit(solution)/shard_map/all_gather | solution.py:202
  67.2 13.3 %shard_map.157 = bf16[2,768,128]{2,1,0:T(8,128)(2,1)} custom-call(s32[2]{0:T(128)} %pad_add_fusion.scalars, bf16[2,768,128]{2,1,0:T(8,128)(2,1)} %bitcast.114, bf16[4,1152,512]{2,1,0:T(8,128)(2,1)} %bitcast.111, bf16[4,1152,512]{2,1,0:T(8,128)(2,1)} %bitcast.112), custom_call_target="tpu_custom_call" | custom-call | tf_op jit(solution)/shard_map/pallas_call | solution.py:151
  80.5 1.3 copy.71
  81.7 3.6 %multiply_reduce_fusion.1 = (f32[128]{0:T(128)S(1)}, f32[128,1536]{1,0:T(8,128)S(1)}) fusion(bf16[128,1536]{0,1:T(8,128)(2,1)S(1)} %bitcast.122, bf16[1536,1536]{1,0:T(8,128)(2,1)} %param.23, bf16[1,128,1536]{2,1,0:T(8,128)(2,1)S(1)} %copy-done.2), kind=kOutput, calls=%fused_computation.43 | convolution fusion | flops 605159296 | bytes 6291968 | tf_op jit(solution)/shard_map/dot_general | solution.py:230
  85.4 1.1 convolution_convert_fusion
  86.5 1.4 fusion.34
  87.9 35.6 %all_to_all.20 = bf16[32,16,1536]{2,1,0:T(8,128)(2,1)} all-to-all(bf16[32,16,1536]{2,1,0:T(8,128)(2,1)S(1)} %get-tuple-element.6), channel_id=1, replica_groups=mesh['req'=32,'hid'=4] {'req'}, dimensions={0} | all-to-all | bytes 3145728 | tf_op jit(solution)/shard_map/all_to_all | solution.py:254
  123.5 3.8 %all-to-all-start = ((bf16[32,16,1536]{2,1,0:T(8,128)(2,1)}), bf16[32,16,1536]{2,1,0:T(8,128)(2,1)S(1)}, u32[]{:S(2)}, u32[]{:S(2)}) async-start(bf16[32,16,1536]{2,1,0:T(8,128)(2,1)} %get-tuple-element.5), calls=%async_computation | async-start | bytes 3145728 | tf_op jit(solution)/shard_map/all_to_all | solution.py:254
  127.2 14.2 %all-gather.7.cloned.1.call-done = bf16[12,1536,192]{1,2,0:T(8,128)(2,1)} async-done(((bf16[3,1536,192]{1,2,0:T(8,128)(2,1)}), bf16[12,1536,192]{1,2,0:T(8,128)(2,1)}) %all-gather.7.cloned.1.call-update) | async-done | bytes 7077904 | tf_op jit(solution)/shard_map/all_gather | solution.py:213
  141.5 4.8 %fusion.6 = f32[4,192,512]{2,1,0:T(8,128)} fusion(bf16[512,1536,1]{1,0,2:T(8,128)(2,1)} %bitcast.120, bf16[4,3,1536,192]{2,3,1,0:T(8,128)(2,1)} %bitcast.130), kind=kOutput, calls=%fused_computation.18 | convolution fusion | flops 1207959552 | bytes 5505024 | tf_op jit(solution)/shard_map/nd,hdf->hnf/dot_general | solution.py:258
  146.2 7.9 %convert_reduce_fusion = bf16[512,1536]{1,0:T(8,128)(2,1)} fusion(bf16[4,3,1536,192]{2,3,1,0:T(8,128)(2,1)} %bitcast.131, f32[4,192,512]{2,1,0:T(8,128)} %fusion.6, bf16[512,1536,1]{1,0,2:T(8,128)(2,1)} %bitcast.121), kind=kOutput, calls=%fused_computation.1 | convolution fusion | flops 2422603776 | bytes 9437184 | tf_op jit(solution)/shard_map/hnf,hdf->hnd/dot_general | solution.py:265
  154.2 1.2 copy-done.1
  155.3 7.9 %all-to-all-start.3 = ((bf16[32,16,1536]{2,1,0:T(8,128)(2,1)}), bf16[32,16,1536]{2,1,0:T(8,128)(2,1)S(1)}, u32[]{:S(2)}, u32[]{:S(2)}) async-start(bf16[32,16,1536]{2,1,0:T(8,128)(2,1)} %bitcast.119), calls=%async_computation.3 | async-start | bytes 3145728 | tf_op jit(solution)/shard_map/all_to_all | solution.py:269
  163.4 4.8 %fusion.7 = f32[4,192,512]{2,1,0:T(8,128)} fusion(bf16[512,1536,1]{1,0,2:T(8,128)(2,1)} %bitcast.117, bf16[4,3,1536,192]{2,3,1,0:T(8,128)(2,1)} %bitcast.132), kind=kOutput, calls=%fused_computation.19 | convolution fusion | flops 1207959552 | bytes 5505024 | tf_op jit(solution)/shard_map/nd,hdf->hnf/dot_general | solution.py:258
  168.2 8.0 %convert_reduce_fusion.1 = bf16[512,1536]{1,0:T(8,128)(2,1)} fusion(bf16[4,3,1536,192]{2,3,1,0:T(8,128)(2,1)} %bitcast.133, f32[4,192,512]{2,1,0:T(8,128)} %fusion.7, bf16[512,1536,1]{1,0,2:T(8,128)(2,1)} %bitcast.118), kind=kOutput, calls=%fused_computation.2 | convolution fusion | flops 2422603776 | bytes 9437184 | tf_op jit(solution)/shard_map/hnf,hdf->hnd/dot_general | solution.py:265
  176.2 9.7 %all-to-all-done.3 = bf16[32,16,1536]{2,1,0:T(8,128)(2,1)S(1)} async-done(((bf16[32,16,1536]{2,1,0:T(8,128)(2,1)}), bf16[32,16,1536]{2,1,0:T(8,128)(2,1)S(1)}, u32[]{:S(2)}, u32[]{:S(2)}) %all-to-all-start.3) | async-done | bytes 1572896 | tf_op jit(solution)/shard_map/all_to_all | solution.py:269
  185.9 4.8 %all-to-all-start.1 = ((bf16[32,16,1536]{2,1,0:T(8,128)(2,1)}), bf16[32,16,1536]{2,1,0:T(8,128)(2,1)}, u32[]{:S(2)}, u32[]{:S(2)}) async-start(bf16[32,16,1536]{2,1,0:T(8,128)(2,1)} %bitcast.116), calls=%async_computation.1 | async-start | bytes 3145728 | tf_op jit(solution)/shard_map/all_to_all | solution.py:269
  191.0 3.8 %gather_fusion = f32[512]{0:T(512)S(1)} fusion(f32[128,32]{0,1:T(8,128)S(1)} %fusion.33, s32[512]{0:T(512)S(1)} %reshape.197), kind=kCustom, calls=%fused_computation | custom fusion | bytes 8192 | tf_op jit(solution)/shard_map/jit(take_along_axis)/gather | solution.py:279
  195.2 3.1 %convolution_bitcast_fusion = f32[512,1536]{1,0:T(8,128)} fusion(bf16[32,16,1536]{2,1,0:T(8,128)(2,1)S(1)} %all-to-all-done.3, s32[32,32]{0,1:T(8,128)S(1)} %multiply_add_fusion, s32[512]{0:T(512)S(1)} %multiply_add_fusion.1), kind=kOutput, calls=%fused_computation.4 | convolution fusion | flops 805830656 | bytes 4724736 | tf_op jit(solution)/shard_map/dot_general | solution.py:272
  198.3 15.3 %all-to-all-done.1 = bf16[32,16,1536]{2,1,0:T(8,128)(2,1)} async-done(((bf16[32,16,1536]{2,1,0:T(8,128)(2,1)}), bf16[32,16,1536]{2,1,0:T(8,128)(2,1)}, u32[]{:S(2)}, u32[]{:S(2)}) %all-to-all-start.1) | async-done | bytes 1572896 | tf_op jit(solution)/shard_map/all_to_all | solution.py:269
  213.5 5.5 %fusion = f32[512,1536]{1,0:T(8,128)} fusion(f32[512,1536]{1,0:T(8,128)} %convolution_bitcast_fusion, bf16[32,16,1536]{2,1,0:T(8,128)(2,1)} %all-to-all-done.1, s32[32,32]{0,1:T(8,128)S(1)} %multiply_add_fusion, s32[512]{0:T(512)S(1)} %multiply_add_fusion.1), kind=kOutput, calls=%fused_computation.6 | convolution fusion | flops 806617088 | bytes 7870464 | tf_op jit(solution)/shard_map/dot_general | solution.py:272
  219.0 4.8 %reshape.195 = f32[128,4,1536]{2,1,0:T(4,128)} reshape(f32[512,1536]{1,0:T(8,128)} %fusion) | data formatting | bytes 6291456 | tf_op jit(solution)/shard_map/reshape | solution.py:278
  223.8 4.2 %multiply_reduce_fusion = f32[128,1536]{1,0:T(8,128)S(1)} fusion(f32[128,4,1536]{2,1,0:T(4,128)} %reshape.195, f32[128,4]{1,0:T(8,128)S(1)} %copy.74), kind=kLoop, calls=%fused_computation.7 | loop fusion | flops 1376256 | bytes 3934208 | tf_op jit(solution)/shard_map/reduce_sum | solution.py:282
  228.0 0.9 fusion.21
  (58 shorter events, 3.5 us)
Async XLA Ops:
  7.2 1.4 copy-start
  7.2 2.7 %copy-start.2 = (bf16[1,128,1536]{2,1,0:T(8,128)(2,1)S(1)}, bf16[1,128,1536]{2,1,0:T(8,128)(2,1)}, u32[]{:S(2)}) copy-start(bf16[1,128,1536]{2,1,0:T(8,128)(2,1)} %param.14) | copy-start | bytes 1179652
  7.2 2.7 %copy-start.13 = (f32[1536]{0:T(1024)S(1)}, f32[1536]{0:T(1024)}, u32[]{:S(2)}) copy-start(f32[1536]{0:T(1024)} %param.20) | copy-start | bytes 18436
  7.2 2.7 %copy-start.12 = (bf16[1536,256]{1,0:T(8,128)(2,1)S(1)}, bf16[1536,256]{1,0:T(8,128)(2,1)}, u32[]{:S(2)}) copy-start(bf16[1536,256]{1,0:T(8,128)(2,1)} %param.21) | copy-start | bytes 2359300
  7.2 60.0 %all-gather.5.cloned.1.call-start = ((), (), s32[]{:S(2)}) async-start(), calls=%async_computation.4 | async-start | bytes 5898240 | tf_op jit(solution)/shard_map/all_gather | solution.py:202
  7.3 3.0 %copy-start.5 = (bf16[1,1024,256]{2,1,0:T(8,128)(2,1)S(1)}, bf16[1,1024,256]{2,1,0:T(8,128)(2,1)}, u32[]{:S(2)}) copy-start(bf16[1,1024,256]{2,1,0:T(8,128)(2,1)} %param.17) | copy-start | bytes 1572868
  7.3 3.0 %copy-start.6 = (bf16[1,1024,256]{2,1,0:T(8,128)(2,1)S(1)}, bf16[1,1024,256]{2,1,0:T(8,128)(2,1)}, u32[]{:S(2)}) copy-start(bf16[1,1024,256]{2,1,0:T(8,128)(2,1)} %param.16) | copy-start | bytes 1572868
  10.0 1.5 copy-start.9
  10.3 1.2 copy-start.10
  10.3 1.7 copy-start.3
  10.3 1.8 copy-start.4
  11.5 130.0 %all-gather.7.cloned.1.call-start = ((), (), s32[]{:S(2)}) async-start(), calls=%async_computation.5 | async-start | bytes 8847360 | tf_op jit(solution)/shard_map/all_gather | solution.py:213
  13.6 3.5 %copy-start.7 = (bf16[1,128,1536]{2,1,0:T(8,128)(2,1)S(1)}, bf16[1,128,1536]{2,1,0:T(8,128)(2,1)}, u32[]{:S(2)}) copy-start(bf16[1,128,1536]{2,1,0:T(8,128)(2,1)} %param.15) | copy-start | bytes 1179652
  81.7 3.7 %copy-start.11 = (f32[1536]{0:T(1024)S(1)}, f32[1536]{0:T(1024)}, u32[]{:S(2)}) copy-start(f32[1536]{0:T(1024)} %param.24) | copy-start | bytes 18436
  123.5 30.7 %all-to-all-start = ((bf16[32,16,1536]{2,1,0:T(8,128)(2,1)}), bf16[32,16,1536]{2,1,0:T(8,128)(2,1)S(1)}, u32[]{:S(2)}, u32[]{:S(2)}) async-start(bf16[32,16,1536]{2,1,0:T(8,128)(2,1)} %get-tuple-element.5), calls=%async_computation | async-start | bytes 3145728 | tf_op jit(solution)/shard_map/all_to_all | solution.py:254
  154.2 1.2 copy-start.1
  155.3 30.5 %all-to-all-start.3 = ((bf16[32,16,1536]{2,1,0:T(8,128)(2,1)}), bf16[32,16,1536]{2,1,0:T(8,128)(2,1)S(1)}, u32[]{:S(2)}, u32[]{:S(2)}) async-start(bf16[32,16,1536]{2,1,0:T(8,128)(2,1)} %bitcast.119), calls=%async_computation.3 | async-start | bytes 3145728 | tf_op jit(solution)/shard_map/all_to_all | solution.py:269
  176.2 14.5 %copy-start.8 = (bf16[1536,32]{0,1:T(8,128)(2,1)S(1)}, bf16[1536,32]{0,1:T(8,128)(2,1)}, u32[]{:S(2)}) copy-start(bf16[1536,32]{0,1:T(8,128)(2,1)} %param.25) | copy-start | bytes 294916
  185.9 27.6 %all-to-all-start.1 = ((bf16[32,16,1536]{2,1,0:T(8,128)(2,1)}), bf16[32,16,1536]{2,1,0:T(8,128)(2,1)}, u32[]{:S(2)}, u32[]{:S(2)}) async-start(bf16[32,16,1536]{2,1,0:T(8,128)(2,1)} %bitcast.116), calls=%async_computation.1 | async-start | bytes 3145728 | tf_op jit(solution)/shard_map/all_to_all | solution.py:269
Sparse Core Ops, SparseCore 0:
  11.6 55.5 all-gather.4
  68.9 72.5 all-gather.6

commit v4 on v2

--- a/solution.py
+++ b/solution.py
@@ -195,21 +195,23 @@
     hid_count = lax.axis_size("hid")
     group_size = QH // KVH
     normed = normalize(hidden_in[0], attn_gain).astype(jnp.bfloat16)
-    new_keys = jnp.dot(normed, key_proj, preferred_element_type=jnp.float32).astype(jnp.bfloat16)
-    new_values = jnp.dot(normed, value_proj, preferred_element_type=jnp.float32).astype(jnp.bfloat16)
+    key_width = key_proj.shape[1]
+    new_kv = jnp.dot(
+        normed, jnp.concatenate([key_proj, value_proj], axis=1), preferred_element_type=jnp.float32
+    ).astype(jnp.bfloat16)
+    new_keys = new_kv[:, :key_width]
+    new_values = new_kv[:, key_width:]
     length = lengths[0]
     cache_local = cache_keys.shape[1]
-    all_kv = lax.all_gather(
-        jnp.concatenate(
-            [
-                jnp.concatenate([cache_keys[0], new_keys], axis=0),
-                jnp.concatenate([cache_values[0], new_values], axis=0),
-            ],
-            axis=1,
-        ),
-        "hid",
+    kv_buffer = jnp.concatenate(
+        [
+            jnp.concatenate([cache_keys[0], cache_values[0]], axis=1),
+            jnp.zeros((own_count, 2 * key_width), jnp.bfloat16),
+        ],
         axis=0,
     )
+    kv_buffer = lax.dynamic_update_slice(kv_buffer, new_kv, (cache_local, 0))
+    all_kv = lax.all_gather(kv_buffer, "hid", axis=0)
     all_weights = lax.all_gather(
         jnp.concatenate([gate_up[0], down_proj[0].T[None]], axis=0), "hid", axis=0
     )

time: 221 us -> 220 us (level)
  transfers between devices with their start and end apart: 3 -> 3, of which waited for: 3 -> 3; matrix products, arithmetic and copies ran while one was open for 8% -> 8% of each run, Pallas kernels for 5% -> 4%
where the time goes in v4:
time: 220 us
  waiting for transfers between devices  85.4 us (39%)
  blocking collectives  56.6 us (26%)
  matrix products  29.8 us (14%)
  between operations  14.9 us (7%)
  Pallas kernels  9.3 us (4%)
  starting transfers between devices  8 us (4%)
  local copies, waits for them, and re-layouts  7.97 us (4%)
  other arithmetic  7.69 us (3%)
    all_to_all x1, blocking collectives, body(): lax.all_to_all(send_rows.reshape(expert_count, capacity, model_width), 'r...  56.6 us
    all_gather x1, waiting for transfers between devices, body(): all_kv = lax.all_gather(kv_buffer, 'hid', axis=0)  48.6 us
    all_to_all x1, waiting for transfers between devices, body(): lax.all_to_all(expert_out.reshape(-1, capacity, model_width), 'req', 0, 0...  34.6 us
    dot_general x1, matrix products, body(): jnp.einsum('hnf,hdf->hnd', activation, all_weights[:, 2], preferred_eleme...  12 us
    pallas_call x1, Pallas kernels, attention(): pl.pallas_call(functools.partial(attention_kernel, token_count), out_shap...  9.3 us
    all_to_all x1, starting transfers between devices, body(): lax.all_to_all(expert_out.reshape(-1, capacity, model_width), 'req', 0, 0...  7.92 us
    dot_general x1, matrix products, body(): jnp.einsum('nd,hdf->hnf', flat_rows, all_weights[:, 1], preferred_element...  6.86 us
  transfers between devices with their start and end apart: 3, of which 3 were waited for; matrix products, arithmetic and copies ran while one was open for 8% of the time, Pallas kernels for 4%

profile of v4, /device:TPU:1, one launch (start us, length us, event | category | flops | bytes accessed | tf_op | source)
XLA Modules:
  0.0 219.8 jit_solution(6843729412735485354)
XLA Ops:
  7.2 1.2 fusion.20
  8.5 2.1 fusion.16
  10.6 1.1 pad_maximum_fusion.1
  11.8 1.5 pad_maximum_fusion
  13.3 0.7 fusion.33
  14.0 0.1 copy.74
  14.2 0.1 reshape.183
  15.0 1.2 reduce-window.6
  16.2 0.2 slice_reduce_fusion
  16.4 0.1 fusion.29
  16.5 0.1 reduce_sum.63
  16.7 0.2 copy.69
  17.0 0.9 copy.70
  17.9 0.6 pad_add_fusion.scalars
  18.5 0.4 fusion.7
  18.9 48.6 %all-gather.5.cloned.1.call-done = bf16[4608,512]{1,0:T(8,128)(2,1)} async-done(((bf16[1152,512]{1,0:T(8,128)(2,1)}), bf16[4608,512]{1,0:T(8,128)(2,1)}) %all-gather.5.cloned.1.call-update) | async-done | bytes 4718608 | tf_op jit(solution)/shard_map/all_gather | solution.py:214
  67.4 9.3 %shard_map.157 = bf16[2,768,128]{2,1,0:T(8,128)(2,1)} custom-call(s32[2]{0:T(128)} %pad_add_fusion.scalars, bf16[2,768,128]{2,1,0:T(8,128)(2,1)} %bitcast.108, bf16[4,1152,512]{2,1,0:T(8,128)(2,1)} %bitcast.102, bf16[4,1152,512]{2,1,0:T(8,128)(2,1)} %bitcast.103), custom_call_target="tpu_custom_call" | custom-call | tf_op jit(solution)/shard_map/pallas_call | solution.py:151
  76.7 1.2 copy.71
  78.0 3.8 %multiply_reduce_fusion = (f32[128]{0:T(128)S(1)}, f32[128,1536]{1,0:T(8,128)S(1)}) fusion(bf16[128,1536]{0,1:T(8,128)(2,1)S(1)} %bitcast.110, bf16[1536,1536]{1,0:T(8,128)(2,1)} %param.23, bf16[1,128,1536]{2,1,0:T(8,128)(2,1)S(1)} %copy-done.1), kind=kOutput, calls=%fused_computation.35 | convolution fusion | flops 605159296 | bytes 6291968 | tf_op jit(solution)/shard_map/dot_general | solution.py:232
  81.8 1.0 convolution_convert_fusion.1
  82.9 56.6 %all_to_all.10 = bf16[32,32,1536]{2,1,0:T(8,128)(2,1)} all-to-all(bf16[32,32,1536]{2,1,0:T(8,128)(2,1)S(1)} %bitcast.104), channel_id=1, replica_groups=mesh['req'=32,'hid'=4] {'req'}, dimensions={0} | all-to-all | bytes 6291456 | tf_op jit(solution)/shard_map/all_to_all | solution.py:250
  139.5 2.2 all-gather.7.cloned.1.call-done
  141.7 6.9 %fusion.3 = f32[4,192,1024]{2,1,0:T(8,128)} fusion(bf16[1024,1536,1]{1,0,2:T(8,128)(2,1)} %bitcast.106, bf16[4,3,1536,192]{2,3,1,0:T(8,128)(2,1)} %bitcast.116), kind=kOutput, calls=%fused_computation.11 | convolution fusion | flops 2415919104 | bytes 8650752 | tf_op jit(solution)/shard_map/nd,hdf->hnf/dot_general | solution.py:257
  148.6 12.0 %fusion = bf16[1024,1536]{1,0:T(8,128)(2,1)} fusion(bf16[4,3,1536,192]{2,3,1,0:T(8,128)(2,1)} %bitcast.117, f32[4,192,1024]{2,1,0:T(8,128)} %fusion.3, bf16[1024,1536,1]{1,0,2:T(8,128)(2,1)} %bitcast.107), kind=kOutput, calls=%fused_computation.5 | convolution fusion | flops 4845207552 | bytes 14155776 | tf_op jit(solution)/shard_map/hnf,hdf->hnd/dot_general | solution.py:261
  160.5 7.9 %all-to-all-start.1 = ((bf16[32,32,1536]{2,1,0:T(8,128)(2,1)}), bf16[32,32,1536]{2,1,0:T(8,128)(2,1)}, u32[]{:S(2)}, u32[]{:S(2)}) async-start(bf16[32,32,1536]{2,1,0:T(8,128)(2,1)} %bitcast.105), calls=%async_computation.1 | async-start | bytes 6291456 | tf_op jit(solution)/shard_map/all_to_all | solution.py:265
  168.5 0.1 copy.72
  168.7 0.7 slice_bitcast_fusion.10
  169.4 0.3 fusion.37
  169.6 3.8 %gather_fusion = f32[512]{0:T(512)S(1)} fusion(f32[128,32]{0,1:T(8,128)S(1)} %fusion.37, s32[512]{0:T(512)S(1)} %reshape.190), kind=kCustom, calls=%fused_computation | custom fusion | bytes 8192 | tf_op jit(solution)/shard_map/jit(take_along_axis)/gather | solution.py:273
  173.7 34.6 %all-to-all-done.1 = bf16[32,32,1536]{2,1,0:T(8,128)(2,1)} async-done(((bf16[32,32,1536]{2,1,0:T(8,128)(2,1)}), bf16[32,32,1536]{2,1,0:T(8,128)(2,1)}, u32[]{:S(2)}, u32[]{:S(2)}) %all-to-all-start.1) | async-done | bytes 3145760 | tf_op jit(solution)/shard_map/all_to_all | solution.py:265
  208.3 3.8 %fusion.8 = f32[128,1536]{1,0:T(8,128)S(1)} fusion(bf16[1024,1536,1]{1,0,2:T(8,128)(2,1)} %bitcast.30, f32[128,4]{0,1:T(4,128)S(1)} %multiply_divide_fusion, s32[128,4]{0,1:T(4,128)S(1)} %fusion.34), kind=kOutput, calls=%fused_computation.19 | convolution fusion | flops 1612513280 | bytes 3936256 | tf_op jit(solution)/shard_map/dot_general | solution.py:268
  212.1 0.9 fusion.23
  (33 shorter events, 0.7 us)
Async XLA Ops:
  7.2 162.2 %copy-start = (bf16[1536,32]{0,1:T(8,128)(2,1)S(1)}, bf16[1536,32]{0,1:T(8,128)(2,1)}, u32[]{:S(2)}) copy-start(bf16[1536,32]{0,1:T(8,128)(2,1)} %param.25) | copy-start | bytes 294916
  7.2 3.4 %copy-start.4 = (bf16[1,1024,256]{2,1,0:T(8,128)(2,1)S(1)}, bf16[1,1024,256]{2,1,0:T(8,128)(2,1)}, u32[]{:S(2)}) copy-start(bf16[1,1024,256]{2,1,0:T(8,128)(2,1)} %param.17) | copy-start | bytes 1572868
  7.2 3.4 %copy-start.5 = (bf16[1,1024,256]{2,1,0:T(8,128)(2,1)S(1)}, bf16[1,1024,256]{2,1,0:T(8,128)(2,1)}, u32[]{:S(2)}) copy-start(bf16[1,1024,256]{2,1,0:T(8,128)(2,1)} %param.16) | copy-start | bytes 1572868
  7.2 60.2 %all-gather.5.cloned.1.call-start = ((), (), s32[]{:S(2)}) async-start(), calls=%async_computation.2 | async-start | bytes 5898240 | tf_op jit(solution)/shard_map/all_gather | solution.py:214
  8.5 3.3 %copy-start.2 = (bf16[1,2,1536,192]{2,3,1,0:T(8,128)(2,1)S(1)}, bf16[1,2,1536,192]{2,3,1,0:T(8,128)(2,1)}, u32[]{:S(2)}) copy-start(bf16[1,2,1536,192]{2,3,1,0:T(8,128)(2,1)} %param.26) | copy-start | bytes 3538948
  8.5 3.3 %copy-start.3 = (bf16[1,192,1536]{2,1,0:T(8,128)(2,1)S(1)}, bf16[1,192,1536]{2,1,0:T(8,128)(2,1)}, u32[]{:S(2)}) copy-start(bf16[1,192,1536]{2,1,0:T(8,128)(2,1)} %param.27) | copy-start | bytes 1769476
  11.7 5.0 %copy-start.6 = (bf16[1,128,1536]{2,1,0:T(8,128)(2,1)S(1)}, bf16[1,128,1536]{2,1,0:T(8,128)(2,1)}, u32[]{:S(2)}) copy-start(bf16[1,128,1536]{2,1,0:T(8,128)(2,1)} %param.15) | copy-start | bytes 1179652
  11.7 130.0 %all-gather.7.cloned.1.call-start = ((), (), s32[]{:S(2)}) async-start(), calls=%async_computation.3 | async-start | bytes 8847360 | tf_op jit(solution)/shard_map/all_gather | solution.py:215
  67.4 10.5 %copy-start.1 = (bf16[1,128,1536]{2,1,0:T(8,128)(2,1)S(1)}, bf16[1,128,1536]{2,1,0:T(8,128)(2,1)}, u32[]{:S(2)}) copy-start(bf16[1,128,1536]{2,1,0:T(8,128)(2,1)} %param.14) | copy-start | bytes 1179652
  78.0 3.8 %copy-start.7 = (f32[1536]{0:T(1024)S(1)}, f32[1536]{0:T(1024)}, u32[]{:S(2)}) copy-start(f32[1536]{0:T(1024)} %param.24) | copy-start | bytes 18436
  160.5 47.7 %all-to-all-start.1 = ((bf16[32,32,1536]{2,1,0:T(8,128)(2,1)}), bf16[32,32,1536]{2,1,0:T(8,128)(2,1)}, u32[]{:S(2)}, u32[]{:S(2)}) async-start(bf16[32,32,1536]{2,1,0:T(8,128)(2,1)} %bitcast.105), calls=%async_computation.1 | async-start | bytes 6291456 | tf_op jit(solution)/shard_map/all_to_all | solution.py:265
Sparse Core Ops, SparseCore 0:
  11.8 55.5 all-gather.4
  69.1 72.5 all-gather.6

commit v5 on v4

--- a/solution.py
+++ b/solution.py
@@ -79,12 +79,14 @@
     )
 
 
-def attention_kernel(token_count, scalars, q_ref, k_ref, v_ref, o_ref, m_ref, l_ref, acc_ref, s_ref):
+def attention_kernel(
+    token_count, scalars, q_ref, k_ref, v_ref, kn_ref, vn_ref, o_ref, m_ref, l_ref, acc_ref, s_ref
+):
     length = scalars[0]
     hid_index = scalars[1]
-    parts, part_rows, _ = k_ref.shape
+    parts, cache_rows, _ = k_ref.shape
+    part_rows = cache_rows + token_count
     rows = q_ref.shape[1]
-    cache_rows = part_rows - token_count
     q = q_ref[0]
     m_ref[...] = jnp.full(m_ref.shape, MASKED_SCORE, jnp.float32)
     l_ref[...] = jnp.zeros(l_ref.shape, jnp.float32)
@@ -114,7 +116,7 @@
         return key_pos <= hid_index * token_count + row_ids % token_count
 
     def first_pass(part, first, size, is_cache, masked):
-        k = k_ref[part, pl.ds(first, size), :]
+        k = k_ref[part, pl.ds(first, size), :] if is_cache else kn_ref[part]
         raw = lax.dot_general(q, k, (((1,), (1,)), ((), ())), preferred_element_type=jnp.float32)
         s = raw * HD ** (-0.5)
         if masked:
@@ -135,18 +137,20 @@
         def _():
             w = jnp.exp(s_ref[:, pl.ds(part * part_rows + first, size)] - m_ref[...])
             l_ref[...] += jnp.sum(w, axis=-1, keepdims=True)
-            v = v_ref[part, pl.ds(first, size), :]
+            v = v_ref[part, pl.ds(first, size), :] if is_cache else vn_ref[part]
             acc_ref[...] += jnp.dot(w.astype(jnp.bfloat16), v, preferred_element_type=jnp.float32)
 
     o_ref[0] = (acc_ref[...] / l_ref[...]).astype(o_ref.dtype)
 
 
-def attention(grouped, all_kv, length, hid_index, token_count, interpret=False):
+def attention(grouped, all_kv, new_kv, length, hid_index, token_count, interpret=False):
     groups, rows, head = grouped.shape
-    parts, part_rows, _ = all_kv.shape
+    parts, cache_rows, _ = all_kv.shape
     scalars = jnp.stack([length, hid_index]).astype(jnp.int32)
-    k_spec = pl.BlockSpec((parts, part_rows, head), lambda g, s: (0, 0, g))
-    v_spec = pl.BlockSpec((parts, part_rows, head), lambda g, s: (0, 0, groups + g))
+    k_spec = pl.BlockSpec((parts, cache_rows, head), lambda g, s: (0, 0, g))
+    v_spec = pl.BlockSpec((parts, cache_rows, head), lambda g, s: (0, 0, groups + g))
+    kn_spec = pl.BlockSpec((parts, token_count, head), lambda g, s: (0, 0, g))
+    vn_spec = pl.BlockSpec((parts, token_count, head), lambda g, s: (0, 0, groups + g))
     row_spec = pl.BlockSpec((1, rows, head), lambda g, s: (g, 0, 0))
     return pl.pallas_call(
         functools.partial(attention_kernel, token_count),
@@ -154,17 +158,17 @@
         grid_spec=pltpu.PrefetchScalarGridSpec(
             num_scalar_prefetch=1,
             grid=(groups,),
-            in_specs=[row_spec, k_spec, v_spec],
+            in_specs=[row_spec, k_spec, v_spec, kn_spec, vn_spec],
             out_specs=row_spec,
             scratch_shapes=[
                 pltpu.VMEM((rows, 1), jnp.float32),
                 pltpu.VMEM((rows, 1), jnp.float32),
                 pltpu.VMEM((rows, head), jnp.float32),
-                pltpu.VMEM((rows, parts * part_rows), jnp.float32),
+                pltpu.VMEM((rows, parts * (cache_rows + token_count)), jnp.float32),
             ],
         ),
         interpret=interpret,
-    )(scalars, grouped, all_kv, all_kv)
+    )(scalars, grouped, all_kv, all_kv, new_kv, new_kv)
 
 
 def expert_activation(row_data, gate_weights):
@@ -203,15 +207,21 @@
     new_values = new_kv[:, key_width:]
     length = lengths[0]
     cache_local = cache_keys.shape[1]
-    kv_buffer = jnp.concatenate(
-        [
-            jnp.concatenate([cache_keys[0], cache_values[0]], axis=1),
-            jnp.zeros((own_count, 2 * key_width), jnp.bfloat16),
-        ],
-        axis=0,
-    )
-    kv_buffer = lax.dynamic_update_slice(kv_buffer, new_kv, (cache_local, 0))
-    all_kv = lax.all_gather(kv_buffer, "hid", axis=0)
+    all_kv = lax.all_gather(
+        jnp.concatenate([cache_keys[0], cache_values[0]], axis=1), "hid", axis=0
+    )
+    received = [new_kv]
+    for shift in range(1, hid_count):
+        pairs = [(source, source + shift) for source in range(hid_count - shift)]
+        received.append(lax.ppermute(new_kv, "hid", pairs))
+    new_parts = []
+    for part in range(hid_count):
+        distance = hid_index - part
+        chosen = received[-1]
+        for shift in range(hid_count - 2, -1, -1):
+            chosen = jnp.where(distance == shift, received[shift], chosen)
+        new_parts.append(chosen)
+    new_parts = jnp.stack(new_parts)
     all_weights = lax.all_gather(
         jnp.concatenate([gate_up[0], down_proj[0].T[None]], axis=0), "hid", axis=0
     )
@@ -222,7 +232,7 @@
         .reshape(KVH, group_size * own_count, HD)
     )
     attended = (
-        attention(grouped, all_kv, length, hid_index, own_count)
+        attention(grouped, all_kv, new_parts, length, hid_index, own_count)
         .reshape(KVH, group_size, own_count, HD)
         .transpose(2, 0, 1, 3)
         .reshape(own_count, QH * HD)

time: 220 us -> 215 us (0.977)
  waiting for transfers between devices: 85.4 us -> 68.5 us
  starting transfers between devices: 8 us -> 17 us
  Pallas kernels: 9.3 us -> 15.2 us
  blocking collectives: 56.6 us -> 52.7 us
    all_gather x1, waiting for transfers between devices: 48.6 us -> 32.4 us  [body(): lax.all_gather(jnp.concatenate([cache_keys[0], cache_values[0]], axis=1),...]
    ppermute x0 -> x3, starting transfers between devices: none -> 8.99 us  [body(): received.append(lax.ppermute(new_kv, 'hid', pairs))]
    pallas_call x1, Pallas kernels: 9.3 us -> 15.2 us  [attention(): pl.pallas_call(functools.partial(attention_kernel, token_count), out_shap...]
    all_to_all x1, blocking collectives: 56.6 us -> 52.7 us  [body(): lax.all_to_all(send_rows.reshape(expert_count, capacity, model_width), 'r...]
    concatenate x0 -> x1, other arithmetic: none -> 2.43 us  [body(): jnp.concatenate([cache_keys[0], cache_values[0]], axis=1)]
  transfers between devices with their start and end apart: 3 -> 6, of which waited for: 3 -> 3; matrix products, arithmetic and copies ran while one was open for 8% -> 9% of each run, Pallas kernels for 4% -> 7%
where the time goes in v5:
time: 215 us; the launch traced here: 214 us
  waiting for transfers between devices  68.5 us (32%)
  blocking collectives  52.7 us (25%)
  matrix products  29.2 us (14%)
  starting transfers between devices  17 us (8%)
  Pallas kernels  15.2 us (7%)
  between operations  15 us (7%)
  other arithmetic  8.82 us (4%)
  local copies, waits for them, and re-layouts  8.03 us (4%)
    all_to_all x1, blocking collectives, body(): lax.all_to_all(send_rows.reshape(expert_count, capacity, model_width), 'r...  52.7 us
    all_to_all x1, waiting for transfers between devices, body(): lax.all_to_all(expert_out.reshape(-1, capacity, model_width), 'req', 0, 0...  34.6 us
    all_gather x1, waiting for transfers between devices, body(): lax.all_gather(jnp.concatenate([cache_keys[0], cache_values[0]], axis=1),...  32.4 us
    pallas_call x1, Pallas kernels, attention(): pl.pallas_call(functools.partial(attention_kernel, token_count), out_shap...  15.2 us
    dot_general x1, matrix products, body(): jnp.einsum('hnf,hdf->hnd', activation, all_weights[:, 2], preferred_eleme...  12 us
    ppermute x3, starting transfers between devices, body(): received.append(lax.ppermute(new_kv, 'hid', pairs))  8.99 us
    all_to_all x1, starting transfers between devices, body(): lax.all_to_all(expert_out.reshape(-1, capacity, model_width), 'req', 0, 0...  7.91 us
    dot_general x1, matrix products, body(): jnp.einsum('nd,hdf->hnf', flat_rows, all_weights[:, 1], preferred_element...  6.86 us
  transfers between devices with their start and end apart: 6, of which 3 were waited for; matrix products, arithmetic and copies ran while one was open for 9% of the time, Pallas kernels for 7%

profile of v5, /device:TPU:1, one launch (start us, length us, event | category | flops | bytes accessed | tf_op | source)
XLA Modules:
  0.0 214.4 jit_solution(14922514725628851688)
XLA Ops:
  7.2 2.4 %pad_maximum_fusion.1 = bf16[1024,512]{1,0:T(8,128)(2,1)} fusion(bf16[1024,256]{1,0:T(8,128)(2,1)} %bitcast.122, bf16[1024,256]{1,0:T(8,128)(2,1)} %bitcast.123), kind=kLoop, calls=%fused_computation.28 | loop fusion | flops 2097152 | bytes 2097152 | tf_op jit(solution)/shard_map/concatenate | solution.py:211
  9.8 1.4 pad_maximum_fusion
  11.2 0.2 fusion.20
  11.4 1.6 fusion.16
  12.9 5.2 %collective-permute-start.2 = (bf16[128,512]{1,0:T(8,128)(2,1)S(1)}, bf16[128,512]{1,0:T(8,128)(2,1)S(1)}, u32[]{:S(2)}, u32[]{:S(2)}) collective-permute-start(bf16[128,512]{1,0:T(8,128)(2,1)S(1)} %fusion.16), channel_id=1, source_target_pairs={{0,3},{4,7},{8,11},{12,15},{16,19},{20,23},{24,27},{28,31},{32,35}... | collective-permute-start | bytes 393224 | tf_op jit(solution)/shard_map/ppermute | solution.py:216
  18.2 1.3 collective-permute-start.1
  19.5 2.5 %collective-permute-start = (bf16[128,512]{1,0:T(8,128)(2,1)S(1)}, bf16[128,512]{1,0:T(8,128)(2,1)S(1)}, u32[]{:S(2)}, u32[]{:S(2)}) collective-permute-start(bf16[128,512]{1,0:T(8,128)(2,1)S(1)} %fusion.16), channel_id=1, source_target_pairs={{0,1},{1,2},{2,3},{4,5},{5,6},{6,7},{8,9},{9,10},{10,11},{12,13},{... | collective-permute-start | bytes 393224 | tf_op jit(solution)/shard_map/ppermute | solution.py:216
  22.0 0.7 fusion.33
  23.7 1.2 reduce-window.6
  24.9 0.2 slice_reduce_fusion
  25.4 0.2 copy.69
  25.7 0.9 copy.70
  26.6 0.6 pad_add_fusion.scalars
  27.2 0.4 fusion.7
  27.7 0.9 pad_maximum_fusion.2.kn_ref.vn_ref
  28.5 32.4 %all-gather.5.cloned.1.call-done = bf16[4096,512]{1,0:T(8,128)(2,1)} async-done(((bf16[1024,512]{1,0:T(8,128)(2,1)}), bf16[4096,512]{1,0:T(8,128)(2,1)}) %all-gather.5.cloned.1.call-update) | async-done | bytes 4194320 | tf_op jit(solution)/shard_map/all_gather | solution.py:210
  60.9 15.2 %shard_map.157 = bf16[2,768,128]{2,1,0:T(8,128)(2,1)} custom-call(s32[2]{0:T(128)} %pad_add_fusion.scalars, bf16[2,768,128]{2,1,0:T(8,128)(2,1)} %bitcast.116, bf16[4,1024,512]{2,1,0:T(8,128)(2,1)} %bitcast.110, bf16[4,1024,512]{2,1,0:T(8,128)(2,1)} %bitcast.111, bf16[4,128,512]{2,1,0:T(8,128)(2,1)} %pad_maximum_fusion.2.kn_ref.vn_ref, ...), custom_call_target="tpu_custom_call" | custom-call | tf_op jit(solution)/shard_map/pallas_call | solution.py:155
  76.1 1.3 copy.71
  77.4 3.6 %multiply_reduce_fusion = (f32[128]{0:T(128)S(1)}, f32[128,1536]{1,0:T(8,128)S(1)}) fusion(bf16[128,1536]{0,1:T(8,128)(2,1)S(1)} %bitcast.118, bf16[1536,1536]{1,0:T(8,128)(2,1)} %param.23, bf16[1,128,1536]{2,1,0:T(8,128)(2,1)S(1)} %copy-done.1), kind=kOutput, calls=%fused_computation.35 | convolution fusion | flops 605159296 | bytes 6291968 | tf_op jit(solution)/shard_map/dot_general | solution.py:242
  81.1 1.0 convolution_convert_fusion.1
  82.2 52.7 %all_to_all.10 = bf16[32,32,1536]{2,1,0:T(8,128)(2,1)} all-to-all(bf16[32,32,1536]{2,1,0:T(8,128)(2,1)S(1)} %bitcast.112), channel_id=1, replica_groups=mesh['req'=32,'hid'=4] {'req'}, dimensions={0} | all-to-all | bytes 6291456 | tf_op jit(solution)/shard_map/all_to_all | solution.py:260
  134.9 1.5 all-gather.7.cloned.1.call-done
  136.4 6.9 %fusion.3 = f32[4,192,1024]{2,1,0:T(8,128)} fusion(bf16[1024,1536,1]{1,0,2:T(8,128)(2,1)} %bitcast.114, bf16[4,3,1536,192]{2,3,1,0:T(8,128)(2,1)} %bitcast.124), kind=kOutput, calls=%fused_computation.11 | convolution fusion | flops 2415919104 | bytes 8650752 | tf_op jit(solution)/shard_map/nd,hdf->hnf/dot_general | solution.py:267
  143.2 12.0 %fusion = bf16[1024,1536]{1,0:T(8,128)(2,1)} fusion(bf16[4,3,1536,192]{2,3,1,0:T(8,128)(2,1)} %bitcast.125, f32[4,192,1024]{2,1,0:T(8,128)} %fusion.3, bf16[1024,1536,1]{1,0,2:T(8,128)(2,1)} %bitcast.115), kind=kOutput, calls=%fused_computation.5 | convolution fusion | flops 4845207552 | bytes 14155776 | tf_op jit(solution)/shard_map/hnf,hdf->hnd/dot_general | solution.py:271
  155.2 7.9 %all-to-all-start.1 = ((bf16[32,32,1536]{2,1,0:T(8,128)(2,1)}), bf16[32,32,1536]{2,1,0:T(8,128)(2,1)}, u32[]{:S(2)}, u32[]{:S(2)}) async-start(bf16[32,32,1536]{2,1,0:T(8,128)(2,1)} %bitcast.113), calls=%async_computation.1 | async-start | bytes 6291456 | tf_op jit(solution)/shard_map/all_to_all | solution.py:275
  163.1 0.1 copy.72
  163.3 0.7 slice_bitcast_fusion.10
  164.0 0.3 fusion.37
  164.3 3.8 %gather_fusion = f32[512]{0:T(512)S(1)} fusion(f32[128,32]{0,1:T(8,128)S(1)} %fusion.37, s32[512]{0:T(512)S(1)} %reshape.190), kind=kCustom, calls=%fused_computation | custom fusion | bytes 8192 | tf_op jit(solution)/shard_map/jit(take_along_axis)/gather | solution.py:283
  168.3 34.6 %all-to-all-done.1 = bf16[32,32,1536]{2,1,0:T(8,128)(2,1)} async-done(((bf16[32,32,1536]{2,1,0:T(8,128)(2,1)}), bf16[32,32,1536]{2,1,0:T(8,128)(2,1)}, u32[]{:S(2)}, u32[]{:S(2)}) %all-to-all-start.1) | async-done | bytes 3145760 | tf_op jit(solution)/shard_map/all_to_all | solution.py:275
  202.9 3.8 %fusion.8 = f32[128,1536]{1,0:T(8,128)S(1)} fusion(bf16[1024,1536,1]{1,0,2:T(8,128)(2,1)} %bitcast.34, f32[128,4]{0,1:T(4,128)S(1)} %multiply_divide_fusion, s32[128,4]{0,1:T(4,128)S(1)} %fusion.34), kind=kOutput, calls=%fused_computation.19 | convolution fusion | flops 1612513280 | bytes 3936256 | tf_op jit(solution)/shard_map/dot_general | solution.py:278
  206.7 0.9 fusion.23
  (41 shorter events, 1.2 us)
Async XLA Ops:
  7.2 156.8 %copy-start = (bf16[1536,32]{0,1:T(8,128)(2,1)S(1)}, bf16[1536,32]{0,1:T(8,128)(2,1)}, u32[]{:S(2)}) copy-start(bf16[1536,32]{0,1:T(8,128)(2,1)} %param.25) | copy-start | bytes 294916
  7.2 2.6 %copy-start.3 = (bf16[1,192,1536]{2,1,0:T(8,128)(2,1)S(1)}, bf16[1,192,1536]{2,1,0:T(8,128)(2,1)}, u32[]{:S(2)}) copy-start(bf16[1,192,1536]{2,1,0:T(8,128)(2,1)} %param.27) | copy-start | bytes 1769476
  7.2 2.6 %copy-start.2 = (bf16[1,2,1536,192]{2,3,1,0:T(8,128)(2,1)S(1)}, bf16[1,2,1536,192]{2,3,1,0:T(8,128)(2,1)}, u32[]{:S(2)}) copy-start(bf16[1,2,1536,192]{2,3,1,0:T(8,128)(2,1)} %param.26) | copy-start | bytes 3538948
  7.2 53.7 %all-gather.5.cloned.1.call-start = ((), (), s32[]{:S(2)}) async-start(), calls=%async_computation.2 | async-start | bytes 5242880 | tf_op jit(solution)/shard_map/all_gather | solution.py:210
  9.7 1.5 copy-start.1
  9.7 1.7 copy-start.6
  9.7 1.7 copy-start.7
  9.7 126.7 %all-gather.7.cloned.1.call-start = ((), (), s32[]{:S(2)}) async-start(), calls=%async_computation.3 | async-start | bytes 8847360 | tf_op jit(solution)/shard_map/all_gather | solution.py:225
  11.2 14.3 %copy-start.4 = (bf16[1,128,1536]{2,1,0:T(8,128)(2,1)S(1)}, bf16[1,128,1536]{2,1,0:T(8,128)(2,1)}, u32[]{:S(2)}) copy-start(bf16[1,128,1536]{2,1,0:T(8,128)(2,1)} %param.15) | copy-start | bytes 1179652
  12.9 14.6 %collective-permute-start.2 = (bf16[128,512]{1,0:T(8,128)(2,1)S(1)}, bf16[128,512]{1,0:T(8,128)(2,1)S(1)}, u32[]{:S(2)}, u32[]{:S(2)}) collective-permute-start(bf16[128,512]{1,0:T(8,128)(2,1)S(1)} %fusion.16), channel_id=1, source_target_pairs={{0,3},{4,7},{8,11},{12,15},{16,19},{20,23},{24,27},{28,31},{32,35}... | collective-permute-start | bytes 393224 | tf_op jit(solution)/shard_map/ppermute | solution.py:216
  18.2 9.4 %collective-permute-start.1 = (bf16[128,512]{1,0:T(8,128)(2,1)S(1)}, bf16[128,512]{1,0:T(8,128)(2,1)S(1)}, u32[]{:S(2)}, u32[]{:S(2)}) collective-permute-start(bf16[128,512]{1,0:T(8,128)(2,1)S(1)} %fusion.16), channel_id=1, source_target_pairs={{0,2},{1,3},{4,6},{5,7},{8,10},{9,11},{12,14},{13,15},{16,18},{17,... | collective-permute-start | bytes 393224 | tf_op jit(solution)/shard_map/ppermute | solution.py:216
  19.5 8.1 %collective-permute-start = (bf16[128,512]{1,0:T(8,128)(2,1)S(1)}, bf16[128,512]{1,0:T(8,128)(2,1)S(1)}, u32[]{:S(2)}, u32[]{:S(2)}) collective-permute-start(bf16[128,512]{1,0:T(8,128)(2,1)S(1)} %fusion.16), channel_id=1, source_target_pairs={{0,1},{1,2},{2,3},{4,5},{5,6},{6,7},{8,9},{9,10},{10,11},{12,13},{... | collective-permute-start | bytes 393224 | tf_op jit(solution)/shard_map/ppermute | solution.py:216
  77.4 3.7 %copy-start.5 = (f32[1536]{0:T(1024)S(1)}, f32[1536]{0:T(1024)}, u32[]{:S(2)}) copy-start(f32[1536]{0:T(1024)} %param.24) | copy-start | bytes 18436
  155.2 47.7 %all-to-all-start.1 = ((bf16[32,32,1536]{2,1,0:T(8,128)(2,1)}), bf16[32,32,1536]{2,1,0:T(8,128)(2,1)}, u32[]{:S(2)}, u32[]{:S(2)}) async-start(bf16[32,32,1536]{2,1,0:T(8,128)(2,1)} %bitcast.113), calls=%async_computation.1 | async-start | bytes 6291456 | tf_op jit(solution)/shard_map/all_to_all | solution.py:275
Sparse Core Ops, SparseCore 0:
  9.8 51.0 all-gather.4
  62.6 73.7 all-gather.6

commit v6 on v5

--- a/solution.py
+++ b/solution.py
@@ -80,75 +80,99 @@
 
 
 def attention_kernel(
-    token_count, scalars, q_ref, k_ref, v_ref, kn_ref, vn_ref, o_ref, m_ref, l_ref, acc_ref, s_ref
+    token_count,
+    scalars,
+    q_ref,
+    k_ref,
+    v0_ref,
+    v1_ref,
+    v2_ref,
+    v3_ref,
+    kn_ref,
+    vn_ref,
+    o_ref,
+    m_ref,
+    l_ref,
+    acc_ref,
+    s_ref,
 ):
     length = scalars[0]
     hid_index = scalars[1]
     parts, cache_rows, _ = k_ref.shape
-    part_rows = cache_rows + token_count
     rows = q_ref.shape[1]
+    v_refs = (v0_ref, v1_ref, v2_ref, v3_ref)
     q = q_ref[0]
     m_ref[...] = jnp.full(m_ref.shape, MASKED_SCORE, jnp.float32)
     l_ref[...] = jnp.zeros(l_ref.shape, jnp.float32)
     acc_ref[...] = jnp.zeros(acc_ref.shape, jnp.float32)
     blocks = []
+    for shift in range(parts):
+        for first in range(0, cache_rows, KEY_BLOCK):
+            blocks.append((shift, first, min(KEY_BLOCK, cache_rows - first), True))
     for part in range(parts):
-        for first in range(0, cache_rows, KEY_BLOCK):
-            blocks.append((part, first, min(KEY_BLOCK, cache_rows - first), True))
-        blocks.append((part, cache_rows, token_count, False))
-
-    def live(part, first, size, is_cache):
+        blocks.append((part, 0, token_count, False))
+
+    def part_of(index, is_cache):
+        return (hid_index - index + parts) % parts if is_cache else index
+
+    def slot(index, first, is_cache):
+        return index * cache_rows + first if is_cache else parts * cache_rows + index * token_count
+
+    def live(index, first, size, is_cache):
         if is_cache:
-            return part * cache_rows + first < length
-        return part <= hid_index
-
-    def whole(part, first, size, is_cache):
+            return part_of(index, True) * cache_rows + first < length
+        return index <= hid_index
+
+    def whole(index, first, size, is_cache):
         if is_cache:
-            return part * cache_rows + first + size <= length
-        return part < hid_index
-
-    def visible(part, first, size, is_cache):
+            return part_of(index, True) * cache_rows + first + size <= length
+        return index < hid_index
+
+    def visible(index, first, size, is_cache):
         if is_cache:
-            pos = part * cache_rows + first + lax.broadcasted_iota(jnp.int32, (1, size), 1)
-            return pos < length
-        key_pos = part * token_count + lax.broadcasted_iota(jnp.int32, (1, size), 1)
+            start = part_of(index, True) * cache_rows + first
+            return start + lax.broadcasted_iota(jnp.int32, (1, size), 1) < length
+        key_pos = index * token_count + lax.broadcasted_iota(jnp.int32, (1, size), 1)
         row_ids = lax.broadcasted_iota(jnp.int32, (rows, 1), 0)
         return key_pos <= hid_index * token_count + row_ids % token_count
 
-    def first_pass(part, first, size, is_cache, masked):
-        k = k_ref[part, pl.ds(first, size), :] if is_cache else kn_ref[part]
+    def first_pass(index, first, size, is_cache, masked):
+        if is_cache:
+            k = k_ref[part_of(index, True), pl.ds(first, size), :]
+        else:
+            k = kn_ref[index]
         raw = lax.dot_general(q, k, (((1,), (1,)), ((), ())), preferred_element_type=jnp.float32)
         s = raw * HD ** (-0.5)
         if masked:
-            s = jnp.where(visible(part, first, size, is_cache), s, MASKED_SCORE)
-        s_ref[:, pl.ds(part * part_rows + first, size)] = s
+            s = jnp.where(visible(index, first, size, is_cache), s, MASKED_SCORE)
+        s_ref[:, pl.ds(slot(index, first, is_cache), size)] = s
         m_ref[...] = jnp.maximum(m_ref[...], jnp.max(s, axis=-1, keepdims=True))
 
-    for part, first, size, is_cache in blocks:
-        is_whole = whole(part, first, size, is_cache)
-        pl.when(is_whole)(functools.partial(first_pass, part, first, size, is_cache, False))
-        pl.when(jnp.logical_and(live(part, first, size, is_cache), jnp.logical_not(is_whole)))(
-            functools.partial(first_pass, part, first, size, is_cache, True)
+    for index, first, size, is_cache in blocks:
+        is_whole = whole(index, first, size, is_cache)
+        pl.when(is_whole)(functools.partial(first_pass, index, first, size, is_cache, False))
+        pl.when(jnp.logical_and(live(index, first, size, is_cache), jnp.logical_not(is_whole)))(
+            functools.partial(first_pass, index, first, size, is_cache, True)
         )
 
-    for part, first, size, is_cache in blocks:
-
-        @pl.when(live(part, first, size, is_cache))
+    for index, first, size, is_cache in blocks:
+
+        @pl.when(live(index, first, size, is_cache))
         def _():
-            w = jnp.exp(s_ref[:, pl.ds(part * part_rows + first, size)] - m_ref[...])
+            w = jnp.exp(s_ref[:, pl.ds(slot(index, first, is_cache), size)] - m_ref[...])
             l_ref[...] += jnp.sum(w, axis=-1, keepdims=True)
-            v = v_ref[part, pl.ds(first, size), :] if is_cache else vn_ref[part]
+            v = v_refs[index][pl.ds(first, size), :] if is_cache else vn_ref[index]
             acc_ref[...] += jnp.dot(w.astype(jnp.bfloat16), v, preferred_element_type=jnp.float32)
 
     o_ref[0] = (acc_ref[...] / l_ref[...]).astype(o_ref.dtype)
 
 
-def attention(grouped, all_kv, new_kv, length, hid_index, token_count, interpret=False):
+def attention(grouped, all_keys, shifted_values, new_kv, length, hid_index, token_count, interpret=False):
     groups, rows, head = grouped.shape
-    parts, cache_rows, _ = all_kv.shape
+    parts, cache_rows, _ = all_keys.shape
     scalars = jnp.stack([length, hid_index]).astype(jnp.int32)
     k_spec = pl.BlockSpec((parts, cache_rows, head), lambda g, s: (0, 0, g))
-    v_spec = pl.BlockSpec((parts, cache_rows, head), lambda g, s: (0, 0, groups + g))
+    v_spec = pl.BlockSpec((cache_rows, head), lambda g, s: (0, g))
     kn_spec = pl.BlockSpec((parts, token_count, head), lambda g, s: (0, 0, g))
     vn_spec = pl.BlockSpec((parts, token_count, head), lambda g, s: (0, 0, groups + g))
     row_spec = pl.BlockSpec((1, rows, head), lambda g, s: (g, 0, 0))
@@ -158,7 +182,7 @@
         grid_spec=pltpu.PrefetchScalarGridSpec(
             num_scalar_prefetch=1,
             grid=(groups,),
-            in_specs=[row_spec, k_spec, v_spec, kn_spec, vn_spec],
+            in_specs=[row_spec, k_spec] + [v_spec] * parts + [kn_spec, vn_spec],
             out_specs=row_spec,
             scratch_shapes=[
                 pltpu.VMEM((rows, 1), jnp.float32),
@@ -168,7 +192,7 @@
             ],
         ),
         interpret=interpret,
-    )(scalars, grouped, all_kv, all_kv, new_kv, new_kv)
+    )(scalars, grouped, all_keys, *shifted_values, new_kv, new_kv)
 
 
 def expert_activation(row_data, gate_weights):
@@ -207,9 +231,11 @@
     new_values = new_kv[:, key_width:]
     length = lengths[0]
     cache_local = cache_keys.shape[1]
-    all_kv = lax.all_gather(
-        jnp.concatenate([cache_keys[0], cache_values[0]], axis=1), "hid", axis=0
-    )
+    all_keys = lax.all_gather(cache_keys[0], "hid", axis=0)
+    shifted_values = [cache_values[0]]
+    for shift in range(1, hid_count):
+        pairs = [(source, (source + shift) % hid_count) for source in range(hid_count)]
+        shifted_values.append(lax.ppermute(cache_values[0], "hid", pairs))
     received = [new_kv]
     for shift in range(1, hid_count):
         pairs = [(source, source + shift) for source in range(hid_count - shift)]
@@ -232,7 +258,7 @@
         .reshape(KVH, group_size * own_count, HD)
     )
     attended = (
-        attention(grouped, all_kv, new_parts, length, hid_index, own_count)
+        attention(grouped, all_keys, shifted_values, new_parts, length, hid_index, own_count)
         .reshape(KVH, group_size, own_count, HD)
         .transpose(2, 0, 1, 3)
         .reshape(own_count, QH * HD)

time: 215 us -> 220 us (1.023)
  Pallas kernels: 15.2 us -> 19.2 us
  starting transfers between devices: 17 us -> 20.1 us
    ppermute x3, waiting for transfers between devices: 0.01 us -> 33.5 us  [body(): received.append(lax.ppermute(new_kv, 'hid', pairs))]
    all_gather x1, waiting for transfers between devices: 32.4 us -> 0.02 us  [body(): all_keys = lax.all_gather(cache_keys[0], 'hid', axis=0)]
    pallas_call x1, Pallas kernels: 15.2 us -> 19.2 us  [attention(): pl.pallas_call(functools.partial(attention_kernel, token_count), out_shap...]
    concatenate x1 -> x0, other arithmetic: 2.43 us -> none  [body(): jnp.concatenate([cache_keys[0], cache_values[0]], axis=1)]
  transfers between devices with their start and end apart: 6 -> 9, of which waited for: 3 -> 2; matrix products, arithmetic and copies ran while one was open for 9% -> 9% of each run, Pallas kernels for 7% -> 9%
where the time goes in v6:
time: 220 us; the launch traced here: 219 us
  waiting for transfers between devices  68.8 us (31%)
  blocking collectives  50.8 us (23%)
  matrix products  27.6 us (13%)
  starting transfers between devices  20.1 us (9%)
  Pallas kernels  19.2 us (9%)
  between operations  15 us (7%)
  local copies, waits for them, and re-layouts  9.04 us (4%)
  other arithmetic  8.73 us (4%)
    all_to_all x1, blocking collectives, body(): lax.all_to_all(send_rows.reshape(expert_count, capacity, model_width), 'r...  50.8 us
    all_to_all x1, waiting for transfers between devices, body(): lax.all_to_all(expert_out.reshape(-1, capacity, model_width), 'req', 0, 0...  34.6 us
    ppermute x3, waiting for transfers between devices, body(): received.append(lax.ppermute(new_kv, 'hid', pairs))  33.5 us
    pallas_call x1, Pallas kernels, attention(): pl.pallas_call(functools.partial(attention_kernel, token_count), out_shap...  19.2 us
    dot_general x1, matrix products, body(): jnp.einsum('hnf,hdf->hnd', activation, all_weights[:, 2], preferred_eleme...  12 us
    ppermute x3, starting transfers between devices, body(): received.append(lax.ppermute(new_kv, 'hid', pairs))  10.6 us
    all_to_all x1, starting transfers between devices, body(): lax.all_to_all(expert_out.reshape(-1, capacity, model_width), 'req', 0, 0...  7.67 us
    dot_general x1, matrix products, body(): jnp.einsum('nd,hdf->hnf', flat_rows, all_weights[:, 1], preferred_element...  6.87 us
  transfers between devices with their start and end apart: 9, of which 2 were waited for; matrix products, arithmetic and copies ran while one was open for 9% of the time, Pallas kernels for 9%

profile of v6, /device:TPU:1, one launch (start us, length us, event | category | flops | bytes accessed | tf_op | source)
XLA Modules:
  0.0 219.3 jit_solution(2548058239083491678)
XLA Ops:
  7.3 0.7 all-gather.4.cloned.1.call-update
  8.0 2.8 %pad_maximum_fusion = bf16[3,1536,192]{1,2,0:T(8,128)(2,1)} fusion(bf16[1,1536,192]{1,2,0:T(8,128)(2,1)} %bitcast.117, bf16[2,1536,192]{1,2,0:T(8,128)(2,1)} %bitcast.116), kind=kLoop, calls=%fused_computation.18 | loop fusion | flops 884736 | bytes 3538944 | tf_op jit(solution)/shard_map/concatenate | solution.py:252
  11.0 0.4 fusion.16
  11.5 5.9 %collective-permute-start.5 = (bf16[128,512]{1,0:T(8,128)(2,1)S(1)}, bf16[128,512]{1,0:T(8,128)(2,1)}, u32[]{:S(2)}, u32[]{:S(2)}) collective-permute-start(bf16[128,512]{1,0:T(8,128)(2,1)S(1)} %fusion.16), channel_id=1, source_target_pairs={{0,3},{4,7},{8,11},{12,15},{16,19},{20,23},{24,27},{28,31},{32,35}... | collective-permute-start | bytes 393224 | tf_op jit(solution)/shard_map/ppermute | solution.py:242
  17.3 1.9 collective-permute-start.4
  19.3 1.7 collective-permute-start.1
  21.0 0.7 fusion.33
  22.0 1.2 reduce-window.6
  23.2 0.2 slice_reduce_fusion
  24.5 0.6 pad_add_fusion.scalars
  25.0 0.2 copy.69
  25.3 0.9 copy.70
  26.2 2.8 %collective-permute-start.3 = (bf16[128,512]{1,0:T(8,128)(2,1)S(1)}, bf16[128,512]{1,0:T(8,128)(2,1)S(1)}, u32[]{:S(2)}, u32[]{:S(2)}) collective-permute-start(bf16[128,512]{1,0:T(8,128)(2,1)S(1)} %fusion.16), channel_id=1, source_target_pairs={{0,1},{1,2},{2,3},{4,5},{5,6},{6,7},{8,9},{9,10},{10,11},{12,13},{... | collective-permute-start | bytes 393224 | tf_op jit(solution)/shard_map/ppermute | solution.py:242
  29.0 0.4 fusion.7
  29.4 33.5 %collective-permute-done.3 = bf16[128,512]{1,0:T(8,128)(2,1)S(1)} collective-permute-done((bf16[128,512]{1,0:T(8,128)(2,1)S(1)}, bf16[128,512]{1,0:T(8,128)(2,1)S(1)}, u32[]{:S(2)}, u32[]{:S(2)}) %collective-permute-start.3) | collective-permute-done | bytes 131104 | tf_op jit(solution)/shard_map/ppermute | solution.py:242
  62.9 1.0 select_bitcast_fusion.3
  63.9 0.9 pad_maximum_fusion.1.kn_ref.vn_ref
  64.9 0.8 copy-done.3
  66.0 19.2 %shard_map.157 = bf16[2,768,128]{2,1,0:T(8,128)(2,1)} custom-call(s32[2]{0:T(128)} %pad_add_fusion.scalars, bf16[2,768,128]{2,1,0:T(8,128)(2,1)} %bitcast.112, bf16[4,1024,256]{2,1,0:T(8,128)(2,1)} %all-gather.4.cloned.1.call-done.k_ref, bf16[1024,256]{1,0:T(8,128)(2,1)} %bitcast.118, bf16[1024,256]{1,0:T(8,128)(2,1)} %copy-done.5, ...), custom_call_target="tpu_custom_call" | custom-call | tf_op jit(solution)/shard_map/pallas_call | solution.py:179
  85.2 1.2 copy.71
  86.4 3.2 %multiply_reduce_fusion = (f32[128]{0:T(128)S(1)}, f32[128,1536]{1,0:T(8,128)S(1)}) fusion(bf16[128,1536]{0,1:T(8,128)(2,1)S(1)} %bitcast.114, bf16[1536,1536]{1,0:T(8,128)(2,1)} %param.23, bf16[1,128,1536]{2,1,0:T(8,128)(2,1)S(1)} %copy-done.1), kind=kOutput, calls=%fused_computation.34 | convolution fusion | flops 605159296 | bytes 6291968 | tf_op jit(solution)/shard_map/dot_general | solution.py:268
  89.7 1.1 convolution_convert_fusion.1
  90.7 50.8 %all_to_all.10 = bf16[32,32,1536]{2,1,0:T(8,128)(2,1)} all-to-all(bf16[32,32,1536]{2,1,0:T(8,128)(2,1)S(1)} %bitcast.108), channel_id=1, replica_groups=mesh['req'=32,'hid'=4] {'req'}, dimensions={0} | all-to-all | bytes 6291456 | tf_op jit(solution)/shard_map/all_to_all | solution.py:286
  141.5 6.9 %fusion.3 = f32[4,192,1024]{2,1,0:T(8,128)} fusion(bf16[1024,1536,1]{1,0,2:T(8,128)(2,1)} %bitcast.110, bf16[4,3,1536,192]{2,3,1,0:T(8,128)(2,1)} %bitcast.122), kind=kOutput, calls=%fused_computation.11 | convolution fusion | flops 2415919104 | bytes 8650752 | tf_op jit(solution)/shard_map/nd,hdf->hnf/dot_general | solution.py:293
  148.4 12.0 %fusion = bf16[1024,1536]{1,0:T(8,128)(2,1)} fusion(bf16[4,3,1536,192]{2,3,1,0:T(8,128)(2,1)} %bitcast.123, f32[4,192,1024]{2,1,0:T(8,128)} %fusion.3, bf16[1024,1536,1]{1,0,2:T(8,128)(2,1)} %bitcast.111), kind=kOutput, calls=%fused_computation.5 | convolution fusion | flops 4845207552 | bytes 14155776 | tf_op jit(solution)/shard_map/hnf,hdf->hnd/dot_general | solution.py:297
  160.4 7.7 %all-to-all-start.1 = ((bf16[32,32,1536]{2,1,0:T(8,128)(2,1)}), bf16[32,32,1536]{2,1,0:T(8,128)(2,1)}, u32[]{:S(2)}, u32[]{:S(2)}) async-start(bf16[32,32,1536]{2,1,0:T(8,128)(2,1)} %bitcast.109), calls=%async_computation.1 | async-start | bytes 6291456 | tf_op jit(solution)/shard_map/all_to_all | solution.py:301
  168.3 0.7 slice_bitcast_fusion.10
  168.9 0.3 fusion.37
  169.2 3.8 %gather_fusion = f32[512]{0:T(512)S(1)} fusion(f32[128,32]{0,1:T(8,128)S(1)} %fusion.37, s32[512]{0:T(512)S(1)} %reshape.190), kind=kCustom, calls=%fused_computation | custom fusion | bytes 8192 | tf_op jit(solution)/shard_map/jit(take_along_axis)/gather | solution.py:309
  173.3 34.6 %all-to-all-done.1 = bf16[32,32,1536]{2,1,0:T(8,128)(2,1)} async-done(((bf16[32,32,1536]{2,1,0:T(8,128)(2,1)}), bf16[32,32,1536]{2,1,0:T(8,128)(2,1)}, u32[]{:S(2)}, u32[]{:S(2)}) %all-to-all-start.1) | async-done | bytes 3145760 | tf_op jit(solution)/shard_map/all_to_all | solution.py:301
  207.9 3.8 %fusion.8 = f32[128,1536]{1,0:T(8,128)S(1)} fusion(bf16[1024,1536,1]{1,0,2:T(8,128)(2,1)} %bitcast.32, f32[128,4]{0,1:T(4,128)S(1)} %multiply_divide_fusion, s32[128,4]{0,1:T(4,128)S(1)} %fusion.34), kind=kOutput, calls=%fused_computation.19 | convolution fusion | flops 1612513280 | bytes 3936256 | tf_op jit(solution)/shard_map/dot_general | solution.py:304
  211.6 0.8 fusion.23
  (56 shorter events, 1.8 us)
Async XLA Ops:
  7.2 161.8 %copy-start = (bf16[1536,32]{0,1:T(8,128)(2,1)S(1)}, bf16[1536,32]{0,1:T(8,128)(2,1)}, u32[]{:S(2)}) copy-start(bf16[1536,32]{0,1:T(8,128)(2,1)} %param.25) | copy-start | bytes 294916
  7.2 3.7 %copy-start.1 = (bf16[1,128,1536]{2,1,0:T(8,128)(2,1)S(1)}, bf16[1,128,1536]{2,1,0:T(8,128)(2,1)}, u32[]{:S(2)}) copy-start(bf16[1,128,1536]{2,1,0:T(8,128)(2,1)} %param.14) | copy-start | bytes 1179652
  7.2 3.8 %copy-start.10 = (bf16[1536,256]{1,0:T(8,128)(2,1)S(1)}, bf16[1536,256]{1,0:T(8,128)(2,1)}, u32[]{:S(2)}) copy-start(bf16[1536,256]{1,0:T(8,128)(2,1)} %param.22) | copy-start | bytes 2359300
  7.2 3.8 %copy-start.11 = (bf16[1536,256]{1,0:T(8,128)(2,1)S(1)}, bf16[1536,256]{1,0:T(8,128)(2,1)}, u32[]{:S(2)}) copy-start(bf16[1536,256]{1,0:T(8,128)(2,1)} %param.21) | copy-start | bytes 2359300
  7.2 3.8 %copy-start.12 = (f32[1536]{0:T(1024)S(1)}, f32[1536]{0:T(1024)}, u32[]{:S(2)}) copy-start(f32[1536]{0:T(1024)} %param.20) | copy-start | bytes 18436
  7.2 57.6 %all-gather.4.cloned.1.call-start = ((), (), s32[]{:S(2)}) async-start(), calls=%async_computation.2 | async-start | bytes 2621440 | tf_op jit(solution)/shard_map/all_gather | solution.py:234
  8.0 133.6 %all-gather.6.cloned.1.call-start = ((), (), s32[]{:S(2)}) async-start(), calls=%async_computation.3 | async-start | bytes 8847360 | tf_op jit(solution)/shard_map/all_gather | solution.py:251
  10.8 8.5 %copy-start.2 = (bf16[1,1024,256]{2,1,0:T(8,128)(2,1)S(1)}, bf16[1,1024,256]{2,1,0:T(8,128)(2,1)}, u32[]{:S(2)}) copy-start(bf16[1,1024,256]{2,1,0:T(8,128)(2,1)} %param.17) | copy-start | bytes 1572868
  10.8 14.2 %copy-start.8 = (bf16[1,128,1536]{2,1,0:T(8,128)(2,1)S(1)}, bf16[1,128,1536]{2,1,0:T(8,128)(2,1)}, u32[]{:S(2)}) copy-start(bf16[1,128,1536]{2,1,0:T(8,128)(2,1)} %param.15) | copy-start | bytes 1179652
  11.5 73.7 %copy-start.6 = (bf16[128,512]{1,0:T(8,128)(2,1)}, bf16[128,512]{1,0:T(8,128)(2,1)S(1)}, u32[]{:S(2)}) copy-start(bf16[128,512]{1,0:T(8,128)(2,1)S(1)} %fusion.16) | copy-start | bytes 393220
  11.5 14.7 %collective-permute-start.5 = (bf16[128,512]{1,0:T(8,128)(2,1)S(1)}, bf16[128,512]{1,0:T(8,128)(2,1)}, u32[]{:S(2)}, u32[]{:S(2)}) collective-permute-start(bf16[128,512]{1,0:T(8,128)(2,1)S(1)} %fusion.16), channel_id=1, source_target_pairs={{0,3},{4,7},{8,11},{12,15},{16,19},{20,23},{24,27},{28,31},{32,35}... | collective-permute-start | bytes 393224 | tf_op jit(solution)/shard_map/ppermute | solution.py:242
  17.3 12.0 %collective-permute-start.4 = (bf16[128,512]{1,0:T(8,128)(2,1)S(1)}, bf16[128,512]{1,0:T(8,128)(2,1)}, u32[]{:S(2)}, u32[]{:S(2)}) collective-permute-start(bf16[128,512]{1,0:T(8,128)(2,1)S(1)} %fusion.16), channel_id=1, source_target_pairs={{0,2},{1,3},{4,6},{5,7},{8,10},{9,11},{12,14},{13,15},{16,18},{17,... | collective-permute-start | bytes 393224 | tf_op jit(solution)/shard_map/ppermute | solution.py:242
  19.3 45.5 %collective-permute-start.2 = (bf16[1024,256]{1,0:T(8,128)(2,1)S(1)}, bf16[1024,256]{1,0:T(8,128)(2,1)S(1)}, u32[]{:S(2)}, u32[]{:S(2)}) collective-permute-start(bf16[1024,256]{1,0:T(8,128)(2,1)S(1)} %bitcast.119), channel_id=1, source_target_pairs={{0,3},{1,0},{2,1},{3,2},{4,7},{5,4},{6,5},{7,6},{8,11},{9,8},{10,9... | collective-permute-start | bytes 1572872 | tf_op jit(solution)/shard_map/ppermute | solution.py:238
  19.3 45.5 %collective-permute-start.1 = (bf16[1024,256]{1,0:T(8,128)(2,1)S(1)}, bf16[1024,256]{1,0:T(8,128)(2,1)S(1)}, u32[]{:S(2)}, u32[]{:S(2)}) collective-permute-start(bf16[1024,256]{1,0:T(8,128)(2,1)S(1)} %bitcast.120), channel_id=1, source_target_pairs={{0,2},{1,3},{2,0},{3,1},{4,6},{5,7},{6,4},{7,5},{8,10},{9,11},{10,... | collective-permute-start | bytes 1572872 | tf_op jit(solution)/shard_map/ppermute | solution.py:238
  21.0 43.8 %collective-permute-start = (bf16[1024,256]{1,0:T(8,128)(2,1)S(1)}, bf16[1024,256]{1,0:T(8,128)(2,1)S(1)}, u32[]{:S(2)}, u32[]{:S(2)}) collective-permute-start(bf16[1024,256]{1,0:T(8,128)(2,1)S(1)} %bitcast.121), channel_id=1, source_target_pairs={{0,1},{1,2},{2,3},{3,0},{4,5},{5,6},{6,7},{7,4},{8,9},{9,10},{10,1... | collective-permute-start | bytes 1572872 | tf_op jit(solution)/shard_map/ppermute | solution.py:238
  26.2 36.7 %collective-permute-start.3 = (bf16[128,512]{1,0:T(8,128)(2,1)S(1)}, bf16[128,512]{1,0:T(8,128)(2,1)S(1)}, u32[]{:S(2)}, u32[]{:S(2)}) collective-permute-start(bf16[128,512]{1,0:T(8,128)(2,1)S(1)} %fusion.16), channel_id=1, source_target_pairs={{0,1},{1,2},{2,3},{4,5},{5,6},{6,7},{8,9},{9,10},{10,11},{12,13},{... | collective-permute-start | bytes 393224 | tf_op jit(solution)/shard_map/ppermute | solution.py:242
  64.8 0.8 copy-start.3
  64.8 1.0 copy-start.4
  64.8 1.1 copy-start.5
  86.4 3.3 %copy-start.9 = (f32[1536]{0:T(1024)S(1)}, f32[1536]{0:T(1024)}, u32[]{:S(2)}) copy-start(f32[1536]{0:T(1024)} %param.24) | copy-start | bytes 18436
  160.4 7.9 %copy-start.7 = (bf16[128,512]{1,0:T(8,128)(2,1)S(1)}, bf16[128,512]{1,0:T(8,128)(2,1)}, u32[]{:S(2)}) copy-start(bf16[128,512]{1,0:T(8,128)(2,1)} %copy-done.6) | copy-start | bytes 393220
  160.4 47.5 %all-to-all-start.1 = ((bf16[32,32,1536]{2,1,0:T(8,128)(2,1)}), bf16[32,32,1536]{2,1,0:T(8,128)(2,1)}, u32[]{:S(2)}, u32[]{:S(2)}) async-start(bf16[32,32,1536]{2,1,0:T(8,128)(2,1)} %bitcast.109), calls=%async_computation.1 | async-start | bytes 6291456 | tf_op jit(solution)/shard_map/all_to_all | solution.py:301
Sparse Core Ops, SparseCore 0:
  9.7 53.3 all-gather.3
  64.7 76.3 all-gather.5

commit v7 on v6

--- a/solution.py
+++ b/solution.py
@@ -83,7 +83,10 @@
     token_count,
     scalars,
     q_ref,
-    k_ref,
+    k0_ref,
+    k1_ref,
+    k2_ref,
+    k3_ref,
     v0_ref,
     v1_ref,
     v2_ref,
@@ -98,9 +101,11 @@
 ):
     length = scalars[0]
     hid_index = scalars[1]
-    parts, cache_rows, _ = k_ref.shape
+    k_refs = (k0_ref, k1_ref, k2_ref, k3_ref)
+    v_refs = (v0_ref, v1_ref, v2_ref, v3_ref)
+    parts = len(k_refs)
+    cache_rows = k0_ref.shape[0]
     rows = q_ref.shape[1]
-    v_refs = (v0_ref, v1_ref, v2_ref, v3_ref)
     q = q_ref[0]
     m_ref[...] = jnp.full(m_ref.shape, MASKED_SCORE, jnp.float32)
     l_ref[...] = jnp.zeros(l_ref.shape, jnp.float32)
@@ -138,7 +143,7 @@
 
     def first_pass(index, first, size, is_cache, masked):
         if is_cache:
-            k = k_ref[part_of(index, True), pl.ds(first, size), :]
+            k = k_refs[index][pl.ds(first, size), :]
         else:
             k = kn_ref[index]
         raw = lax.dot_general(q, k, (((1,), (1,)), ((), ())), preferred_element_type=jnp.float32)
@@ -167,12 +172,13 @@
     o_ref[0] = (acc_ref[...] / l_ref[...]).astype(o_ref.dtype)
 
 
-def attention(grouped, all_keys, shifted_values, new_kv, length, hid_index, token_count, interpret=False):
+def attention(grouped, shifted_kv, new_kv, length, hid_index, token_count, interpret=False):
     groups, rows, head = grouped.shape
-    parts, cache_rows, _ = all_keys.shape
+    parts = len(shifted_kv)
+    cache_rows = shifted_kv[0].shape[0]
     scalars = jnp.stack([length, hid_index]).astype(jnp.int32)
-    k_spec = pl.BlockSpec((parts, cache_rows, head), lambda g, s: (0, 0, g))
-    v_spec = pl.BlockSpec((cache_rows, head), lambda g, s: (0, g))
+    k_spec = pl.BlockSpec((cache_rows, head), lambda g, s: (0, g))
+    v_spec = pl.BlockSpec((cache_rows, head), lambda g, s: (0, groups + g))
     kn_spec = pl.BlockSpec((parts, token_count, head), lambda g, s: (0, 0, g))
     vn_spec = pl.BlockSpec((parts, token_count, head), lambda g, s: (0, 0, groups + g))
     row_spec = pl.BlockSpec((1, rows, head), lambda g, s: (g, 0, 0))
@@ -182,7 +188,7 @@
         grid_spec=pltpu.PrefetchScalarGridSpec(
             num_scalar_prefetch=1,
             grid=(groups,),
-            in_specs=[row_spec, k_spec] + [v_spec] * parts + [kn_spec, vn_spec],
+            in_specs=[row_spec] + [k_spec] * parts + [v_spec] * parts + [kn_spec, vn_spec],
             out_specs=row_spec,
             scratch_shapes=[
                 pltpu.VMEM((rows, 1), jnp.float32),
@@ -192,7 +198,28 @@
             ],
         ),
         interpret=interpret,
-    )(scalars, grouped, all_keys, *shifted_values, new_kv, new_kv)
+    )(scalars, grouped, *shifted_kv, *shifted_kv, new_kv, new_kv)
+
+
+def ring_gather(shard, split_axis, axis_name="hid"):
+    count = lax.axis_size(axis_name)
+    up = [(source, (source + 1) % count) for source in range(count)]
+    down = [(source, (source - 1) % count) for source in range(count)]
+    from_below = lax.ppermute(shard, axis_name, up)
+    from_above = lax.ppermute(shard, axis_name, down)
+    half = shard.shape[split_axis] // 2
+    far = jnp.concatenate(
+        [
+            lax.ppermute(lax.slice_in_dim(from_below, 0, half, axis=split_axis), axis_name, up),
+            lax.ppermute(
+                lax.slice_in_dim(from_above, half, shard.shape[split_axis], axis=split_axis),
+                axis_name,
+                down,
+            ),
+        ],
+        axis=split_axis,
+    )
+    return [shard, from_below, far, from_above]
 
 
 def expert_activation(row_data, gate_weights):
@@ -231,11 +258,7 @@
     new_values = new_kv[:, key_width:]
     length = lengths[0]
     cache_local = cache_keys.shape[1]
-    all_keys = lax.all_gather(cache_keys[0], "hid", axis=0)
-    shifted_values = [cache_values[0]]
-    for shift in range(1, hid_count):
-        pairs = [(source, (source + shift) % hid_count) for source in range(hid_count)]
-        shifted_values.append(lax.ppermute(cache_values[0], "hid", pairs))
+    shifted_kv = ring_gather(jnp.concatenate([cache_keys[0], cache_values[0]], axis=1), 0)
     received = [new_kv]
     for shift in range(1, hid_count):
         pairs = [(source, source + shift) for source in range(hid_count - shift)]
@@ -248,9 +271,10 @@
             chosen = jnp.where(distance == shift, received[shift], chosen)
         new_parts.append(chosen)
     new_parts = jnp.stack(new_parts)
-    all_weights = lax.all_gather(
-        jnp.concatenate([gate_up[0], down_proj[0].T[None]], axis=0), "hid", axis=0
-    )
+    stacked_weights, _ = lax.optimization_barrier(
+        (jnp.concatenate([gate_up[0], down_proj[0].T[None]], axis=0), shifted_kv[2])
+    )
+    shifted_weights = ring_gather(stacked_weights, 1)
     grouped = (
         queries[0]
         .reshape(own_count, KVH, group_size, HD)
@@ -258,7 +282,7 @@
         .reshape(KVH, group_size * own_count, HD)
     )
     attended = (
-        attention(grouped, all_keys, shifted_values, new_parts, length, hid_index, own_count)
+        attention(grouped, shifted_kv, new_parts, length, hid_index, own_count)
         .reshape(KVH, group_size, own_count, HD)
         .transpose(2, 0, 1, 3)
         .reshape(own_count, QH * HD)
@@ -287,17 +311,16 @@
         send_rows.reshape(expert_count, capacity, model_width), "req", 0, 0, tiled=True
     )
     flat_rows = grouped_rows.reshape(-1, model_width)
-    gate_out = jnp.einsum(
-        "nd,hdf->hnf", flat_rows, all_weights[:, 0], preferred_element_type=jnp.float32
-    )
-    up_out = jnp.einsum(
-        "nd,hdf->hnf", flat_rows, all_weights[:, 1], preferred_element_type=jnp.float32
-    )
-    activation = (jnp.maximum(gate_out, 0.0) * up_out).astype(jnp.bfloat16)
-    partials = jnp.einsum(
-        "hnf,hdf->hnd", activation, all_weights[:, 2], preferred_element_type=jnp.float32
-    ).astype(jnp.bfloat16)
-    expert_out = jnp.sum(partials.astype(jnp.float32), axis=0).astype(jnp.bfloat16)
+    expert_sum = None
+    for weights_now in shifted_weights:
+        gate_out = jnp.dot(flat_rows, weights_now[0], preferred_element_type=jnp.float32)
+        up_out = jnp.dot(flat_rows, weights_now[1], preferred_element_type=jnp.float32)
+        activation = (jnp.maximum(gate_out, 0.0) * up_out).astype(jnp.bfloat16)
+        partial = lax.dot_general(
+            activation, weights_now[2], (((1,), (1,)), ((), ())), preferred_element_type=jnp.float32
+        ).astype(jnp.bfloat16)
+        expert_sum = partial.astype(jnp.float32) if expert_sum is None else expert_sum + partial
+    expert_out = expert_sum.astype(jnp.bfloat16)
     returned = lax.all_to_all(
         expert_out.reshape(-1, capacity, model_width), "req", 0, 0, tiled=True
     )

time: 220 us -> 247 us (1.12)
  blocking collectives: 50.8 us -> 0 us
  waiting for transfers between devices: 68.8 us -> 104 us
  starting transfers between devices: 20.1 us -> 42.9 us
  matrix products: 27.6 us -> 48.7 us
  between operations: 15 us -> 1.55 us
  local copies, waits for them, and re-layouts: 9.04 us -> 18.1 us
    ppermute x3 -> x8, waiting for transfers between devices: 0.01 us -> 69.8 us  [the longest x2 46.2 us: ring_gather(): from_below = lax.ppermute(shard, axis_name, up)]
    all_to_all x1 -> x0, blocking collectives: 50.8 us -> none  [body(): lax.all_to_all(send_rows.reshape(expert_count, capacity, model_width), 'r...]
    ppermute x3, waiting for transfers between devices: 33.5 us -> 0.01 us  [body(): received.append(lax.ppermute(new_kv, 'hid', pairs))]
    dot_general x2 -> x8, matrix products: 18.8 us -> 36.8 us  [the longest x4 24.2 us: body(): lax.dot_general(activation, weights_now[2], (((1,), (1,)), ((), ())), pre...]
    ppermute x3 -> x8, starting transfers between devices: 1.73 us -> 15.2 us  [the longest x2 5.73 us: ring_gather(): from_above = lax.ppermute(shard, axis_name, down)]
    all_to_all x0 -> x1, starting transfers between devices: none -> 10 us  [body(): lax.all_to_all(send_rows.reshape(expert_count, capacity, model_width), 'r...]
    unnamed x27, local copies, waits for them, and re-layouts: 1.36 us -> 6.39 us
  transfers between devices with their start and end apart: 9 -> 13, of which waited for: 2 -> 5; matrix products, arithmetic and copies ran while one was open for 9% -> 9% of each run, Pallas kernels for 9% -> 0%
where the time goes in v7:
time: 247 us
  waiting for transfers between devices  104 us (42%)
  matrix products  48.7 us (20%)
  starting transfers between devices  42.9 us (17%)
  Pallas kernels  21.3 us (9%)
  local copies, waits for them, and re-layouts  18.1 us (7%)
  other arithmetic  9.95 us (4%)
    ppermute x2, waiting for transfers between devices, ring_gather(): from_below = lax.ppermute(shard, axis_name, up)  46.2 us
    all_to_all x1, waiting for transfers between devices, body(): lax.all_to_all(expert_out.reshape(-1, capacity, model_width), 'req', 0, 0...  34.6 us
    dot_general x4, matrix products, body(): lax.dot_general(activation, weights_now[2], (((1,), (1,)), ((), ())), pre...  24.2 us
    ppermute x2, waiting for transfers between devices, ring_gather(): lax.ppermute(lax.slice_in_dim(from_below, 0, half, axis=split_axis), axis...  23.6 us
    pallas_call x1, Pallas kernels, attention(): pl.pallas_call(functools.partial(attention_kernel, token_count), out_shap...  21.3 us
    all_to_all x1, starting transfers between devices, body(): lax.all_to_all(send_rows.reshape(expert_count, capacity, model_width), 'r...  10 us
    dot_general x3, matrix products, body(): jnp.dot(flat_rows, weights_now[1], preferred_element_type=jnp.float32)  9.43 us
    ppermute x3, starting transfers between devices, body(): received.append(lax.ppermute(new_kv, 'hid', pairs))  8.98 us
  transfers between devices with their start and end apart: 13, of which 5 were waited for; matrix products, arithmetic and copies ran while one was open for 9% of the time, Pallas kernels for 0%

profile of v7, /device:TPU:1, one launch (start us, length us, event | category | flops | bytes accessed | tf_op | source)
XLA Modules:
  0.0 246.9 jit_solution(8926457856038435548)
XLA Ops:
  0.6 1.3 pad_maximum_fusion.1.k0_ref.v0_ref
  2.0 2.1 collective-permute-start
  4.1 1.3 collective-permute-start.2
  6.6 1.9 fusion.19
  8.5 2.7 %collective-permute-start.4 = (bf16[128,512]{1,0:T(8,128)(2,1)S(1)}, bf16[128,512]{1,0:T(8,128)(2,1)}, u32[]{:S(2)}, u32[]{:S(2)}) collective-permute-start(bf16[128,512]{1,0:T(8,128)(2,1)S(1)} %fusion.19), channel_id=1, source_target_pairs={{0,1},{1,2},{2,3},{4,5},{5,6},{6,7},{8,9},{9,10},{10,11},{12,13},{... | collective-permute-start | bytes 393224 | tf_op jit(solution)/shard_map/ppermute | solution.py:265
  11.2 4.4 %collective-permute-start.5 = (bf16[128,512]{1,0:T(8,128)(2,1)S(1)}, bf16[128,512]{1,0:T(8,128)(2,1)}, u32[]{:S(2)}, u32[]{:S(2)}) collective-permute-start(bf16[128,512]{1,0:T(8,128)(2,1)S(1)} %fusion.19), channel_id=1, source_target_pairs={{0,2},{1,3},{4,6},{5,7},{8,10},{9,11},{12,14},{13,15},{16,18},{17,... | collective-permute-start | bytes 393224 | tf_op jit(solution)/shard_map/ppermute | solution.py:265
  15.6 1.9 collective-permute-start.6
  20.3 7.6 %collective-permute-done.k1_ref.v1_ref = bf16[1024,512]{1,0:T(8,128)(2,1)S(1)} collective-permute-done((bf16[1024,512]{1,0:T(8,128)(2,1)S(1)}, bf16[1024,512]{1,0:T(8,128)(2,1)S(1)}, u32[]{:S(2)}, u32[]{:S(2)}) %collective-permute-start) | collective-permute-done | bytes 1048608 | tf_op jit(solution)/shard_map/ppermute | solution.py:208
  30.9 2.4 collective-permute-start.3
  38.1 4.8 %collective-permute-done.1 = bf16[512,512]{1,0:T(8,128)(2,1)} collective-permute-done((bf16[512,512]{1,0:T(8,128)(2,1)}, bf16[512,512]{1,0:T(8,128)(2,1)}, u32[]{:S(2)}, u32[]{:S(2)}) %collective-permute-start.1) | collective-permute-done | bytes 524320 | tf_op jit(solution)/shard_map/ppermute | solution.py:213
  46.0 21.3 %shard_map.157 = bf16[2,768,128]{2,1,0:T(8,128)(2,1)} custom-call(s32[2]{0:T(128)} %pad_add_fusion.scalars, bf16[2,768,128]{2,1,0:T(8,128)(2,1)} %bitcast.143, bf16[1024,512]{1,0:T(8,128)(2,1)} %copy-done.3, bf16[1024,512]{1,0:T(8,128)(2,1)} %copy-done.4, bf16[1024,512]{1,0:T(8,128)(2,1)} %copy-done.6, bf16[1024,512]{1,0:T(8,128)(2,1)} %copy-done.5, ...), custom_call_target="tpu_custom_call" | custom-call | tf_op jit(solution)/shard_map/pallas_call | solution.py:185
  68.6 3.2 %multiply_reduce_fusion = (f32[128]{0:T(128)S(1)}, f32[128,1536]{1,0:T(8,128)S(1)}) fusion(bf16[128,1536]{0,1:T(8,128)(2,1)S(1)} %bitcast.145, bf16[1536,1536]{1,0:T(8,128)(2,1)} %param.23, bf16[1,128,1536]{2,1,0:T(8,128)(2,1)S(1)} %copy-done.9), kind=kOutput, calls=%fused_computation.43 | convolution fusion | flops 605159296 | bytes 6291968 | tf_op jit(solution)/shard_map/dot_general | solution.py:292
  72.8 2.7 %convolution_convert_fusion.4 = bf16[1024,1536]{1,0:T(8,128)(2,1)} fusion(pred[1024,128]{1,0:T(8,128)(4,1)S(1)} %fusion.4, f32[128,1536]{1,0:T(8,128)S(1)} %get-tuple-element.14, f32[1536]{0:T(1024)S(1)} %copy-done.11, f32[128]{0:T(128)S(1)} %add_rsqrt_fusion), kind=kOutput, calls=%fused_computation.6 | convolution fusion | flops 404815872 | bytes 4069888 | tf_op jit(solution)/shard_map/dot_general | solution.py:309
  75.5 10.0 %all-to-all-start = ((bf16[32,32,1536]{2,1,0:T(8,128)(2,1)}), bf16[32,32,1536]{2,1,0:T(8,128)(2,1)S(1)}, u32[]{:S(2)}, u32[]{:S(2)}) async-start(bf16[32,32,1536]{2,1,0:T(8,128)(2,1)} %bitcast.141), calls=%async_computation | async-start | bytes 6291456 | tf_op jit(solution)/shard_map/all_to_all | solution.py:310
  85.5 1.6 pad_maximum_fusion
  87.1 3.0 %collective-permute-start.7 = (bf16[3,1536,192]{1,2,0:T(8,128)(2,1)S(1)}, bf16[3,1536,192]{1,2,0:T(8,128)(2,1)S(1)}, u32[]{:S(2)}, u32[]{:S(2)}) collective-permute-start(bf16[3,1536,192]{1,2,0:T(8,128)(2,1)S(1)} %pad_maximum_fusion), channel_id=1, source_target_pairs={{0,1},{1,2},{2,3},{3,0},{4,5},{5,6},{6,7},{7,4},{8,9},{9,10},{10,1... | collective-permute-start | bytes 5308424 | tf_op jit(solution)/shard_map/ppermute | solution.py:208
  90.1 4.4 %collective-permute-start.9 = (bf16[3,1536,192]{1,2,0:T(8,128)(2,1)S(1)}, bf16[3,1536,192]{1,2,0:T(8,128)(2,1)S(1)}, u32[]{:S(2)}, u32[]{:S(2)}) collective-permute-start(bf16[3,1536,192]{1,2,0:T(8,128)(2,1)S(1)} %pad_maximum_fusion), channel_id=1, source_target_pairs={{0,3},{1,0},{2,1},{3,2},{4,7},{5,4},{6,5},{7,6},{8,11},{9,8},{10,9... | collective-permute-start | bytes 5308424 | tf_op jit(solution)/shard_map/ppermute | solution.py:209
  94.5 38.7 %collective-permute-done.7 = bf16[3,1536,192]{1,2,0:T(8,128)(2,1)S(1)} collective-permute-done((bf16[3,1536,192]{1,2,0:T(8,128)(2,1)S(1)}, bf16[3,1536,192]{1,2,0:T(8,128)(2,1)S(1)}, u32[]{:S(2)}, u32[]{:S(2)}) %collective-permute-start.7) | collective-permute-done | bytes 1769504 | tf_op jit(solution)/shard_map/ppermute | solution.py:208
  134.4 1.6 collective-permute-start.10
  136.1 18.8 %collective-permute-done.8 = bf16[3,768,192]{1,2,0:T(8,128)(2,1)S(1)} collective-permute-done((bf16[3,768,192]{1,2,0:T(8,128)(2,1)S(1)}, bf16[3,768,192]{1,2,0:T(8,128)(2,1)S(1)}, u32[]{:S(2)}, u32[]{:S(2)}) %collective-permute-start.8) | collective-permute-done | bytes 884768 | tf_op jit(solution)/shard_map/ppermute | solution.py:213
  157.0 3.1 %convolution_maximum_fusion.3 = f32[1024,192]{0,1:T(8,128)} fusion(bf16[1024,1536]{1,0:T(8,128)(2,1)S(1)} %bitcast.133, bf16[3,1536,192]{1,2,0:T(8,128)(2,1)} %copy-done.7), kind=kOutput, calls=%fused_computation.25 | convolution fusion | flops 604176384 | bytes 4521984 | tf_op jit(solution)/shard_map/dot_general | solution.py:316
  160.1 5.2 %convolution_convert_fusion.3 = bf16[1024,1536]{1,0:T(8,128)(2,1)} fusion(f32[1024,192]{0,1:T(8,128)} %convolution_maximum_fusion.3, bf16[1024,1536]{1,0:T(8,128)(2,1)S(1)} %bitcast.134, bf16[3,1536,192]{1,2,0:T(8,128)(2,1)} %copy-done.7), kind=kOutput, calls=%fused_computation.5 | convolution fusion | flops 1209925632 | bytes 8257536 | tf_op jit(solution)/shard_map/dot_general | solution.py:319
  165.3 3.2 %fusion.27 = f32[1024,192]{0,1:T(8,128)} fusion(bf16[1024,1536]{1,0:T(8,128)(2,1)S(1)} %bitcast.135, bf16[3,1536,192]{1,2,0:T(8,128)(2,1)} %constant_dynamic-update-slice_fusion.2), kind=kOutput, calls=%fused_computation.50 | convolution fusion | flops 603979776 | bytes 4521984 | tf_op jit(solution)/shard_map/dot_general | solution.py:317
  168.5 5.2 %convolution_convert_fusion.1 = bf16[1024,1536]{1,0:T(8,128)(2,1)} fusion(f32[1024,192]{0,1:T(8,128)} %fusion.27, bf16[1024,1536]{1,0:T(8,128)(2,1)S(1)} %bitcast.136, bf16[3,1536,192]{1,2,0:T(8,128)(2,1)} %constant_dynamic-update-slice_fusion.2), kind=kOutput, calls=%fused_computation.3 | convolution fusion | flops 1210122240 | bytes 8257536 | tf_op jit(solution)/shard_map/dot_general | solution.py:319
  173.7 3.1 %fusion.28 = f32[1024,192]{0,1:T(8,128)} fusion(bf16[1024,1536]{1,0:T(8,128)(2,1)S(1)} %bitcast.137, bf16[3,1536,192]{1,2,0:T(8,128)(2,1)} %copy-done.10), kind=kOutput, calls=%fused_computation.54 | convolution fusion | flops 603979776 | bytes 4521984 | tf_op jit(solution)/shard_map/dot_general | solution.py:317
  176.8 3.1 %fusion.26 = f32[1024,192]{0,1:T(8,128)} fusion(bf16[1024,1536]{1,0:T(8,128)(2,1)S(1)} %bitcast.138, bf16[3,1536,192]{1,2,0:T(8,128)(2,1)} %copy-done.8), kind=kOutput, calls=%fused_computation.46 | convolution fusion | flops 603979776 | bytes 4521984 | tf_op jit(solution)/shard_map/dot_general | solution.py:317
  179.9 5.2 %convolution_convert_fusion.2 = bf16[1024,1536]{1,0:T(8,128)(2,1)} fusion(f32[1024,192]{0,1:T(8,128)} %fusion.28, bf16[1024,1536]{1,0:T(8,128)(2,1)S(1)} %bitcast.139, bf16[3,1536,192]{1,2,0:T(8,128)(2,1)} %copy-done.10), kind=kOutput, calls=%fused_computation.4 | convolution fusion | flops 1210122240 | bytes 8257536 | tf_op jit(solution)/shard_map/dot_general | solution.py:319
  185.1 8.6 %add_convert_fusion = bf16[1024,1536]{1,0:T(8,128)(2,1)} fusion(bf16[1024,1536]{1,0:T(8,128)(2,1)} %convolution_convert_fusion.1, bf16[1024,1536]{1,0:T(8,128)(2,1)} %convolution_convert_fusion.2, bf16[1024,1536]{1,0:T(8,128)(2,1)} %convolution_convert_fusion.3, f32[1024,192]{0,1:T(8,128)} %fusion.26, bf16[1024,1536]{1,0:T(8,128)(2,1)S(1)} %bitcast.140, ...), kind=kOutput, calls=%fused_computation.1 | convolution fusion | flops 1222705152 | bytes 17694720 | tf_op jit(solution)/shard_map/dot_general | solution.py:319
  193.7 8.7 %all-to-all-start.1 = ((bf16[32,32,1536]{2,1,0:T(8,128)(2,1)}), bf16[32,32,1536]{2,1,0:T(8,128)(2,1)}, u32[]{:S(2)}, u32[]{:S(2)}) async-start(bf16[32,32,1536]{2,1,0:T(8,128)(2,1)} %bitcast.142), calls=%async_computation.1 | async-start | bytes 6291456 | tf_op jit(solution)/shard_map/all_to_all | solution.py:324
  203.6 3.8 %gather_fusion = f32[512]{0:T(512)S(1)} fusion(f32[128,32]{0,1:T(8,128)S(1)} %fusion.56, s32[512]{0:T(512)S(1)} %reshape.190), kind=kCustom, calls=%fused_computation | custom fusion | bytes 8192 | tf_op jit(solution)/shard_map/jit(take_along_axis)/gather | solution.py:332
  207.6 34.6 %all-to-all-done.1 = bf16[32,32,1536]{2,1,0:T(8,128)(2,1)} async-done(((bf16[32,32,1536]{2,1,0:T(8,128)(2,1)}), bf16[32,32,1536]{2,1,0:T(8,128)(2,1)}, u32[]{:S(2)}, u32[]{:S(2)}) %all-to-all-start.1) | async-done | bytes 3145760 | tf_op jit(solution)/shard_map/all_to_all | solution.py:324
  242.2 3.8 %fusion.5 = f32[128,1536]{1,0:T(8,128)S(1)} fusion(bf16[1024,1536,1]{1,0,2:T(8,128)(2,1)} %bitcast.39, f32[128,4]{0,1:T(4,128)S(1)} %multiply_divide_fusion, s32[128,4]{0,1:T(4,128)S(1)} %fusion.51), kind=kOutput, calls=%fused_computation.16 | convolution fusion | flops 1612513280 | bytes 3936256 | tf_op jit(solution)/shard_map/dot_general | solution.py:327
  (74 shorter events, 22.0 us)
Async XLA Ops:
  0.6 202.7 %copy-start = (bf16[1536,32]{0,1:T(8,128)(2,1)S(1)}, bf16[1536,32]{0,1:T(8,128)(2,1)}, u32[]{:S(2)}) copy-start(bf16[1536,32]{0,1:T(8,128)(2,1)} %param.25) | copy-start | bytes 294916
  2.0 29.0 %copy-start.3 = (bf16[1024,512]{1,0:T(8,128)(2,1)}, bf16[1024,512]{1,0:T(8,128)(2,1)S(1)}, u32[]{:S(2)}) copy-start(bf16[1024,512]{1,0:T(8,128)(2,1)S(1)} %pad_maximum_fusion.1.k0_ref.v0_ref) | copy-start | bytes 3145732
  2.0 25.9 %collective-permute-start = (bf16[1024,512]{1,0:T(8,128)(2,1)S(1)}, bf16[1024,512]{1,0:T(8,128)(2,1)S(1)}, u32[]{:S(2)}, u32[]{:S(2)}) collective-permute-start(bf16[1024,512]{1,0:T(8,128)(2,1)S(1)} %pad_maximum_fusion.1.k0_ref.v0_ref), channel_id=1, source_target_pairs={{0,1},{1,2},{2,3},{3,0},{4,5},{5,6},{6,7},{7,4},{8,9},{9,10},{10,1... | collective-permute-start | bytes 3145736 | tf_op jit(solution)/shard_map/ppermute | solution.py:208
  4.1 25.9 %collective-permute-start.2 = (bf16[1024,512]{1,0:T(8,128)(2,1)S(1)}, bf16[1024,512]{1,0:T(8,128)(2,1)S(1)}, u32[]{:S(2)}, u32[]{:S(2)}) collective-permute-start(bf16[1024,512]{1,0:T(8,128)(2,1)S(1)} %pad_maximum_fusion.1.k0_ref.v0_ref), channel_id=1, source_target_pairs={{0,3},{1,0},{2,1},{3,2},{4,7},{5,4},{6,5},{7,6},{8,11},{9,8},{10,9... | collective-permute-start | bytes 3145736 | tf_op jit(solution)/shard_map/ppermute | solution.py:209
  8.5 27.5 %collective-permute-start.4 = (bf16[128,512]{1,0:T(8,128)(2,1)S(1)}, bf16[128,512]{1,0:T(8,128)(2,1)}, u32[]{:S(2)}, u32[]{:S(2)}) collective-permute-start(bf16[128,512]{1,0:T(8,128)(2,1)S(1)} %fusion.19), channel_id=1, source_target_pairs={{0,1},{1,2},{2,3},{4,5},{5,6},{6,7},{8,9},{9,10},{10,11},{12,13},{... | collective-permute-start | bytes 393224 | tf_op jit(solution)/shard_map/ppermute | solution.py:265
  11.2 24.9 %collective-permute-start.5 = (bf16[128,512]{1,0:T(8,128)(2,1)S(1)}, bf16[128,512]{1,0:T(8,128)(2,1)}, u32[]{:S(2)}, u32[]{:S(2)}) collective-permute-start(bf16[128,512]{1,0:T(8,128)(2,1)S(1)} %fusion.19), channel_id=1, source_target_pairs={{0,2},{1,3},{4,6},{5,7},{8,10},{9,11},{12,14},{13,15},{16,18},{17,... | collective-permute-start | bytes 393224 | tf_op jit(solution)/shard_map/ppermute | solution.py:265
  15.6 20.5 %collective-permute-start.6 = (bf16[128,512]{1,0:T(8,128)(2,1)S(1)}, bf16[128,512]{1,0:T(8,128)(2,1)}, u32[]{:S(2)}, u32[]{:S(2)}) collective-permute-start(bf16[128,512]{1,0:T(8,128)(2,1)S(1)} %fusion.19), channel_id=1, source_target_pairs={{0,3},{4,7},{8,11},{12,15},{16,19},{20,23},{24,27},{28,31},{32,35}... | collective-permute-start | bytes 393224 | tf_op jit(solution)/shard_map/ppermute | solution.py:265
  27.8 16.1 %copy-start.4 = (bf16[1024,512]{1,0:T(8,128)(2,1)}, bf16[1024,512]{1,0:T(8,128)(2,1)S(1)}, u32[]{:S(2)}) copy-start(bf16[1024,512]{1,0:T(8,128)(2,1)S(1)} %collective-permute-done.k1_ref.v1_ref) | copy-start | bytes 3145732
  28.7 14.2 %collective-permute-start.1 = (bf16[512,512]{1,0:T(8,128)(2,1)}, bf16[512,512]{1,0:T(8,128)(2,1)}, u32[]{:S(2)}, u32[]{:S(2)}) collective-permute-start(bf16[512,512]{1,0:T(8,128)(2,1)} %slice.82), channel_id=1, source_target_pairs={{0,1},{1,2},{2,3},{3,0},{4,5},{5,6},{6,7},{7,4},{8,9},{9,10},{10,1... | collective-permute-start | bytes 1572872 | tf_op jit(solution)/shard_map/ppermute | solution.py:213
  30.0 15.0 %copy-start.5 = (bf16[1024,512]{1,0:T(8,128)(2,1)}, bf16[1024,512]{1,0:T(8,128)(2,1)S(1)}, u32[]{:S(2)}) copy-start(bf16[1024,512]{1,0:T(8,128)(2,1)S(1)} %collective-permute-done.2.k3_ref.v3_ref) | copy-start | bytes 3145732
  30.9 13.0 %collective-permute-start.3 = (bf16[512,512]{1,0:T(8,128)(2,1)}, bf16[512,512]{1,0:T(8,128)(2,1)}, u32[]{:S(2)}, u32[]{:S(2)}) collective-permute-start(bf16[512,512]{1,0:T(8,128)(2,1)} %slice.83), channel_id=1, source_target_pairs={{0,3},{1,0},{2,1},{3,2},{4,7},{5,4},{6,5},{7,6},{8,11},{9,8},{10,9... | collective-permute-start | bytes 1572872 | tf_op jit(solution)/shard_map/ppermute | solution.py:214
  45.1 1.0 copy-start.6
  46.0 22.5 %copy-start.9 = (bf16[1,128,1536]{2,1,0:T(8,128)(2,1)S(1)}, bf16[1,128,1536]{2,1,0:T(8,128)(2,1)}, u32[]{:S(2)}) copy-start(bf16[1,128,1536]{2,1,0:T(8,128)(2,1)} %param.14) | copy-start | bytes 1179652
  68.6 4.2 %copy-start.11 = (f32[1536]{0:T(1024)S(1)}, f32[1536]{0:T(1024)}, u32[]{:S(2)}) copy-start(f32[1536]{0:T(1024)} %param.24) | copy-start | bytes 18436
  71.8 1.0 copy-start.1
  75.5 81.5 %all-to-all-start = ((bf16[32,32,1536]{2,1,0:T(8,128)(2,1)}), bf16[32,32,1536]{2,1,0:T(8,128)(2,1)S(1)}, u32[]{:S(2)}, u32[]{:S(2)}) async-start(bf16[32,32,1536]{2,1,0:T(8,128)(2,1)} %bitcast.141), calls=%async_computation | async-start | bytes 6291456 | tf_op jit(solution)/shard_map/all_to_all | solution.py:310
  87.1 68.8 %copy-start.7 = (bf16[3,1536,192]{1,2,0:T(8,128)(2,1)}, bf16[3,1536,192]{1,2,0:T(8,128)(2,1)S(1)}, u32[]{:S(2)}) copy-start(bf16[3,1536,192]{1,2,0:T(8,128)(2,1)S(1)} %pad_maximum_fusion) | copy-start | bytes 5308420
  87.1 46.0 %collective-permute-start.7 = (bf16[3,1536,192]{1,2,0:T(8,128)(2,1)S(1)}, bf16[3,1536,192]{1,2,0:T(8,128)(2,1)S(1)}, u32[]{:S(2)}, u32[]{:S(2)}) collective-permute-start(bf16[3,1536,192]{1,2,0:T(8,128)(2,1)S(1)} %pad_maximum_fusion), channel_id=1, source_target_pairs={{0,1},{1,2},{2,3},{3,0},{4,5},{5,6},{6,7},{7,4},{8,9},{9,10},{10,1... | collective-permute-start | bytes 5308424 | tf_op jit(solution)/shard_map/ppermute | solution.py:208
  90.1 44.3 %collective-permute-start.9 = (bf16[3,1536,192]{1,2,0:T(8,128)(2,1)S(1)}, bf16[3,1536,192]{1,2,0:T(8,128)(2,1)S(1)}, u32[]{:S(2)}, u32[]{:S(2)}) collective-permute-start(bf16[3,1536,192]{1,2,0:T(8,128)(2,1)S(1)} %pad_maximum_fusion), channel_id=1, source_target_pairs={{0,3},{1,0},{2,1},{3,2},{4,7},{5,4},{6,5},{7,6},{8,11},{9,8},{10,9... | collective-permute-start | bytes 5308424 | tf_op jit(solution)/shard_map/ppermute | solution.py:209
  133.1 1.3 copy-start.10
  133.2 21.7 %collective-permute-start.8 = (bf16[3,768,192]{1,2,0:T(8,128)(2,1)S(1)}, bf16[3,768,192]{1,2,0:T(8,128)(2,1)S(1)}, u32[]{:S(2)}, u32[]{:S(2)}) collective-permute-start(bf16[3,768,192]{1,2,0:T(8,128)(2,1)S(1)} %slice.88), channel_id=1, source_target_pairs={{0,1},{1,2},{2,3},{3,0},{4,5},{5,6},{6,7},{7,4},{8,9},{9,10},{10,1... | collective-permute-start | bytes 2654216 | tf_op jit(solution)/shard_map/ppermute | solution.py:213
  134.4 21.5 %copy-start.8 = (bf16[3,1536,192]{1,2,0:T(8,128)(2,1)}, bf16[3,1536,192]{1,2,0:T(8,128)(2,1)S(1)}, u32[]{:S(2)}) copy-start(bf16[3,1536,192]{1,2,0:T(8,128)(2,1)S(1)} %collective-permute-done.9) | copy-start | bytes 5308420
  134.4 21.5 %collective-permute-start.10 = (bf16[3,768,192]{1,2,0:T(8,128)(2,1)S(1)}, bf16[3,768,192]{1,2,0:T(8,128)(2,1)S(1)}, u32[]{:S(2)}, u32[]{:S(2)}) collective-permute-start(bf16[3,768,192]{1,2,0:T(8,128)(2,1)S(1)} %slice.89), channel_id=1, source_target_pairs={{0,3},{1,0},{2,1},{3,2},{4,7},{5,4},{6,5},{7,6},{8,11},{9,8},{10,9... | collective-permute-start | bytes 2654216 | tf_op jit(solution)/shard_map/ppermute | solution.py:214
  193.7 9.6 %copy-start.2 = (f32[128,1536]{1,0:T(8,128)S(1)}, f32[128,1536]{1,0:T(8,128)}, u32[]{:S(2)}) copy-start(f32[128,1536]{1,0:T(8,128)} %copy-done.1) | copy-start | bytes 2359300
  193.7 48.5 %all-to-all-start.1 = ((bf16[32,32,1536]{2,1,0:T(8,128)(2,1)}), bf16[32,32,1536]{2,1,0:T(8,128)(2,1)}, u32[]{:S(2)}, u32[]{:S(2)}) async-start(bf16[32,32,1536]{2,1,0:T(8,128)(2,1)} %bitcast.142), calls=%async_computation.1 | async-start | bytes 6291456 | tf_op jit(solution)/shard_map/all_to_all | solution.py:324

commit v8 on v7

--- a/solution.py
+++ b/solution.py
@@ -201,25 +201,31 @@
     )(scalars, grouped, *shifted_kv, *shifted_kv, new_kv, new_kv)
 
 
-def ring_gather(shard, split_axis, axis_name="hid"):
+def ring_neighbours(shard, axis_name="hid"):
     count = lax.axis_size(axis_name)
     up = [(source, (source + 1) % count) for source in range(count)]
     down = [(source, (source - 1) % count) for source in range(count)]
-    from_below = lax.ppermute(shard, axis_name, up)
-    from_above = lax.ppermute(shard, axis_name, down)
-    half = shard.shape[split_axis] // 2
-    far = jnp.concatenate(
+    return lax.ppermute(shard, axis_name, up), lax.ppermute(shard, axis_name, down)
+
+
+def ring_far(from_below, from_above, split_axis, axis_name="hid"):
+    count = lax.axis_size(axis_name)
+    up = [(source, (source + 1) % count) for source in range(count)]
+    down = [(source, (source - 1) % count) for source in range(count)]
+    extent = from_below.shape[split_axis]
+    half = extent // 2
+    return jnp.concatenate(
         [
             lax.ppermute(lax.slice_in_dim(from_below, 0, half, axis=split_axis), axis_name, up),
-            lax.ppermute(
-                lax.slice_in_dim(from_above, half, shard.shape[split_axis], axis=split_axis),
-                axis_name,
-                down,
-            ),
+            lax.ppermute(lax.slice_in_dim(from_above, half, extent, axis=split_axis), axis_name, down),
         ],
         axis=split_axis,
     )
-    return [shard, from_below, far, from_above]
+
+
+def ring_gather(shard, split_axis, axis_name="hid"):
+    from_below, from_above = ring_neighbours(shard, axis_name)
+    return [shard, from_below, ring_far(from_below, from_above, split_axis, axis_name), from_above]
 
 
 def expert_activation(row_data, gate_weights):
@@ -274,7 +280,7 @@
     stacked_weights, _ = lax.optimization_barrier(
         (jnp.concatenate([gate_up[0], down_proj[0].T[None]], axis=0), shifted_kv[2])
     )
-    shifted_weights = ring_gather(stacked_weights, 1)
+    weights_below, weights_above = ring_neighbours(stacked_weights)
     grouped = (
         queries[0]
         .reshape(own_count, KVH, group_size, HD)
@@ -292,6 +298,15 @@
         + jnp.dot(attended, out_proj, preferred_element_type=jnp.float32)
     ).astype(jnp.bfloat16)
     moe_in = normalize(mid_stream, moe_gain).astype(jnp.bfloat16)
+    moe_in, weights_below, weights_above = lax.optimization_barrier(
+        (moe_in, weights_below, weights_above)
+    )
+    shifted_weights = [
+        stacked_weights,
+        weights_below,
+        ring_far(weights_below, weights_above, 1),
+        weights_above,
+    ]
     logits = jnp.dot(moe_in, router, preferred_element_type=jnp.float32)
     expert_count = router.shape[1]
     top_count = routes.shape[2]

time: 247 us -> 228 us (0.923)
  waiting for transfers between devices: 104 us -> 91.4 us
  Pallas kernels: 21.3 us -> 15.4 us
  starting transfers between devices: 42.9 us -> 38.4 us
    ppermute x8, waiting for transfers between devices: 69.8 us -> 43.3 us  [the longest x2 23.7 us: ring_far(): lax.ppermute(lax.slice_in_dim(from_below, 0, half, axis=split_axis), axis...]
    all_to_all x1, waiting for transfers between devices: 0.01 us -> 14.2 us  [body(): lax.all_to_all(send_rows.reshape(expert_count, capacity, model_width), 'r...]
    dot_general x1 -> x3, matrix products: 3.14 us -> 9.45 us  [body(): jnp.dot(flat_rows, weights_now[0], preferred_element_type=jnp.float32)]
    dot_general x3 -> x1, matrix products: 9.43 us -> 3.12 us  [body(): jnp.dot(flat_rows, weights_now[1], preferred_element_type=jnp.float32)]
    pallas_call x1, Pallas kernels: 21.3 us -> 15.4 us  [attention(): pl.pallas_call(functools.partial(attention_kernel, token_count), out_shap...]
    ppermute x8, starting transfers between devices: 15.2 us -> 11.3 us  [the longest x2 5.13 us: ring_far(): lax.ppermute(lax.slice_in_dim(from_above, half, extent, axis=split_axis),...]
    all_to_all x1, starting transfers between devices: 10 us -> 13.5 us  [body(): lax.all_to_all(send_rows.reshape(expert_count, capacity, model_width), 'r...]
    all_to_all x1, starting transfers between devices: 8.7 us -> 5.2 us  [body(): lax.all_to_all(expert_out.reshape(-1, capacity, model_width), 'req', 0, 0...]
  transfers between devices with their start and end apart: 13 -> 13, of which waited for: 5 -> 6; matrix products, arithmetic and copies ran while one was open for 9% -> 15% of each run, Pallas kernels for 0% -> 7%
where the time goes in v8:
time: 228 us; the launch traced here: 226 us
  waiting for transfers between devices  91.4 us (40%)
  matrix products  49.2 us (22%)
  starting transfers between devices  38.4 us (17%)
  local copies, waits for them, and re-layouts  19.2 us (8%)
  Pallas kernels  15.4 us (7%)
  other arithmetic  11.3 us (5%)
    all_to_all x1, waiting for transfers between devices, body(): lax.all_to_all(expert_out.reshape(-1, capacity, model_width), 'req', 0, 0...  33.9 us
    dot_general x4, matrix products, body(): lax.dot_general(activation, weights_now[2], (((1,), (1,)), ((), ())), pre...  24.1 us
    ppermute x2, waiting for transfers between devices, ring_far(): lax.ppermute(lax.slice_in_dim(from_below, 0, half, axis=split_axis), axis...  23.7 us
    pallas_call x1, Pallas kernels, attention(): pl.pallas_call(functools.partial(attention_kernel, token_count), out_shap...  15.4 us
    all_to_all x1, waiting for transfers between devices, body(): lax.all_to_all(send_rows.reshape(expert_count, capacity, model_width), 'r...  14.2 us
    all_to_all x1, starting transfers between devices, body(): lax.all_to_all(send_rows.reshape(expert_count, capacity, model_width), 'r...  13.5 us
    ppermute x2, waiting for transfers between devices, ring_neighbours(): lax.ppermute(shard, axis_name, down)  10.1 us
    dot_general x3, matrix products, body(): jnp.dot(flat_rows, weights_now[0], preferred_element_type=jnp.float32)  9.45 us
  transfers between devices with their start and end apart: 13, of which 6 were waited for; matrix products, arithmetic and copies ran while one was open for 15% of the time, Pallas kernels for 7%

profile of v8, /device:TPU:1, one launch (start us, length us, event | category | flops | bytes accessed | tf_op | source)
XLA Modules:
  0.0 226.4 jit_solution(6390913743508450960)
XLA Ops:
  2.0 2.1 collective-permute-start
  4.1 1.3 collective-permute-start.2
  6.6 2.6 %fusion.17 = bf16[128,512]{1,0:T(8,128)(2,1)} fusion(bf16[1536,256]{1,0:T(8,128)(2,1)} %param.22, bf16[1536,256]{1,0:T(8,128)(2,1)} %param.21, bf16[1,128,1536]{2,1,0:T(8,128)(2,1)} %param.14, f32[1536]{0:T(1024)} %param.20, f32[128]{0:T(128)S(1)} %add_rsqrt_fusion.1), kind=kOutput, calls=%fused_computation.35 | convolution fusion | flops 205324288 | bytes 2103808 | tf_op jit(solution)/shard_map/dot_general | solution.py:260
  9.2 3.9 %collective-permute-start.6 = (bf16[128,512]{1,0:T(8,128)(2,1)}, bf16[128,512]{1,0:T(8,128)(2,1)}, u32[]{:S(2)}, u32[]{:S(2)}) collective-permute-start(bf16[128,512]{1,0:T(8,128)(2,1)} %fusion.17), channel_id=1, source_target_pairs={{0,3},{4,7},{8,11},{12,15},{16,19},{20,23},{24,27},{28,31},{32,35}... | collective-permute-start | bytes 393224 | tf_op jit(solution)/shard_map/ppermute | solution.py:271
  13.1 1.9 collective-permute-start.5
  15.0 2.5 %collective-permute-start.4 = (bf16[128,512]{1,0:T(8,128)(2,1)}, bf16[128,512]{1,0:T(8,128)(2,1)}, u32[]{:S(2)}, u32[]{:S(2)}) collective-permute-start(bf16[128,512]{1,0:T(8,128)(2,1)} %fusion.17), channel_id=1, source_target_pairs={{0,1},{1,2},{2,3},{4,5},{5,6},{6,7},{8,9},{9,10},{10,11},{12,13},{... | collective-permute-start | bytes 393224 | tf_op jit(solution)/shard_map/ppermute | solution.py:271
  18.4 9.4 %collective-permute-done.k1_ref.v1_ref = bf16[1024,512]{1,0:T(8,128)(2,1)S(1)} collective-permute-done((bf16[1024,512]{1,0:T(8,128)(2,1)S(1)}, bf16[1024,512]{1,0:T(8,128)(2,1)S(1)}, u32[]{:S(2)}, u32[]{:S(2)}) %collective-permute-start) | collective-permute-done | bytes 1048608 | tf_op jit(solution)/shard_map/ppermute | solution.py:208
  31.5 2.4 %collective-permute-start.3 = (bf16[512,512]{1,0:T(8,128)(2,1)}, bf16[512,512]{1,0:T(8,128)(2,1)}, u32[]{:S(2)}, u32[]{:S(2)}) collective-permute-start(bf16[512,512]{1,0:T(8,128)(2,1)} %slice.83), channel_id=1, source_target_pairs={{0,3},{1,0},{2,1},{3,2},{4,7},{5,4},{6,5},{7,6},{8,11},{9,8},{10,9... | collective-permute-start | bytes 1572872 | tf_op jit(solution)/shard_map/ppermute | solution.py:220
  34.1 2.8 %pad_maximum_fusion = bf16[3,1536,192]{1,2,0:T(8,128)(2,1)} fusion(bf16[1,1536,192]{1,2,0:T(8,128)(2,1)} %bitcast.150, bf16[2,1536,192]{1,2,0:T(8,128)(2,1)} %bitcast.149), kind=kLoop, calls=%fused_computation.15 | loop fusion | flops 884736 | bytes 3538944 | tf_op jit(solution)/shard_map/concatenate | solution.py:281
  37.0 5.5 %collective-permute-done.1 = bf16[512,512]{1,0:T(8,128)(2,1)} collective-permute-done((bf16[512,512]{1,0:T(8,128)(2,1)}, bf16[512,512]{1,0:T(8,128)(2,1)}, u32[]{:S(2)}, u32[]{:S(2)}) %collective-permute-start.1) | collective-permute-done | bytes 524320 | tf_op jit(solution)/shard_map/ppermute | solution.py:219
  44.7 1.9 collective-permute-start.8
  52.9 15.4 %shard_map.157 = bf16[2,768,128]{2,1,0:T(8,128)(2,1)} custom-call(s32[2]{0:T(128)} %pad_add_fusion.scalars, bf16[2,768,128]{2,1,0:T(8,128)(2,1)} %bitcast.145, bf16[1024,512]{1,0:T(8,128)(2,1)} %copy-done.1, bf16[1024,512]{1,0:T(8,128)(2,1)} %copy-done.4, bf16[1024,512]{1,0:T(8,128)(2,1)} %copy-done.6, bf16[1024,512]{1,0:T(8,128)(2,1)} %copy-done.5, ...), custom_call_target="tpu_custom_call" | custom-call | tf_op jit(solution)/shard_map/pallas_call | solution.py:185
  69.5 3.2 %multiply_reduce_fusion = (f32[128]{0:T(128)S(1)}, f32[128,1536]{1,0:T(8,128)S(1)}) fusion(bf16[128,1536]{0,1:T(8,128)(2,1)S(1)} %bitcast.147, bf16[1536,1536]{1,0:T(8,128)(2,1)} %param.23, bf16[1,128,1536]{2,1,0:T(8,128)(2,1)S(1)} %copy-done.10), kind=kOutput, calls=%fused_computation.43 | convolution fusion | flops 605159296 | bytes 6291968 | tf_op jit(solution)/shard_map/dot_general | solution.py:298
  73.9 10.1 %collective-permute-done.8 = bf16[3,1536,192]{1,2,0:T(8,128)(2,1)} collective-permute-done((bf16[3,1536,192]{1,2,0:T(8,128)(2,1)}, bf16[3,1536,192]{1,2,0:T(8,128)(2,1)}, u32[]{:S(2)}, u32[]{:S(2)}) %collective-permute-start.8) | collective-permute-done | bytes 1769504 | tf_op jit(solution)/shard_map/ppermute | solution.py:208
  84.0 2.6 %convolution_convert_fusion.4 = bf16[1024,1536]{1,0:T(8,128)(2,1)} fusion(pred[1024,128]{1,0:T(8,128)(4,1)S(1)} %fusion.4, bf16[128,1536]{1,0:T(8,128)(2,1)S(1)} %multiply_convert_fusion), kind=kOutput, calls=%fused_computation.6 | convolution fusion | flops 404226048 | bytes 3670016 | tf_op jit(solution)/shard_map/dot_general | solution.py:324
  86.6 13.5 %all-to-all-start = ((bf16[32,32,1536]{2,1,0:T(8,128)(2,1)}), bf16[32,32,1536]{2,1,0:T(8,128)(2,1)S(1)}, u32[]{:S(2)}, u32[]{:S(2)}) async-start(bf16[32,32,1536]{2,1,0:T(8,128)(2,1)} %bitcast.143), calls=%async_computation | async-start | bytes 6291456 | tf_op jit(solution)/shard_map/all_to_all | solution.py:325
  102.7 2.7 %collective-permute-start.10 = (bf16[3,768,192]{1,2,0:T(8,128)(2,1)S(1)}, bf16[3,768,192]{1,2,0:T(8,128)(2,1)S(1)}, u32[]{:S(2)}, u32[]{:S(2)}) collective-permute-start(bf16[3,768,192]{1,2,0:T(8,128)(2,1)S(1)} %slice.71), channel_id=1, source_target_pairs={{0,3},{1,0},{2,1},{3,2},{4,7},{5,4},{6,5},{7,6},{8,11},{9,8},{10,9... | collective-permute-start | bytes 2654216 | tf_op jit(solution)/shard_map/ppermute | solution.py:220
  105.4 18.2 %collective-permute-done.9 = bf16[3,768,192]{1,2,0:T(8,128)(2,1)S(1)} collective-permute-done((bf16[3,768,192]{1,2,0:T(8,128)(2,1)S(1)}, bf16[3,768,192]{1,2,0:T(8,128)(2,1)S(1)}, u32[]{:S(2)}, u32[]{:S(2)}) %collective-permute-start.9) | collective-permute-done | bytes 884768 | tf_op jit(solution)/shard_map/ppermute | solution.py:219
  125.7 14.2 %all-to-all-done = bf16[32,32,1536]{2,1,0:T(8,128)(2,1)S(1)} async-done(((bf16[32,32,1536]{2,1,0:T(8,128)(2,1)}), bf16[32,32,1536]{2,1,0:T(8,128)(2,1)S(1)}, u32[]{:S(2)}, u32[]{:S(2)}) %all-to-all-start) | async-done | bytes 3145760 | tf_op jit(solution)/shard_map/all_to_all | solution.py:325
  139.9 3.1 %convolution_maximum_fusion = f32[1024,192]{0,1:T(8,128)} fusion(bf16[1024,1536]{1,0:T(8,128)(2,1)S(1)} %bitcast.135, bf16[3,1536,192]{1,2,0:T(8,128)(2,1)} %collective-permute-done.8), kind=kOutput, calls=%fused_computation.22 | convolution fusion | flops 604176384 | bytes 4521984 | tf_op jit(solution)/shard_map/dot_general | solution.py:331
  143.0 3.2 %convolution_maximum_fusion.2 = f32[1024,192]{0,1:T(8,128)} fusion(bf16[1024,1536]{1,0:T(8,128)(2,1)S(1)} %bitcast.136, bf16[3,1536,192]{1,2,0:T(8,128)(2,1)} %copy-done.9), kind=kOutput, calls=%fused_computation.25 | convolution fusion | flops 604176384 | bytes 4521984 | tf_op jit(solution)/shard_map/dot_general | solution.py:331
  146.2 3.1 %convolution_maximum_fusion.3 = f32[1024,192]{0,1:T(8,128)} fusion(bf16[1024,1536]{1,0:T(8,128)(2,1)S(1)} %bitcast.137, bf16[3,1536,192]{1,2,0:T(8,128)(2,1)} %pad_maximum_fusion), kind=kOutput, calls=%fused_computation.27 | convolution fusion | flops 604176384 | bytes 4521984 | tf_op jit(solution)/shard_map/dot_general | solution.py:331
  149.4 5.2 %convolution_convert_fusion = bf16[1024,1536]{1,0:T(8,128)(2,1)} fusion(f32[1024,192]{0,1:T(8,128)} %convolution_maximum_fusion, bf16[1024,1536]{1,0:T(8,128)(2,1)S(1)} %bitcast.138, bf16[3,1536,192]{1,2,0:T(8,128)(2,1)} %collective-permute-done.8), kind=kOutput, calls=%fused_computation.2 | convolution fusion | flops 1209925632 | bytes 8257536 | tf_op jit(solution)/shard_map/dot_general | solution.py:334
  154.5 3.1 %fusion.24 = f32[1024,192]{0,1:T(8,128)} fusion(bf16[1024,1536]{1,0:T(8,128)(2,1)S(1)} %bitcast.139, bf16[3,1536,192]{1,2,0:T(8,128)(2,1)} %constant_dynamic-update-slice_fusion.2), kind=kOutput, calls=%fused_computation.46 | convolution fusion | flops 603979776 | bytes 4521984 | tf_op jit(solution)/shard_map/dot_general | solution.py:332
  157.7 5.2 %convolution_convert_fusion.2 = bf16[1024,1536]{1,0:T(8,128)(2,1)} fusion(f32[1024,192]{0,1:T(8,128)} %convolution_maximum_fusion.2, bf16[1024,1536]{1,0:T(8,128)(2,1)S(1)} %bitcast.140, bf16[3,1536,192]{1,2,0:T(8,128)(2,1)} %copy-done.9), kind=kOutput, calls=%fused_computation.4 | convolution fusion | flops 1209925632 | bytes 8257536 | tf_op jit(solution)/shard_map/dot_general | solution.py:334
  162.9 5.2 %convolution_convert_fusion.3 = bf16[1024,1536]{1,0:T(8,128)(2,1)} fusion(f32[1024,192]{0,1:T(8,128)} %convolution_maximum_fusion.3, bf16[1024,1536]{1,0:T(8,128)(2,1)S(1)} %bitcast.141, bf16[3,1536,192]{1,2,0:T(8,128)(2,1)} %pad_maximum_fusion), kind=kOutput, calls=%fused_computation.5 | convolution fusion | flops 1209925632 | bytes 8257536 | tf_op jit(solution)/shard_map/dot_general | solution.py:334
  168.1 8.5 %add_convert_fusion = bf16[1024,1536]{1,0:T(8,128)(2,1)} fusion(bf16[1024,1536]{1,0:T(8,128)(2,1)} %convolution_convert_fusion, bf16[1024,1536]{1,0:T(8,128)(2,1)} %convolution_convert_fusion.2, bf16[1024,1536]{1,0:T(8,128)(2,1)} %convolution_convert_fusion.3, f32[1024,192]{0,1:T(8,128)} %fusion.24, bf16[1024,1536]{1,0:T(8,128)(2,1)S(1)} %bitcast.142, ...), kind=kOutput, calls=%fused_computation.1 | convolution fusion | flops 1222705152 | bytes 17694720 | tf_op jit(solution)/shard_map/dot_general | solution.py:334
  176.6 5.2 %all-to-all-start.1 = ((bf16[32,32,1536]{2,1,0:T(8,128)(2,1)}), bf16[32,32,1536]{2,1,0:T(8,128)(2,1)}, u32[]{:S(2)}, u32[]{:S(2)}) async-start(bf16[32,32,1536]{2,1,0:T(8,128)(2,1)} %bitcast.144), calls=%async_computation.1 | async-start | bytes 6291456 | tf_op jit(solution)/shard_map/all_to_all | solution.py:339
  182.1 1.5 slice_bitcast_fusion.7
  183.8 3.8 %gather_fusion = f32[512]{0:T(512)S(1)} fusion(f32[128,32]{0,1:T(8,128)S(1)} %fusion.64, s32[512]{0:T(512)S(1)} %reshape.190), kind=kCustom, calls=%fused_computation | custom fusion | bytes 8192 | tf_op jit(solution)/shard_map/jit(take_along_axis)/gather | solution.py:347
  187.8 33.9 %all-to-all-done.1 = bf16[32,32,1536]{2,1,0:T(8,128)(2,1)} async-done(((bf16[32,32,1536]{2,1,0:T(8,128)(2,1)}), bf16[32,32,1536]{2,1,0:T(8,128)(2,1)}, u32[]{:S(2)}, u32[]{:S(2)}) %all-to-all-start.1) | async-done | bytes 3145760 | tf_op jit(solution)/shard_map/all_to_all | solution.py:339
  221.7 3.8 %fusion.5 = f32[128,1536]{1,0:T(8,128)S(1)} fusion(bf16[1024,1536,1]{1,0,2:T(8,128)(2,1)} %bitcast.39, f32[128,4]{0,1:T(4,128)S(1)} %multiply_divide_fusion, s32[128,4]{0,1:T(4,128)S(1)} %fusion.61), kind=kOutput, calls=%fused_computation.16 | convolution fusion | flops 1612513280 | bytes 3936256 | tf_op jit(solution)/shard_map/dot_general | solution.py:342
  (75 shorter events, 23.4 us)
Async XLA Ops:
  0.6 183.0 %copy-start = (bf16[1536,32]{0,1:T(8,128)(2,1)S(1)}, bf16[1536,32]{0,1:T(8,128)(2,1)}, u32[]{:S(2)}) copy-start(bf16[1536,32]{0,1:T(8,128)(2,1)} %param.25) | copy-start | bytes 294916
  2.0 29.5 %copy-start.1 = (bf16[1024,512]{1,0:T(8,128)(2,1)}, bf16[1024,512]{1,0:T(8,128)(2,1)S(1)}, u32[]{:S(2)}) copy-start(bf16[1024,512]{1,0:T(8,128)(2,1)S(1)} %pad_maximum_fusion.1.k0_ref.v0_ref) | copy-start | bytes 3145732
  2.0 25.9 %collective-permute-start = (bf16[1024,512]{1,0:T(8,128)(2,1)S(1)}, bf16[1024,512]{1,0:T(8,128)(2,1)S(1)}, u32[]{:S(2)}, u32[]{:S(2)}) collective-permute-start(bf16[1024,512]{1,0:T(8,128)(2,1)S(1)} %pad_maximum_fusion.1.k0_ref.v0_ref), channel_id=1, source_target_pairs={{0,1},{1,2},{2,3},{3,0},{4,5},{5,6},{6,7},{7,4},{8,9},{9,10},{10,1... | collective-permute-start | bytes 3145736 | tf_op jit(solution)/shard_map/ppermute | solution.py:208
  4.1 26.5 %collective-permute-start.2 = (bf16[1024,512]{1,0:T(8,128)(2,1)S(1)}, bf16[1024,512]{1,0:T(8,128)(2,1)S(1)}, u32[]{:S(2)}, u32[]{:S(2)}) collective-permute-start(bf16[1024,512]{1,0:T(8,128)(2,1)S(1)} %pad_maximum_fusion.1.k0_ref.v0_ref), channel_id=1, source_target_pairs={{0,3},{1,0},{2,1},{3,2},{4,7},{5,4},{6,5},{7,6},{8,11},{9,8},{10,9... | collective-permute-start | bytes 3145736 | tf_op jit(solution)/shard_map/ppermute | solution.py:208
  9.2 41.6 %collective-permute-start.6 = (bf16[128,512]{1,0:T(8,128)(2,1)}, bf16[128,512]{1,0:T(8,128)(2,1)}, u32[]{:S(2)}, u32[]{:S(2)}) collective-permute-start(bf16[128,512]{1,0:T(8,128)(2,1)} %fusion.17), channel_id=1, source_target_pairs={{0,3},{4,7},{8,11},{12,15},{16,19},{20,23},{24,27},{28,31},{32,35}... | collective-permute-start | bytes 393224 | tf_op jit(solution)/shard_map/ppermute | solution.py:271
  13.1 37.7 %collective-permute-start.5 = (bf16[128,512]{1,0:T(8,128)(2,1)}, bf16[128,512]{1,0:T(8,128)(2,1)}, u32[]{:S(2)}, u32[]{:S(2)}) collective-permute-start(bf16[128,512]{1,0:T(8,128)(2,1)} %fusion.17), channel_id=1, source_target_pairs={{0,2},{1,3},{4,6},{5,7},{8,10},{9,11},{12,14},{13,15},{16,18},{17,... | collective-permute-start | bytes 393224 | tf_op jit(solution)/shard_map/ppermute | solution.py:271
  15.0 35.8 %collective-permute-start.4 = (bf16[128,512]{1,0:T(8,128)(2,1)}, bf16[128,512]{1,0:T(8,128)(2,1)}, u32[]{:S(2)}, u32[]{:S(2)}) collective-permute-start(bf16[128,512]{1,0:T(8,128)(2,1)} %fusion.17), channel_id=1, source_target_pairs={{0,1},{1,2},{2,3},{4,5},{5,6},{6,7},{8,9},{9,10},{10,11},{12,13},{... | collective-permute-start | bytes 393224 | tf_op jit(solution)/shard_map/ppermute | solution.py:271
  27.8 15.7 %copy-start.4 = (bf16[1024,512]{1,0:T(8,128)(2,1)}, bf16[1024,512]{1,0:T(8,128)(2,1)S(1)}, u32[]{:S(2)}) copy-start(bf16[1024,512]{1,0:T(8,128)(2,1)S(1)} %collective-permute-done.k1_ref.v1_ref) | copy-start | bytes 3145732
  28.7 13.8 %collective-permute-start.1 = (bf16[512,512]{1,0:T(8,128)(2,1)}, bf16[512,512]{1,0:T(8,128)(2,1)}, u32[]{:S(2)}, u32[]{:S(2)}) collective-permute-start(bf16[512,512]{1,0:T(8,128)(2,1)} %slice.82), channel_id=1, source_target_pairs={{0,1},{1,2},{2,3},{3,0},{4,5},{5,6},{6,7},{7,4},{8,9},{9,10},{10,1... | collective-permute-start | bytes 1572872 | tf_op jit(solution)/shard_map/ppermute | solution.py:219
  30.5 14.1 %copy-start.5 = (bf16[1024,512]{1,0:T(8,128)(2,1)}, bf16[1024,512]{1,0:T(8,128)(2,1)S(1)}, u32[]{:S(2)}) copy-start(bf16[1024,512]{1,0:T(8,128)(2,1)S(1)} %collective-permute-done.2.k3_ref.v3_ref) | copy-start | bytes 3145732
  31.5 12.1 %collective-permute-start.3 = (bf16[512,512]{1,0:T(8,128)(2,1)}, bf16[512,512]{1,0:T(8,128)(2,1)}, u32[]{:S(2)}, u32[]{:S(2)}) collective-permute-start(bf16[512,512]{1,0:T(8,128)(2,1)} %slice.83), channel_id=1, source_target_pairs={{0,3},{1,0},{2,1},{3,2},{4,7},{5,4},{6,5},{7,6},{8,11},{9,8},{10,9... | collective-permute-start | bytes 1572872 | tf_op jit(solution)/shard_map/ppermute | solution.py:220
  44.7 8.2 %copy-start.6 = (bf16[1024,512]{1,0:T(8,128)(2,1)}, bf16[1024,512]{1,0:T(8,128)(2,1)S(1)}, u32[]{:S(2)}) copy-start(bf16[1024,512]{1,0:T(8,128)(2,1)S(1)} %constant_dynamic-update-slice_fusion.k2_ref.v2_ref) | copy-start | bytes 3145732
  44.7 39.3 %collective-permute-start.8 = (bf16[3,1536,192]{1,2,0:T(8,128)(2,1)}, bf16[3,1536,192]{1,2,0:T(8,128)(2,1)}, u32[]{:S(2)}, u32[]{:S(2)}) collective-permute-start(bf16[3,1536,192]{1,2,0:T(8,128)(2,1)} %pad_maximum_fusion), channel_id=1, source_target_pairs={{0,3},{1,0},{2,1},{3,2},{4,7},{5,4},{6,5},{7,6},{8,11},{9,8},{10,9... | collective-permute-start | bytes 5308424 | tf_op jit(solution)/shard_map/ppermute | solution.py:208
  46.6 37.4 %collective-permute-start.7 = (bf16[3,1536,192]{1,2,0:T(8,128)(2,1)}, bf16[3,1536,192]{1,2,0:T(8,128)(2,1)S(1)}, u32[]{:S(2)}, u32[]{:S(2)}) collective-permute-start(bf16[3,1536,192]{1,2,0:T(8,128)(2,1)} %pad_maximum_fusion), channel_id=1, source_target_pairs={{0,1},{1,2},{2,3},{3,0},{4,5},{5,6},{6,7},{7,4},{8,9},{9,10},{10,1... | collective-permute-start | bytes 5308424 | tf_op jit(solution)/shard_map/ppermute | solution.py:208
  52.9 16.6 %copy-start.10 = (bf16[1,128,1536]{2,1,0:T(8,128)(2,1)S(1)}, bf16[1,128,1536]{2,1,0:T(8,128)(2,1)}, u32[]{:S(2)}) copy-start(bf16[1,128,1536]{2,1,0:T(8,128)(2,1)} %param.14) | copy-start | bytes 1179652
  69.5 4.2 %copy-start.11 = (f32[1536]{0:T(1024)S(1)}, f32[1536]{0:T(1024)}, u32[]{:S(2)}) copy-start(f32[1536]{0:T(1024)} %param.24) | copy-start | bytes 18436
  72.8 1.0 copy-start.2
  73.9 10.1 %copy-start.7 = (bf16[128,1536]{1,0:T(8,128)(2,1)}, bf16[128,1536]{1,0:T(8,128)(2,1)S(1)}, u32[]{:S(2)}) copy-start(bf16[128,1536]{1,0:T(8,128)(2,1)S(1)} %multiply_convert_fusion) | copy-start | bytes 1179652
  84.0 2.6 %copy-start.9 = (bf16[3,1536,192]{1,2,0:T(8,128)(2,1)}, bf16[3,1536,192]{1,2,0:T(8,128)(2,1)S(1)}, u32[]{:S(2)}) copy-start(bf16[3,1536,192]{1,2,0:T(8,128)(2,1)S(1)} %collective-permute-done.7) | copy-start | bytes 5308420
  86.6 53.3 %all-to-all-start = ((bf16[32,32,1536]{2,1,0:T(8,128)(2,1)}), bf16[32,32,1536]{2,1,0:T(8,128)(2,1)S(1)}, u32[]{:S(2)}, u32[]{:S(2)}) async-start(bf16[32,32,1536]{2,1,0:T(8,128)(2,1)} %bitcast.143), calls=%async_computation | async-start | bytes 6291456 | tf_op jit(solution)/shard_map/all_to_all | solution.py:325
  101.4 22.3 %collective-permute-start.9 = (bf16[3,768,192]{1,2,0:T(8,128)(2,1)S(1)}, bf16[3,768,192]{1,2,0:T(8,128)(2,1)S(1)}, u32[]{:S(2)}, u32[]{:S(2)}) collective-permute-start(bf16[3,768,192]{1,2,0:T(8,128)(2,1)S(1)} %slice.70), channel_id=1, source_target_pairs={{0,1},{1,2},{2,3},{3,0},{4,5},{5,6},{6,7},{7,4},{8,9},{9,10},{10,1... | collective-permute-start | bytes 2654216 | tf_op jit(solution)/shard_map/ppermute | solution.py:219
  102.7 21.9 %collective-permute-start.10 = (bf16[3,768,192]{1,2,0:T(8,128)(2,1)S(1)}, bf16[3,768,192]{1,2,0:T(8,128)(2,1)S(1)}, u32[]{:S(2)}, u32[]{:S(2)}) collective-permute-start(bf16[3,768,192]{1,2,0:T(8,128)(2,1)S(1)} %slice.71), channel_id=1, source_target_pairs={{0,3},{1,0},{2,1},{3,2},{4,7},{5,4},{6,5},{7,6},{8,11},{9,8},{10,9... | collective-permute-start | bytes 2654216 | tf_op jit(solution)/shard_map/ppermute | solution.py:220
  176.6 7.0 %copy-start.8 = (bf16[128,1536]{1,0:T(8,128)(2,1)S(1)}, bf16[128,1536]{1,0:T(8,128)(2,1)}, u32[]{:S(2)}) copy-start(bf16[128,1536]{1,0:T(8,128)(2,1)} %copy-done.7) | copy-start | bytes 1179652
  176.6 45.1 %all-to-all-start.1 = ((bf16[32,32,1536]{2,1,0:T(8,128)(2,1)}), bf16[32,32,1536]{2,1,0:T(8,128)(2,1)}, u32[]{:S(2)}, u32[]{:S(2)}) async-start(bf16[32,32,1536]{2,1,0:T(8,128)(2,1)} %bitcast.144), calls=%async_computation.1 | async-start | bytes 6291456 | tf_op jit(solution)/shard_map/all_to_all | solution.py:339
  221.7 3.9 %copy-start.3 = (f32[128,1536]{1,0:T(8,128)S(1)}, f32[128,1536]{1,0:T(8,128)}, u32[]{:S(2)}) copy-start(f32[128,1536]{1,0:T(8,128)} %copy-done.2) | copy-start | bytes 2359300

commit v9 on v8

--- a/solution.py
+++ b/solution.py
@@ -277,8 +277,8 @@
             chosen = jnp.where(distance == shift, received[shift], chosen)
         new_parts.append(chosen)
     new_parts = jnp.stack(new_parts)
-    stacked_weights, _ = lax.optimization_barrier(
-        (jnp.concatenate([gate_up[0], down_proj[0].T[None]], axis=0), shifted_kv[2])
+    stacked_weights, _, _ = lax.optimization_barrier(
+        (jnp.concatenate([gate_up[0], down_proj[0].T[None]], axis=0), shifted_kv[2], new_parts)
     )
     weights_below, weights_above = ring_neighbours(stacked_weights)
     grouped = (
@@ -301,12 +301,9 @@
     moe_in, weights_below, weights_above = lax.optimization_barrier(
         (moe_in, weights_below, weights_above)
     )
-    shifted_weights = [
-        stacked_weights,
-        weights_below,
-        ring_far(weights_below, weights_above, 1),
-        weights_above,
-    ]
+    all_weights = jnp.stack(
+        [stacked_weights, weights_below, ring_far(weights_below, weights_above, 1), weights_above]
+    )
     logits = jnp.dot(moe_in, router, preferred_element_type=jnp.float32)
     expert_count = router.shape[1]
     top_count = routes.shape[2]
@@ -326,16 +323,17 @@
         send_rows.reshape(expert_count, capacity, model_width), "req", 0, 0, tiled=True
     )
     flat_rows = grouped_rows.reshape(-1, model_width)
-    expert_sum = None
-    for weights_now in shifted_weights:
-        gate_out = jnp.dot(flat_rows, weights_now[0], preferred_element_type=jnp.float32)
-        up_out = jnp.dot(flat_rows, weights_now[1], preferred_element_type=jnp.float32)
-        activation = (jnp.maximum(gate_out, 0.0) * up_out).astype(jnp.bfloat16)
-        partial = lax.dot_general(
-            activation, weights_now[2], (((1,), (1,)), ((), ())), preferred_element_type=jnp.float32
-        ).astype(jnp.bfloat16)
-        expert_sum = partial.astype(jnp.float32) if expert_sum is None else expert_sum + partial
-    expert_out = expert_sum.astype(jnp.bfloat16)
+    gate_out = jnp.einsum(
+        "nd,hdf->hnf", flat_rows, all_weights[:, 0], preferred_element_type=jnp.float32
+    )
+    up_out = jnp.einsum(
+        "nd,hdf->hnf", flat_rows, all_weights[:, 1], preferred_element_type=jnp.float32
+    )
+    activation = (jnp.maximum(gate_out, 0.0) * up_out).astype(jnp.bfloat16)
+    partials = jnp.einsum(
+        "hnf,hdf->hnd", activation, all_weights[:, 2], preferred_element_type=jnp.float32
+    ).astype(jnp.bfloat16)
+    expert_out = jnp.sum(partials.astype(jnp.float32), axis=0).astype(jnp.bfloat16)
     returned = lax.all_to_all(
         expert_out.reshape(-1, capacity, model_width), "req", 0, 0, tiled=True
     )

time: 228 us -> 212 us (0.930)
  matrix products: 49.2 us -> 31.5 us
  Pallas kernels: 15.4 us -> 9.56 us
  other arithmetic: 11.3 us -> 15.6 us
  waiting for transfers between devices: 91.4 us -> 95.3 us
    ppermute x2, waiting for transfers between devices: 0.01 us -> 19.5 us  [ring_far(): lax.ppermute(lax.slice_in_dim(from_above, half, extent, axis=split_axis),...]
    dot_general x8 -> x2, matrix products: 36.7 us -> 18.8 us  [the longest x1 12 us: body(): jnp.einsum('hnf,hdf->hnd', activation, all_weights[:, 2], preferred_eleme...]
    ppermute x2, waiting for transfers between devices: 23.7 us -> 8.13 us  [ring_far(): lax.ppermute(lax.slice_in_dim(from_below, 0, half, axis=split_axis), axis...]
    ppermute x2, waiting for transfers between devices: 10.1 us -> 23 us  [ring_neighbours(): lax.ppermute(shard, axis_name, down)]
    ppermute x2, waiting for transfers between devices: 9.4 us -> 1.3 us  [ring_neighbours(): lax.ppermute(shard, axis_name, up)]
    pallas_call x1, Pallas kernels: 15.4 us -> 9.56 us  [attention(): pl.pallas_call(functools.partial(attention_kernel, token_count), out_shap...]
    another operation x2 -> x4, other arithmetic: 1.2 us -> 6.87 us  [the longest x2 5.67 us: body(): jnp.stack([stacked_weights, weights_below, ring_far(weights_below, weight...]
    all_to_all x1, waiting for transfers between devices: 14.2 us -> 9.42 us  [body(): lax.all_to_all(send_rows.reshape(expert_count, capacity, model_width), 'r...]
  transfers between devices with their start and end apart: 13 -> 13, of which waited for: 6 -> 8; matrix products, arithmetic and copies ran while one was open for 15% -> 18% of each run, Pallas kernels for 7% -> 5%
where the time goes in v9:
time: 212 us; the launch traced here: 211 us
  waiting for transfers between devices  95.3 us (45%)
  starting transfers between devices  39.2 us (18%)
  matrix products  31.5 us (15%)
  local copies, waits for them, and re-layouts  18.4 us (9%)
  other arithmetic  15.6 us (7%)
  Pallas kernels  9.56 us (5%)
    all_to_all x1, waiting for transfers between devices, body(): lax.all_to_all(expert_out.reshape(-1, capacity, model_width), 'req', 0, 0...  33.9 us
    ppermute x2, waiting for transfers between devices, ring_neighbours(): lax.ppermute(shard, axis_name, down)  23 us
    ppermute x2, waiting for transfers between devices, ring_far(): lax.ppermute(lax.slice_in_dim(from_above, half, extent, axis=split_axis),...  19.5 us
    all_to_all x1, starting transfers between devices, body(): lax.all_to_all(send_rows.reshape(expert_count, capacity, model_width), 'r...  12.8 us
    dot_general x1, matrix products, body(): jnp.einsum('hnf,hdf->hnd', activation, all_weights[:, 2], preferred_eleme...  12 us
    ppermute x3, starting transfers between devices, body(): received.append(lax.ppermute(new_kv, 'hid', pairs))  9.63 us
    pallas_call x1, Pallas kernels, attention(): pl.pallas_call(functools.partial(attention_kernel, token_count), out_shap...  9.56 us
    all_to_all x1, waiting for transfers between devices, body(): lax.all_to_all(send_rows.reshape(expert_count, capacity, model_width), 'r...  9.42 us
  transfers between devices with their start and end apart: 13, of which 8 were waited for; matrix products, arithmetic and copies ran while one was open for 18% of the time, Pallas kernels for 5%

profile of v9, /device:TPU:1, one launch (start us, length us, event | category | flops | bytes accessed | tf_op | source)
XLA Modules:
  0.0 211.1 jit_solution(15685030462228799805)
XLA Ops:
  0.7 1.3 pad_maximum_fusion.2.k0_ref.v0_ref
  2.0 3.4 %collective-permute-start.2 = (bf16[1024,512]{1,0:T(8,128)(2,1)S(1)}, bf16[1024,512]{1,0:T(8,128)(2,1)}, u32[]{:S(2)}, u32[]{:S(2)}) collective-permute-start(bf16[1024,512]{1,0:T(8,128)(2,1)S(1)} %pad_maximum_fusion.2.k0_ref.v0_ref), channel_id=1, source_target_pairs={{0,3},{1,0},{2,1},{3,2},{4,7},{5,4},{6,5},{7,6},{8,11},{9,8},{10,9... | collective-permute-start | bytes 3145736 | tf_op jit(solution)/shard_map/ppermute | solution.py:208
  6.5 2.6 %fusion.16 = bf16[128,512]{1,0:T(8,128)(2,1)} fusion(bf16[1536,256]{1,0:T(8,128)(2,1)} %param.22, bf16[1536,256]{1,0:T(8,128)(2,1)} %param.21, bf16[1,128,1536]{2,1,0:T(8,128)(2,1)} %param.14, f32[1536]{0:T(1024)} %param.20, f32[128]{0:T(128)S(1)} %add_rsqrt_fusion.1), kind=kOutput, calls=%fused_computation.29 | convolution fusion | flops 205324288 | bytes 2103808 | tf_op jit(solution)/shard_map/dot_general | solution.py:260
  9.1 5.2 %collective-permute-start.6 = (bf16[128,512]{1,0:T(8,128)(2,1)}, bf16[128,512]{1,0:T(8,128)(2,1)}, u32[]{:S(2)}, u32[]{:S(2)}) collective-permute-start(bf16[128,512]{1,0:T(8,128)(2,1)} %fusion.16), channel_id=1, source_target_pairs={{0,3},{4,7},{8,11},{12,15},{16,19},{20,23},{24,27},{28,31},{32,35}... | collective-permute-start | bytes 393224 | tf_op jit(solution)/shard_map/ppermute | solution.py:271
  14.4 1.9 collective-permute-start.5
  16.3 2.5 %collective-permute-start.4 = (bf16[128,512]{1,0:T(8,128)(2,1)}, bf16[128,512]{1,0:T(8,128)(2,1)}, u32[]{:S(2)}, u32[]{:S(2)}) collective-permute-start(bf16[128,512]{1,0:T(8,128)(2,1)} %fusion.16), channel_id=1, source_target_pairs={{0,1},{1,2},{2,3},{4,5},{5,6},{6,7},{8,9},{9,10},{10,11},{12,13},{... | collective-permute-start | bytes 393224 | tf_op jit(solution)/shard_map/ppermute | solution.py:271
  20.2 1.4 pad_maximum_fusion.1
  21.6 6.7 %collective-permute-done.2.k3_ref.v3_ref = bf16[1024,512]{1,0:T(8,128)(2,1)} collective-permute-done((bf16[1024,512]{1,0:T(8,128)(2,1)S(1)}, bf16[1024,512]{1,0:T(8,128)(2,1)}, u32[]{:S(2)}, u32[]{:S(2)}) %collective-permute-start.2) | collective-permute-done | bytes 1048608 | tf_op jit(solution)/shard_map/ppermute | solution.py:208
  28.4 1.9 slice.47
  30.2 5.2 %collective-permute-start.3 = (bf16[512,512]{1,0:T(8,128)(2,1)}, bf16[512,512]{1,0:T(8,128)(2,1)S(1)}, u32[]{:S(2)}, u32[]{:S(2)}) collective-permute-start(bf16[512,512]{1,0:T(8,128)(2,1)} %slice.47), channel_id=1, source_target_pairs={{0,3},{1,0},{2,1},{3,2},{4,7},{5,4},{6,5},{7,6},{8,11},{9,8},{10,9... | collective-permute-start | bytes 1572872 | tf_op jit(solution)/shard_map/ppermute | solution.py:220
  41.5 7.0 %collective-permute-done.1 = bf16[512,512]{1,0:T(8,128)(2,1)} collective-permute-done((bf16[512,512]{1,0:T(8,128)(2,1)S(1)}, bf16[512,512]{1,0:T(8,128)(2,1)}, u32[]{:S(2)}, u32[]{:S(2)}) %collective-permute-start.1) | collective-permute-done | bytes 524320 | tf_op jit(solution)/shard_map/ppermute | solution.py:219
  49.6 1.5 collective-permute-start.7
  51.6 1.2 copy.61
  54.8 9.6 %shard_map.157 = bf16[2,768,128]{2,1,0:T(8,128)(2,1)} custom-call(s32[2]{0:T(128)} %pad_add_fusion.scalars, bf16[2,768,128]{2,1,0:T(8,128)(2,1)} %bitcast.117, bf16[1024,512]{1,0:T(8,128)(2,1)} %copy-done.1, bf16[1024,512]{1,0:T(8,128)(2,1)} %collective-permute-done.k1_ref.v1_ref, bf16[1024,512]{1,0:T(8,128)(2,1)} %copy-done.2, ...), custom_call_target="tpu_custom_call" | custom-call | tf_op jit(solution)/shard_map/pallas_call | solution.py:185
  64.3 1.9 copy.63
  66.3 3.4 %multiply_reduce_fusion = (f32[128]{0:T(128)S(1)}, f32[128,1536]{1,0:T(8,128)S(1)}) fusion(bf16[128,1536]{0,1:T(8,128)(2,1)} %bitcast.119, bf16[1536,1536]{1,0:T(8,128)(2,1)} %param.23, bf16[1,128,1536]{2,1,0:T(8,128)(2,1)S(1)} %copy-done.3), kind=kOutput, calls=%fused_computation.37 | convolution fusion | flops 605159296 | bytes 6291968 | tf_op jit(solution)/shard_map/dot_general | solution.py:298
  69.8 16.3 %collective-permute-done.8 = bf16[3,1536,192]{1,2,0:T(8,128)(2,1)} collective-permute-done((bf16[3,1536,192]{1,2,0:T(8,128)(2,1)S(1)}, bf16[3,1536,192]{1,2,0:T(8,128)(2,1)}, u32[]{:S(2)}, u32[]{:S(2)}) %collective-permute-start.8) | collective-permute-done | bytes 1769504 | tf_op jit(solution)/shard_map/ppermute | solution.py:208
  86.1 1.3 collective-permute-done.7
  87.4 2.7 %convolution_convert_fusion.1 = bf16[1024,1536]{1,0:T(8,128)(2,1)} fusion(pred[1024,128]{1,0:T(8,128)(4,1)S(1)} %fusion.7, bf16[128,1536]{1,0:T(8,128)(2,1)S(1)} %multiply_convert_fusion.1), kind=kOutput, calls=%fused_computation.3 | convolution fusion | flops 404226048 | bytes 3670016 | tf_op jit(solution)/shard_map/dot_general | solution.py:321
  90.1 12.8 %all-to-all-start = ((bf16[32,32,1536]{2,1,0:T(8,128)(2,1)}), bf16[32,32,1536]{2,1,0:T(8,128)(2,1)}, u32[]{:S(2)}, u32[]{:S(2)}) async-start(bf16[32,32,1536]{2,1,0:T(8,128)(2,1)} %bitcast.31), calls=%async_computation | async-start | bytes 6291456 | tf_op jit(solution)/shard_map/all_to_all | solution.py:322
  102.9 1.2 slice.37
  105.4 1.5 collective-permute-start.9
  106.9 19.5 %collective-permute-done.10 = bf16[3,768,192]{1,2,0:T(8,128)(2,1)S(1)} collective-permute-done((bf16[3,768,192]{1,2,0:T(8,128)(2,1)S(1)}, bf16[3,768,192]{1,2,0:T(8,128)(2,1)S(1)}, u32[]{:S(2)}, u32[]{:S(2)}) %collective-permute-start.10) | collective-permute-done | bytes 884768 | tf_op jit(solution)/shard_map/ppermute | solution.py:220
  127.8 5.5 %pad_maximum_fusion = bf16[4,3,1536,192]{2,3,0,1:T(8,128)(2,1)} fusion(bf16[1,3,1536,192]{2,3,0,1:T(8,128)(2,1)} %bitcast.29, bf16[1,3,1536,192]{2,3,0,1:T(8,128)(2,1)S(1)} %maximum_bitcast_fusion, bf16[1,3,1536,192]{2,3,0,1:T(8,128)(2,1)} %bitcast.26, bf16[1,3,1536,192]{2,3,0,1:T(8,128)(2,1)S(1)} %bitcast.115), kind=kLoop, calls=%fused_computation.2 | loop fusion | flops 10616832 | bytes 14155776 | tf_op jit(solution)/shard_map/stack | solution.py:304
  133.3 9.4 %all-to-all-done = bf16[32,32,1536]{2,1,0:T(8,128)(2,1)} async-done(((bf16[32,32,1536]{2,1,0:T(8,128)(2,1)}), bf16[32,32,1536]{2,1,0:T(8,128)(2,1)}, u32[]{:S(2)}, u32[]{:S(2)}) %all-to-all-start) | async-done | bytes 3145760 | tf_op jit(solution)/shard_map/all_to_all | solution.py:322
  142.7 6.9 %fusion.4 = f32[4,192,1024]{2,1,0:T(8,128)} fusion(bf16[1024,1536,1]{1,0,2:T(8,128)(2,1)} %bitcast.33, bf16[4,3,1536,192]{2,3,0,1:T(8,128)(2,1)} %pad_maximum_fusion), kind=kOutput, calls=%fused_computation.14 | convolution fusion | flops 2415919104 | bytes 8650752 | tf_op jit(solution)/shard_map/nd,hdf->hnf/dot_general | solution.py:326
  149.6 12.0 %fusion = bf16[1024,1536]{1,0:T(8,128)(2,1)} fusion(bf16[4,3,1536,192]{2,3,0,1:T(8,128)(2,1)} %pad_maximum_fusion, f32[4,192,1024]{2,1,0:T(8,128)} %fusion.4, bf16[1024,1536,1]{1,0,2:T(8,128)(2,1)} %bitcast.33), kind=kOutput, calls=%fused_computation.6 | convolution fusion | flops 4845207552 | bytes 14155776 | tf_op jit(solution)/shard_map/hnf,hdf->hnd/dot_general | solution.py:333
  161.5 5.0 %all-to-all-start.1 = ((bf16[32,32,1536]{2,1,0:T(8,128)(2,1)}), bf16[32,32,1536]{2,1,0:T(8,128)(2,1)}, u32[]{:S(2)}, u32[]{:S(2)}) async-start(bf16[32,32,1536]{2,1,0:T(8,128)(2,1)} %bitcast.116), calls=%async_computation.1 | async-start | bytes 6291456 | tf_op jit(solution)/shard_map/all_to_all | solution.py:337
  166.8 1.5 slice_bitcast_fusion.10
  168.5 3.8 %gather_fusion = f32[512]{0:T(512)S(1)} fusion(f32[128,32]{0,1:T(8,128)S(1)} %fusion.37, s32[512]{0:T(512)S(1)} %reshape.190), kind=kCustom, calls=%fused_computation | custom fusion | bytes 8192 | tf_op jit(solution)/shard_map/jit(take_along_axis)/gather | solution.py:345
  172.5 33.9 %all-to-all-done.1 = bf16[32,32,1536]{2,1,0:T(8,128)(2,1)} async-done(((bf16[32,32,1536]{2,1,0:T(8,128)(2,1)}), bf16[32,32,1536]{2,1,0:T(8,128)(2,1)}, u32[]{:S(2)}, u32[]{:S(2)}) %all-to-all-start.1) | async-done | bytes 3145760 | tf_op jit(solution)/shard_map/all_to_all | solution.py:337
  206.5 3.8 %fusion.8 = f32[128,1536]{1,0:T(8,128)S(1)} fusion(bf16[1024,1536,1]{1,0,2:T(8,128)(2,1)} %bitcast.39, f32[128,4]{0,1:T(4,128)S(1)} %multiply_divide_fusion, s32[128,4]{0,1:T(4,128)S(1)} %fusion.34), kind=kOutput, calls=%fused_computation.21 | convolution fusion | flops 1612513280 | bytes 3936256 | tf_op jit(solution)/shard_map/dot_general | solution.py:340
  (59 shorter events, 15.8 us)
Async XLA Ops:
  0.6 167.7 %copy-start = (bf16[1536,32]{0,1:T(8,128)(2,1)S(1)}, bf16[1536,32]{0,1:T(8,128)(2,1)}, u32[]{:S(2)}) copy-start(bf16[1536,32]{0,1:T(8,128)(2,1)} %param.25) | copy-start | bytes 294916
  0.6 19.6 %copy-start.4 = (bf16[1,192,1536]{2,1,0:T(8,128)(2,1)S(1)}, bf16[1,192,1536]{2,1,0:T(8,128)(2,1)}, u32[]{:S(2)}) copy-start(bf16[1,192,1536]{2,1,0:T(8,128)(2,1)} %param.27) | copy-start | bytes 1769476
  2.0 19.6 %copy-start.1 = (bf16[1024,512]{1,0:T(8,128)(2,1)}, bf16[1024,512]{1,0:T(8,128)(2,1)S(1)}, u32[]{:S(2)}) copy-start(bf16[1024,512]{1,0:T(8,128)(2,1)S(1)} %pad_maximum_fusion.2.k0_ref.v0_ref) | copy-start | bytes 3145732
  2.0 26.3 %collective-permute-start.2 = (bf16[1024,512]{1,0:T(8,128)(2,1)S(1)}, bf16[1024,512]{1,0:T(8,128)(2,1)}, u32[]{:S(2)}, u32[]{:S(2)}) collective-permute-start(bf16[1024,512]{1,0:T(8,128)(2,1)S(1)} %pad_maximum_fusion.2.k0_ref.v0_ref), channel_id=1, source_target_pairs={{0,3},{1,0},{2,1},{3,2},{4,7},{5,4},{6,5},{7,6},{8,11},{9,8},{10,9... | collective-permute-start | bytes 3145736 | tf_op jit(solution)/shard_map/ppermute | solution.py:208
  5.4 30.0 %collective-permute-start = (bf16[1024,512]{1,0:T(8,128)(2,1)S(1)}, bf16[1024,512]{1,0:T(8,128)(2,1)}, u32[]{:S(2)}, u32[]{:S(2)}) collective-permute-start(bf16[1024,512]{1,0:T(8,128)(2,1)S(1)} %pad_maximum_fusion.2.k0_ref.v0_ref), channel_id=1, source_target_pairs={{0,1},{1,2},{2,3},{3,0},{4,5},{5,6},{6,7},{7,4},{8,9},{9,10},{10,1... | collective-permute-start | bytes 3145736 | tf_op jit(solution)/shard_map/ppermute | solution.py:208
  9.1 30.3 %collective-permute-start.6 = (bf16[128,512]{1,0:T(8,128)(2,1)}, bf16[128,512]{1,0:T(8,128)(2,1)}, u32[]{:S(2)}, u32[]{:S(2)}) collective-permute-start(bf16[128,512]{1,0:T(8,128)(2,1)} %fusion.16), channel_id=1, source_target_pairs={{0,3},{4,7},{8,11},{12,15},{16,19},{20,23},{24,27},{28,31},{32,35}... | collective-permute-start | bytes 393224 | tf_op jit(solution)/shard_map/ppermute | solution.py:271
  14.4 25.0 %collective-permute-start.5 = (bf16[128,512]{1,0:T(8,128)(2,1)}, bf16[128,512]{1,0:T(8,128)(2,1)}, u32[]{:S(2)}, u32[]{:S(2)}) collective-permute-start(bf16[128,512]{1,0:T(8,128)(2,1)} %fusion.16), channel_id=1, source_target_pairs={{0,2},{1,3},{4,6},{5,7},{8,10},{9,11},{12,14},{13,15},{16,18},{17,... | collective-permute-start | bytes 393224 | tf_op jit(solution)/shard_map/ppermute | solution.py:271
  16.3 23.1 %collective-permute-start.4 = (bf16[128,512]{1,0:T(8,128)(2,1)}, bf16[128,512]{1,0:T(8,128)(2,1)}, u32[]{:S(2)}, u32[]{:S(2)}) collective-permute-start(bf16[128,512]{1,0:T(8,128)(2,1)} %fusion.16), channel_id=1, source_target_pairs={{0,1},{1,2},{2,3},{4,5},{5,6},{6,7},{8,9},{9,10},{10,11},{12,13},{... | collective-permute-start | bytes 393224 | tf_op jit(solution)/shard_map/ppermute | solution.py:271
  19.6 0.6 copy-start.5
  30.2 19.3 %collective-permute-start.3 = (bf16[512,512]{1,0:T(8,128)(2,1)}, bf16[512,512]{1,0:T(8,128)(2,1)S(1)}, u32[]{:S(2)}, u32[]{:S(2)}) collective-permute-start(bf16[512,512]{1,0:T(8,128)(2,1)} %slice.47), channel_id=1, source_target_pairs={{0,3},{1,0},{2,1},{3,2},{4,7},{5,4},{6,5},{7,6},{8,11},{9,8},{10,9... | collective-permute-start | bytes 1572872 | tf_op jit(solution)/shard_map/ppermute | solution.py:220
  36.5 11.9 %collective-permute-start.1 = (bf16[512,512]{1,0:T(8,128)(2,1)S(1)}, bf16[512,512]{1,0:T(8,128)(2,1)}, u32[]{:S(2)}, u32[]{:S(2)}) collective-permute-start(bf16[512,512]{1,0:T(8,128)(2,1)S(1)} %slice.46), channel_id=1, source_target_pairs={{0,1},{1,2},{2,3},{3,0},{4,5},{5,6},{6,7},{7,4},{8,9},{9,10},{10,1... | collective-permute-start | bytes 1572872 | tf_op jit(solution)/shard_map/ppermute | solution.py:219
  49.6 5.2 %copy-start.2 = (bf16[1024,512]{1,0:T(8,128)(2,1)}, bf16[1024,512]{1,0:T(8,128)(2,1)S(1)}, u32[]{:S(2)}) copy-start(bf16[1024,512]{1,0:T(8,128)(2,1)S(1)} %constant_dynamic-update-slice_fusion.k2_ref.v2_ref) | copy-start | bytes 3145732
  49.6 36.5 %collective-permute-start.8 = (bf16[3,1536,192]{1,2,0:T(8,128)(2,1)S(1)}, bf16[3,1536,192]{1,2,0:T(8,128)(2,1)}, u32[]{:S(2)}, u32[]{:S(2)}) collective-permute-start(bf16[3,1536,192]{1,2,0:T(8,128)(2,1)S(1)} %pad_maximum_fusion.1), channel_id=1, source_target_pairs={{0,3},{1,0},{2,1},{3,2},{4,7},{5,4},{6,5},{7,6},{8,11},{9,8},{10,9... | collective-permute-start | bytes 5308424 | tf_op jit(solution)/shard_map/ppermute | solution.py:208
  49.6 37.8 %collective-permute-start.7 = (bf16[3,1536,192]{1,2,0:T(8,128)(2,1)S(1)}, bf16[3,1536,192]{1,2,0:T(8,128)(2,1)}, u32[]{:S(2)}, u32[]{:S(2)}) collective-permute-start(bf16[3,1536,192]{1,2,0:T(8,128)(2,1)S(1)} %pad_maximum_fusion.1), channel_id=1, source_target_pairs={{0,1},{1,2},{2,3},{3,0},{4,5},{5,6},{6,7},{7,4},{8,9},{9,10},{10,1... | collective-permute-start | bytes 5308424 | tf_op jit(solution)/shard_map/ppermute | solution.py:208
  54.8 11.5 %copy-start.3 = (bf16[1,128,1536]{2,1,0:T(8,128)(2,1)S(1)}, bf16[1,128,1536]{2,1,0:T(8,128)(2,1)}, u32[]{:S(2)}) copy-start(bf16[1,128,1536]{2,1,0:T(8,128)(2,1)} %param.14) | copy-start | bytes 1179652
  66.3 3.4 %copy-start.6 = (f32[1536]{0:T(1024)S(1)}, f32[1536]{0:T(1024)}, u32[]{:S(2)}) copy-start(f32[1536]{0:T(1024)} %param.24) | copy-start | bytes 18436
  90.1 52.6 %all-to-all-start = ((bf16[32,32,1536]{2,1,0:T(8,128)(2,1)}), bf16[32,32,1536]{2,1,0:T(8,128)(2,1)}, u32[]{:S(2)}, u32[]{:S(2)}) async-start(bf16[32,32,1536]{2,1,0:T(8,128)(2,1)} %bitcast.31), calls=%async_computation | async-start | bytes 6291456 | tf_op jit(solution)/shard_map/all_to_all | solution.py:322
  105.4 21.1 %collective-permute-start.10 = (bf16[3,768,192]{1,2,0:T(8,128)(2,1)S(1)}, bf16[3,768,192]{1,2,0:T(8,128)(2,1)S(1)}, u32[]{:S(2)}, u32[]{:S(2)}) collective-permute-start(bf16[3,768,192]{1,2,0:T(8,128)(2,1)S(1)} %slice.38), channel_id=1, source_target_pairs={{0,3},{1,0},{2,1},{3,2},{4,7},{5,4},{6,5},{7,6},{8,11},{9,8},{10,9... | collective-permute-start | bytes 2654216 | tf_op jit(solution)/shard_map/ppermute | solution.py:220
  105.4 22.2 %collective-permute-start.9 = (bf16[3,768,192]{1,2,0:T(8,128)(2,1)S(1)}, bf16[3,768,192]{1,2,0:T(8,128)(2,1)S(1)}, u32[]{:S(2)}, u32[]{:S(2)}) collective-permute-start(bf16[3,768,192]{1,2,0:T(8,128)(2,1)S(1)} %slice.37), channel_id=1, source_target_pairs={{0,1},{1,2},{2,3},{3,0},{4,5},{5,6},{6,7},{7,4},{8,9},{9,10},{10,1... | collective-permute-start | bytes 2654216 | tf_op jit(solution)/shard_map/ppermute | solution.py:219
  161.5 45.0 %all-to-all-start.1 = ((bf16[32,32,1536]{2,1,0:T(8,128)(2,1)}), bf16[32,32,1536]{2,1,0:T(8,128)(2,1)}, u32[]{:S(2)}, u32[]{:S(2)}) async-start(bf16[32,32,1536]{2,1,0:T(8,128)(2,1)} %bitcast.116), calls=%async_computation.1 | async-start | bytes 6291456 | tf_op jit(solution)/shard_map/all_to_all | solution.py:337

commit v10 on v9

--- a/solution.py
+++ b/solution.py
@@ -298,12 +298,6 @@
         + jnp.dot(attended, out_proj, preferred_element_type=jnp.float32)
     ).astype(jnp.bfloat16)
     moe_in = normalize(mid_stream, moe_gain).astype(jnp.bfloat16)
-    moe_in, weights_below, weights_above = lax.optimization_barrier(
-        (moe_in, weights_below, weights_above)
-    )
-    all_weights = jnp.stack(
-        [stacked_weights, weights_below, ring_far(weights_below, weights_above, 1), weights_above]
-    )
     logits = jnp.dot(moe_in, router, preferred_element_type=jnp.float32)
     expert_count = router.shape[1]
     top_count = routes.shape[2]
@@ -319,6 +313,12 @@
     pick = targets[None, :] == jnp.arange(slot_count, dtype=jnp.int32)[:, None]
     pick_rows = jnp.any(pick.reshape(slot_count, own_count, top_count), axis=-1).astype(jnp.bfloat16)
     send_rows = jnp.dot(pick_rows, moe_in, preferred_element_type=jnp.float32).astype(jnp.bfloat16)
+    send_rows, weights_below, weights_above = lax.optimization_barrier(
+        (send_rows, weights_below, weights_above)
+    )
+    all_weights = jnp.stack(
+        [stacked_weights, weights_below, ring_far(weights_below, weights_above, 1), weights_above]
+    )
     grouped_rows = lax.all_to_all(
         send_rows.reshape(expert_count, capacity, model_width), "req", 0, 0, tiled=True
     )

time: 212 us -> 209 us (0.986)
  local copies, waits for them, and re-layouts: 18.4 us -> 15.6 us
    ppermute x2, waiting for transfers between devices: 1.3 us -> 14.1 us  [ring_neighbours(): lax.ppermute(shard, axis_name, up)]
    ppermute x2, waiting for transfers between devices: 23 us -> 10.2 us  [ring_neighbours(): lax.ppermute(shard, axis_name, down)]
  transfers between devices with their start and end apart: 13 -> 13, of which waited for: 8 -> 9; matrix products, arithmetic and copies ran while one was open for 18% -> 17% of each run, Pallas kernels for 5% -> 6%
where the time goes in v10:
time: 209 us; the launch traced here: 208 us
  waiting for transfers between devices  93.3 us (45%)
  starting transfers between devices  39 us (19%)
  matrix products  30.9 us (15%)
  other arithmetic  16.1 us (8%)
  local copies, waits for them, and re-layouts  15.6 us (7%)
  Pallas kernels  11.5 us (6%)
    all_to_all x1, waiting for transfers between devices, body(): lax.all_to_all(expert_out.reshape(-1, capacity, model_width), 'req', 0, 0...  34.7 us
    ppermute x2, waiting for transfers between devices, ring_far(): lax.ppermute(lax.slice_in_dim(from_above, half, extent, axis=split_axis),...  20 us
    ppermute x2, waiting for transfers between devices, ring_neighbours(): lax.ppermute(shard, axis_name, up)  14.1 us
    all_to_all x1, starting transfers between devices, body(): lax.all_to_all(send_rows.reshape(expert_count, capacity, model_width), 'r...  14.1 us
    dot_general x1, matrix products, body(): jnp.einsum('hnf,hdf->hnd', activation, all_weights[:, 2], preferred_eleme...  12 us
    pallas_call x1, Pallas kernels, attention(): pl.pallas_call(functools.partial(attention_kernel, token_count), out_shap...  11.5 us
    ppermute x2, waiting for transfers between devices, ring_neighbours(): lax.ppermute(shard, axis_name, down)  10.2 us
    ppermute x3, starting transfers between devices, body(): received.append(lax.ppermute(new_kv, 'hid', pairs))  8.39 us
  transfers between devices with their start and end apart: 13, of which 9 were waited for; matrix products, arithmetic and copies ran while one was open for 17% of the time, Pallas kernels for 6%

profile of v10, /device:TPU:1, one launch (start us, length us, event | category | flops | bytes accessed | tf_op | source)
XLA Modules:
  0.0 208.0 jit_solution(9126019689210074345)
XLA Ops:
  0.7 1.4 pad_maximum_fusion.2.k0_ref.v0_ref
  2.1 2.1 %collective-permute-start = (bf16[1024,512]{1,0:T(8,128)(2,1)S(1)}, bf16[1024,512]{1,0:T(8,128)(2,1)S(1)}, u32[]{:S(2)}, u32[]{:S(2)}) collective-permute-start(bf16[1024,512]{1,0:T(8,128)(2,1)S(1)} %pad_maximum_fusion.2.k0_ref.v0_ref), channel_id=1, source_target_pairs={{0,1},{1,2},{2,3},{3,0},{4,5},{5,6},{6,7},{7,4},{8,9},{9,10},{10,1... | collective-permute-start | bytes 3145736 | tf_op jit(solution)/shard_map/ppermute | solution.py:208
  4.2 1.3 collective-permute-start.2
  6.7 1.9 fusion.16
  8.7 3.9 %collective-permute-start.6 = (bf16[128,512]{1,0:T(8,128)(2,1)S(1)}, bf16[128,512]{1,0:T(8,128)(2,1)}, u32[]{:S(2)}, u32[]{:S(2)}) collective-permute-start(bf16[128,512]{1,0:T(8,128)(2,1)S(1)} %fusion.16), channel_id=1, source_target_pairs={{0,3},{4,7},{8,11},{12,15},{16,19},{20,23},{24,27},{28,31},{32,35}... | collective-permute-start | bytes 393224 | tf_op jit(solution)/shard_map/ppermute | solution.py:271
  12.6 1.9 collective-permute-start.5
  14.5 2.5 %collective-permute-start.4 = (bf16[128,512]{1,0:T(8,128)(2,1)S(1)}, bf16[128,512]{1,0:T(8,128)(2,1)}, u32[]{:S(2)}, u32[]{:S(2)}) collective-permute-start(bf16[128,512]{1,0:T(8,128)(2,1)S(1)} %fusion.16), channel_id=1, source_target_pairs={{0,1},{1,2},{2,3},{4,5},{5,6},{6,7},{8,9},{9,10},{10,11},{12,13},{... | collective-permute-start | bytes 393224 | tf_op jit(solution)/shard_map/ppermute | solution.py:271
  17.0 10.9 %collective-permute-done.k1_ref.v1_ref = bf16[1024,512]{1,0:T(8,128)(2,1)S(1)} collective-permute-done((bf16[1024,512]{1,0:T(8,128)(2,1)S(1)}, bf16[1024,512]{1,0:T(8,128)(2,1)S(1)}, u32[]{:S(2)}, u32[]{:S(2)}) %collective-permute-start) | collective-permute-done | bytes 1048608 | tf_op jit(solution)/shard_map/ppermute | solution.py:208
  29.4 1.4 pad_maximum_fusion.1
  30.8 2.0 slice.47
  32.9 2.3 %collective-permute-start.3 = (bf16[512,512]{1,0:T(8,128)(2,1)}, bf16[512,512]{1,0:T(8,128)(2,1)}, u32[]{:S(2)}, u32[]{:S(2)}) collective-permute-start(bf16[512,512]{1,0:T(8,128)(2,1)} %slice.47), channel_id=1, source_target_pairs={{0,3},{1,0},{2,1},{3,2},{4,7},{5,4},{6,5},{7,6},{8,11},{9,8},{10,9... | collective-permute-start | bytes 1572872 | tf_op jit(solution)/shard_map/ppermute | solution.py:220
  38.8 3.7 %collective-permute-done.1 = bf16[512,512]{1,0:T(8,128)(2,1)S(1)} collective-permute-done((bf16[512,512]{1,0:T(8,128)(2,1)S(1)}, bf16[512,512]{1,0:T(8,128)(2,1)S(1)}, u32[]{:S(2)}, u32[]{:S(2)}) %collective-permute-start.1) | collective-permute-done | bytes 524320 | tf_op jit(solution)/shard_map/ppermute | solution.py:219
  45.3 3.4 %collective-permute-start.8 = (bf16[3,1536,192]{1,2,0:T(8,128)(2,1)S(1)}, bf16[3,1536,192]{1,2,0:T(8,128)(2,1)}, u32[]{:S(2)}, u32[]{:S(2)}) collective-permute-start(bf16[3,1536,192]{1,2,0:T(8,128)(2,1)S(1)} %copy-done.2), channel_id=1, source_target_pairs={{0,3},{1,0},{2,1},{3,2},{4,7},{5,4},{6,5},{7,6},{8,11},{9,8},{10,9... | collective-permute-start | bytes 5308424 | tf_op jit(solution)/shard_map/ppermute | solution.py:208
  53.3 11.5 %shard_map.157 = bf16[2,768,128]{2,1,0:T(8,128)(2,1)} custom-call(s32[2]{0:T(128)} %pad_add_fusion.scalars, bf16[2,768,128]{2,1,0:T(8,128)(2,1)} %bitcast.115, bf16[1024,512]{1,0:T(8,128)(2,1)} %copy-done.1, bf16[1024,512]{1,0:T(8,128)(2,1)} %copy-done.3, bf16[1024,512]{1,0:T(8,128)(2,1)} %copy-done.4, ...), custom_call_target="tpu_custom_call" | custom-call | tf_op jit(solution)/shard_map/pallas_call | solution.py:185
  66.1 3.3 %multiply_reduce_fusion = (f32[128]{0:T(128)S(1)}, f32[128,1536]{1,0:T(8,128)S(1)}) fusion(bf16[128,1536]{0,1:T(8,128)(2,1)S(1)} %bitcast.117, bf16[1536,1536]{1,0:T(8,128)(2,1)} %param.23, bf16[1,128,1536]{2,1,0:T(8,128)(2,1)S(1)} %copy-done.5), kind=kOutput, calls=%fused_computation.37 | convolution fusion | flops 605159296 | bytes 6291968 | tf_op jit(solution)/shard_map/dot_general | solution.py:298
  69.4 2.8 %convolution_convert_fusion.1 = bf16[1024,1536]{1,0:T(8,128)(2,1)} fusion(pred[1024,128]{1,0:T(8,128)(4,1)S(1)} %copy-done.8, f32[128,1536]{1,0:T(8,128)S(1)} %get-tuple-element.20, f32[1536]{0:T(1024)S(1)} %copy-done.12, f32[128]{0:T(128)S(1)} %add_rsqrt_fusion), kind=kOutput, calls=%fused_computation.3 | convolution fusion | flops 404815872 | bytes 4069888 | tf_op jit(solution)/shard_map/dot_general | solution.py:315
  72.2 10.2 %collective-permute-done.8 = bf16[3,1536,192]{1,2,0:T(8,128)(2,1)} collective-permute-done((bf16[3,1536,192]{1,2,0:T(8,128)(2,1)S(1)}, bf16[3,1536,192]{1,2,0:T(8,128)(2,1)}, u32[]{:S(2)}, u32[]{:S(2)}) %collective-permute-start.8) | collective-permute-done | bytes 1769504 | tf_op jit(solution)/shard_map/ppermute | solution.py:208
  82.4 3.2 %collective-permute-done.7 = bf16[3,1536,192]{1,2,0:T(8,128)(2,1)} collective-permute-done((bf16[3,1536,192]{1,2,0:T(8,128)(2,1)S(1)}, bf16[3,1536,192]{1,2,0:T(8,128)(2,1)}, u32[]{:S(2)}, u32[]{:S(2)}) %collective-permute-start.7) | collective-permute-done | bytes 1769504 | tf_op jit(solution)/shard_map/ppermute | solution.py:208
  85.6 14.1 %all-to-all-start = ((bf16[32,32,1536]{2,1,0:T(8,128)(2,1)}), bf16[32,32,1536]{2,1,0:T(8,128)(2,1)}, u32[]{:S(2)}, u32[]{:S(2)}) async-start(bf16[32,32,1536]{2,1,0:T(8,128)(2,1)} %bitcast.31), calls=%async_computation | async-start | bytes 6291456 | tf_op jit(solution)/shard_map/all_to_all | solution.py:322
  99.7 1.2 slice.37
  100.9 1.2 slice.38
  102.1 1.8 collective-permute-start.10
  103.9 19.3 %collective-permute-done.10 = bf16[3,768,192]{1,2,0:T(8,128)(2,1)S(1)} collective-permute-done((bf16[3,768,192]{1,2,0:T(8,128)(2,1)S(1)}, bf16[3,768,192]{1,2,0:T(8,128)(2,1)S(1)}, u32[]{:S(2)}, u32[]{:S(2)}) %collective-permute-start.10) | collective-permute-done | bytes 884768 | tf_op jit(solution)/shard_map/ppermute | solution.py:220
  123.2 2.6 %collective-permute-done.9 = bf16[3,768,192]{1,2,0:T(8,128)(2,1)S(1)} collective-permute-done((bf16[3,768,192]{1,2,0:T(8,128)(2,1)S(1)}, bf16[3,768,192]{1,2,0:T(8,128)(2,1)S(1)}, u32[]{:S(2)}, u32[]{:S(2)}) %collective-permute-start.9) | collective-permute-done | bytes 884768 | tf_op jit(solution)/shard_map/ppermute | solution.py:219
  126.0 5.5 %pad_maximum_fusion = bf16[4,3,1536,192]{2,3,0,1:T(8,128)(2,1)} fusion(bf16[1,3,1536,192]{2,3,0,1:T(8,128)(2,1)} %bitcast.29, bf16[1,3,1536,192]{2,3,0,1:T(8,128)(2,1)S(1)} %maximum_bitcast_fusion, bf16[1,3,1536,192]{2,3,0,1:T(8,128)(2,1)} %bitcast.26, bf16[1,3,1536,192]{2,3,0,1:T(8,128)(2,1)S(1)} %bitcast.113), kind=kLoop, calls=%fused_computation.2 | loop fusion | flops 10616832 | bytes 14155776 | tf_op jit(solution)/shard_map/stack | solution.py:319
  131.6 7.9 %all-to-all-done = bf16[32,32,1536]{2,1,0:T(8,128)(2,1)} async-done(((bf16[32,32,1536]{2,1,0:T(8,128)(2,1)}), bf16[32,32,1536]{2,1,0:T(8,128)(2,1)}, u32[]{:S(2)}, u32[]{:S(2)}) %all-to-all-start) | async-done | bytes 3145760 | tf_op jit(solution)/shard_map/all_to_all | solution.py:322
  139.5 6.9 %fusion.4 = f32[4,192,1024]{2,1,0:T(8,128)} fusion(bf16[1024,1536,1]{1,0,2:T(8,128)(2,1)} %bitcast.33, bf16[4,3,1536,192]{2,3,0,1:T(8,128)(2,1)} %pad_maximum_fusion), kind=kOutput, calls=%fused_computation.14 | convolution fusion | flops 2415919104 | bytes 8650752 | tf_op jit(solution)/shard_map/nd,hdf->hnf/dot_general | solution.py:326
  146.3 12.0 %fusion = bf16[1024,1536]{1,0:T(8,128)(2,1)} fusion(bf16[4,3,1536,192]{2,3,0,1:T(8,128)(2,1)} %pad_maximum_fusion, f32[4,192,1024]{2,1,0:T(8,128)} %fusion.4, bf16[1024,1536,1]{1,0,2:T(8,128)(2,1)} %bitcast.33), kind=kOutput, calls=%fused_computation.6 | convolution fusion | flops 4845207552 | bytes 14155776 | tf_op jit(solution)/shard_map/hnf,hdf->hnd/dot_general | solution.py:333
  158.3 5.2 %all-to-all-start.1 = ((bf16[32,32,1536]{2,1,0:T(8,128)(2,1)}), bf16[32,32,1536]{2,1,0:T(8,128)(2,1)}, u32[]{:S(2)}, u32[]{:S(2)}) async-start(bf16[32,32,1536]{2,1,0:T(8,128)(2,1)} %bitcast.114), calls=%async_computation.1 | async-start | bytes 6291456 | tf_op jit(solution)/shard_map/all_to_all | solution.py:337
  164.7 3.8 %gather_fusion = f32[512]{0:T(512)S(1)} fusion(f32[128,32]{0,1:T(8,128)S(1)} %fusion.37, s32[512]{0:T(512)S(1)} %reshape.190), kind=kCustom, calls=%fused_computation | custom fusion | bytes 8192 | tf_op jit(solution)/shard_map/jit(take_along_axis)/gather | solution.py:345
  168.7 34.7 %all-to-all-done.1 = bf16[32,32,1536]{2,1,0:T(8,128)(2,1)} async-done(((bf16[32,32,1536]{2,1,0:T(8,128)(2,1)}), bf16[32,32,1536]{2,1,0:T(8,128)(2,1)}, u32[]{:S(2)}, u32[]{:S(2)}) %all-to-all-start.1) | async-done | bytes 3145760 | tf_op jit(solution)/shard_map/all_to_all | solution.py:337
  203.4 3.8 %fusion.8 = f32[128,1536]{1,0:T(8,128)S(1)} fusion(bf16[1024,1536,1]{1,0,2:T(8,128)(2,1)} %bitcast.39, f32[128,4]{0,1:T(4,128)S(1)} %multiply_divide_fusion, s32[128,4]{0,1:T(4,128)S(1)} %fusion.34), kind=kOutput, calls=%fused_computation.21 | convolution fusion | flops 1612513280 | bytes 3936256 | tf_op jit(solution)/shard_map/dot_general | solution.py:340
  (70 shorter events, 16.6 us)
Async XLA Ops:
  0.6 163.8 %copy-start = (bf16[1536,32]{0,1:T(8,128)(2,1)S(1)}, bf16[1536,32]{0,1:T(8,128)(2,1)}, u32[]{:S(2)}) copy-start(bf16[1536,32]{0,1:T(8,128)(2,1)} %param.25) | copy-start | bytes 294916
  0.6 28.8 %copy-start.6 = (bf16[1,2,1536,192]{2,3,1,0:T(8,128)(2,1)S(1)}, bf16[1,2,1536,192]{2,3,1,0:T(8,128)(2,1)}, u32[]{:S(2)}) copy-start(bf16[1,2,1536,192]{2,3,1,0:T(8,128)(2,1)} %param.26) | copy-start | bytes 3538948
  0.7 28.8 %copy-start.7 = (bf16[1,192,1536]{2,1,0:T(8,128)(2,1)S(1)}, bf16[1,192,1536]{2,1,0:T(8,128)(2,1)}, u32[]{:S(2)}) copy-start(bf16[1,192,1536]{2,1,0:T(8,128)(2,1)} %param.27) | copy-start | bytes 1769476
  2.1 28.7 %copy-start.1 = (bf16[1024,512]{1,0:T(8,128)(2,1)}, bf16[1024,512]{1,0:T(8,128)(2,1)S(1)}, u32[]{:S(2)}) copy-start(bf16[1024,512]{1,0:T(8,128)(2,1)S(1)} %pad_maximum_fusion.2.k0_ref.v0_ref) | copy-start | bytes 3145732
  2.1 25.9 %collective-permute-start = (bf16[1024,512]{1,0:T(8,128)(2,1)S(1)}, bf16[1024,512]{1,0:T(8,128)(2,1)S(1)}, u32[]{:S(2)}, u32[]{:S(2)}) collective-permute-start(bf16[1024,512]{1,0:T(8,128)(2,1)S(1)} %pad_maximum_fusion.2.k0_ref.v0_ref), channel_id=1, source_target_pairs={{0,1},{1,2},{2,3},{3,0},{4,5},{5,6},{6,7},{7,4},{8,9},{9,10},{10,1... | collective-permute-start | bytes 3145736 | tf_op jit(solution)/shard_map/ppermute | solution.py:208
  4.2 26.6 %collective-permute-start.2 = (bf16[1024,512]{1,0:T(8,128)(2,1)S(1)}, bf16[1024,512]{1,0:T(8,128)(2,1)}, u32[]{:S(2)}, u32[]{:S(2)}) collective-permute-start(bf16[1024,512]{1,0:T(8,128)(2,1)S(1)} %pad_maximum_fusion.2.k0_ref.v0_ref), channel_id=1, source_target_pairs={{0,3},{1,0},{2,1},{3,2},{4,7},{5,4},{6,5},{7,6},{8,11},{9,8},{10,9... | collective-permute-start | bytes 3145736 | tf_op jit(solution)/shard_map/ppermute | solution.py:208
  8.6 56.2 %copy-start.9 = (bf16[128,512]{1,0:T(8,128)(2,1)}, bf16[128,512]{1,0:T(8,128)(2,1)S(1)}, u32[]{:S(2)}) copy-start(bf16[128,512]{1,0:T(8,128)(2,1)S(1)} %fusion.16) | copy-start | bytes 393220
  8.7 28.2 %collective-permute-start.6 = (bf16[128,512]{1,0:T(8,128)(2,1)S(1)}, bf16[128,512]{1,0:T(8,128)(2,1)}, u32[]{:S(2)}, u32[]{:S(2)}) collective-permute-start(bf16[128,512]{1,0:T(8,128)(2,1)S(1)} %fusion.16), channel_id=1, source_target_pairs={{0,3},{4,7},{8,11},{12,15},{16,19},{20,23},{24,27},{28,31},{32,35}... | collective-permute-start | bytes 393224 | tf_op jit(solution)/shard_map/ppermute | solution.py:271
  12.6 24.2 %collective-permute-start.5 = (bf16[128,512]{1,0:T(8,128)(2,1)S(1)}, bf16[128,512]{1,0:T(8,128)(2,1)}, u32[]{:S(2)}, u32[]{:S(2)}) collective-permute-start(bf16[128,512]{1,0:T(8,128)(2,1)S(1)} %fusion.16), channel_id=1, source_target_pairs={{0,2},{1,3},{4,6},{5,7},{8,10},{9,11},{12,14},{13,15},{16,18},{17,... | collective-permute-start | bytes 393224 | tf_op jit(solution)/shard_map/ppermute | solution.py:271
  14.5 22.3 %collective-permute-start.4 = (bf16[128,512]{1,0:T(8,128)(2,1)S(1)}, bf16[128,512]{1,0:T(8,128)(2,1)}, u32[]{:S(2)}, u32[]{:S(2)}) collective-permute-start(bf16[128,512]{1,0:T(8,128)(2,1)S(1)} %fusion.16), channel_id=1, source_target_pairs={{0,1},{1,2},{2,3},{4,5},{5,6},{6,7},{8,9},{9,10},{10,11},{12,13},{... | collective-permute-start | bytes 393224 | tf_op jit(solution)/shard_map/ppermute | solution.py:271
  28.0 1.0 copy-start.3
  29.0 13.5 %collective-permute-start.1 = (bf16[512,512]{1,0:T(8,128)(2,1)S(1)}, bf16[512,512]{1,0:T(8,128)(2,1)S(1)}, u32[]{:S(2)}, u32[]{:S(2)}) collective-permute-start(bf16[512,512]{1,0:T(8,128)(2,1)S(1)} %slice.46), channel_id=1, source_target_pairs={{0,1},{1,2},{2,3},{3,0},{4,5},{5,6},{6,7},{7,4},{8,9},{9,10},{10,1... | collective-permute-start | bytes 1572872 | tf_op jit(solution)/shard_map/ppermute | solution.py:219
  30.8 19.7 %copy-start.11 = (bf16[1,128,1536]{2,1,0:T(8,128)(2,1)S(1)}, bf16[1,128,1536]{2,1,0:T(8,128)(2,1)}, u32[]{:S(2)}) copy-start(bf16[1,128,1536]{2,1,0:T(8,128)(2,1)} %param.15) | copy-start | bytes 1179652
  30.8 14.5 %copy-start.2 = (bf16[3,1536,192]{1,2,0:T(8,128)(2,1)S(1)}, bf16[3,1536,192]{1,2,0:T(8,128)(2,1)}, u32[]{:S(2)}) copy-start(bf16[3,1536,192]{1,2,0:T(8,128)(2,1)} %pad_maximum_fusion.1) | copy-start | bytes 5308420
  32.9 10.4 %collective-permute-start.3 = (bf16[512,512]{1,0:T(8,128)(2,1)}, bf16[512,512]{1,0:T(8,128)(2,1)}, u32[]{:S(2)}, u32[]{:S(2)}) collective-permute-start(bf16[512,512]{1,0:T(8,128)(2,1)} %slice.47), channel_id=1, source_target_pairs={{0,3},{1,0},{2,1},{3,2},{4,7},{5,4},{6,5},{7,6},{8,11},{9,8},{10,9... | collective-permute-start | bytes 1572872 | tf_op jit(solution)/shard_map/ppermute | solution.py:220
  44.3 1.0 copy-start.4
  45.3 37.0 %collective-permute-start.8 = (bf16[3,1536,192]{1,2,0:T(8,128)(2,1)S(1)}, bf16[3,1536,192]{1,2,0:T(8,128)(2,1)}, u32[]{:S(2)}, u32[]{:S(2)}) collective-permute-start(bf16[3,1536,192]{1,2,0:T(8,128)(2,1)S(1)} %copy-done.2), channel_id=1, source_target_pairs={{0,3},{1,0},{2,1},{3,2},{4,7},{5,4},{6,5},{7,6},{8,11},{9,8},{10,9... | collective-permute-start | bytes 5308424 | tf_op jit(solution)/shard_map/ppermute | solution.py:208
  48.8 36.8 %collective-permute-start.7 = (bf16[3,1536,192]{1,2,0:T(8,128)(2,1)S(1)}, bf16[3,1536,192]{1,2,0:T(8,128)(2,1)}, u32[]{:S(2)}, u32[]{:S(2)}) collective-permute-start(bf16[3,1536,192]{1,2,0:T(8,128)(2,1)S(1)} %copy-done.2), channel_id=1, source_target_pairs={{0,1},{1,2},{2,3},{3,0},{4,5},{5,6},{6,7},{7,4},{8,9},{9,10},{10,1... | collective-permute-start | bytes 5308424 | tf_op jit(solution)/shard_map/ppermute | solution.py:208
  53.3 12.7 %copy-start.5 = (bf16[1,128,1536]{2,1,0:T(8,128)(2,1)S(1)}, bf16[1,128,1536]{2,1,0:T(8,128)(2,1)}, u32[]{:S(2)}) copy-start(bf16[1,128,1536]{2,1,0:T(8,128)(2,1)} %param.14) | copy-start | bytes 1179652
  66.0 3.3 %copy-start.8 = (pred[1024,128]{1,0:T(8,128)(4,1)S(1)}, pred[1024,128]{1,0:T(8,128)(4,1)}, u32[]{:S(2)}) copy-start(pred[1024,128]{1,0:T(8,128)(4,1)} %fusion.7) | copy-start | bytes 393220
  66.1 3.3 %copy-start.12 = (f32[1536]{0:T(1024)S(1)}, f32[1536]{0:T(1024)}, u32[]{:S(2)}) copy-start(f32[1536]{0:T(1024)} %param.24) | copy-start | bytes 18436
  85.6 53.9 %all-to-all-start = ((bf16[32,32,1536]{2,1,0:T(8,128)(2,1)}), bf16[32,32,1536]{2,1,0:T(8,128)(2,1)}, u32[]{:S(2)}, u32[]{:S(2)}) async-start(bf16[32,32,1536]{2,1,0:T(8,128)(2,1)} %bitcast.31), calls=%async_computation | async-start | bytes 6291456 | tf_op jit(solution)/shard_map/all_to_all | solution.py:322
  102.1 21.1 %collective-permute-start.10 = (bf16[3,768,192]{1,2,0:T(8,128)(2,1)S(1)}, bf16[3,768,192]{1,2,0:T(8,128)(2,1)S(1)}, u32[]{:S(2)}, u32[]{:S(2)}) collective-permute-start(bf16[3,768,192]{1,2,0:T(8,128)(2,1)S(1)} %slice.38), channel_id=1, source_target_pairs={{0,3},{1,0},{2,1},{3,2},{4,7},{5,4},{6,5},{7,6},{8,11},{9,8},{10,9... | collective-permute-start | bytes 2654216 | tf_op jit(solution)/shard_map/ppermute | solution.py:220
  103.9 21.9 %collective-permute-start.9 = (bf16[3,768,192]{1,2,0:T(8,128)(2,1)S(1)}, bf16[3,768,192]{1,2,0:T(8,128)(2,1)S(1)}, u32[]{:S(2)}, u32[]{:S(2)}) collective-permute-start(bf16[3,768,192]{1,2,0:T(8,128)(2,1)S(1)} %slice.37), channel_id=1, source_target_pairs={{0,1},{1,2},{2,3},{3,0},{4,5},{5,6},{6,7},{7,4},{8,9},{9,10},{10,1... | collective-permute-start | bytes 2654216 | tf_op jit(solution)/shard_map/ppermute | solution.py:219
  158.3 5.4 %copy-start.10 = (bf16[128,512]{1,0:T(8,128)(2,1)S(1)}, bf16[128,512]{1,0:T(8,128)(2,1)}, u32[]{:S(2)}) copy-start(bf16[128,512]{1,0:T(8,128)(2,1)} %copy-done.9) | copy-start | bytes 393220
  158.3 45.1 %all-to-all-start.1 = ((bf16[32,32,1536]{2,1,0:T(8,128)(2,1)}), bf16[32,32,1536]{2,1,0:T(8,128)(2,1)}, u32[]{:S(2)}, u32[]{:S(2)}) async-start(bf16[32,32,1536]{2,1,0:T(8,128)(2,1)} %bitcast.114), calls=%async_computation.1 | async-start | bytes 6291456 | tf_op jit(solution)/shard_map/all_to_all | solution.py:337

commit v11 on v10

--- a/solution.py
+++ b/solution.py
@@ -280,7 +280,7 @@
     stacked_weights, _, _ = lax.optimization_barrier(
         (jnp.concatenate([gate_up[0], down_proj[0].T[None]], axis=0), shifted_kv[2], new_parts)
     )
-    weights_below, weights_above = ring_neighbours(stacked_weights)
+    weights_below, weights_above = ring_neighbours(stacked_weights[:2])
     grouped = (
         queries[0]
         .reshape(own_count, KVH, group_size, HD)
@@ -316,8 +316,15 @@
     send_rows, weights_below, weights_above = lax.optimization_barrier(
         (send_rows, weights_below, weights_above)
     )
+    shifted_down = ring_gather(stacked_weights[2:], 1)
+    shifted_gate_up = [
+        stacked_weights[:2],
+        weights_below,
+        ring_far(weights_below, weights_above, 1),
+        weights_above,
+    ]
     all_weights = jnp.stack(
-        [stacked_weights, weights_below, ring_far(weights_below, weights_above, 1), weights_above]
+        [jnp.concatenate([both, down], axis=0) for both, down in zip(shifted_gate_up, shifted_down)]
     )
     grouped_rows = lax.all_to_all(
         send_rows.reshape(expert_count, capacity, model_width), "req", 0, 0, tiled=True

time: 209 us -> 209 us (level)
  waiting for transfers between devices: 93.3 us -> 69.1 us
  starting transfers between devices: 39 us -> 55.7 us
  Pallas kernels: 11.5 us -> 15.4 us
  local copies, waits for them, and re-layouts: 15.6 us -> 18 us
    ppermute x2 -> x3, waiting for transfers between devices: 14.1 us -> 0.01 us  [ring_neighbours(): lax.ppermute(shard, axis_name, up)]
    all_to_all x1, waiting for transfers between devices: 7.92 us -> 0.01 us  [body(): lax.all_to_all(send_rows.reshape(expert_count, capacity, model_width), 'r...]
    ppermute x2 -> x3, waiting for transfers between devices: 20 us -> 12.4 us  [ring_far(): lax.ppermute(lax.slice_in_dim(from_above, half, extent, axis=split_axis),...]
    ppermute x2 -> x3, starting transfers between devices: 4.07 us -> 11.5 us  [ring_far(): lax.ppermute(lax.slice_in_dim(from_above, half, extent, axis=split_axis),...]
    ppermute x2 -> x3, waiting for transfers between devices: 6.3 us -> 10.2 us  [ring_far(): lax.ppermute(lax.slice_in_dim(from_below, 0, half, axis=split_axis), axis...]
    pallas_call x1, Pallas kernels: 11.5 us -> 15.4 us  [attention(): pl.pallas_call(functools.partial(attention_kernel, token_count), out_shap...]
    ppermute x2 -> x3, starting transfers between devices: 4.76 us -> 8.12 us  [ring_neighbours(): lax.ppermute(shard, axis_name, down)]
    all_to_all x1, starting transfers between devices: 5.18 us -> 8.38 us  [body(): lax.all_to_all(expert_out.reshape(-1, capacity, model_width), 'req', 0, 0...]
  transfers between devices with their start and end apart: 13 -> 17, of which waited for: 9 -> 6; matrix products, arithmetic and copies ran while one was open for 17% -> 19% of each run, Pallas kernels for 6% -> 7%
where the time goes in v11:
time: 209 us; the launch traced here: 208 us
  waiting for transfers between devices  69.1 us (33%)
  starting transfers between devices  55.7 us (27%)
  matrix products  31.6 us (15%)
  local copies, waits for them, and re-layouts  18 us (9%)
  other arithmetic  16.3 us (8%)
  Pallas kernels  15.4 us (7%)
    all_to_all x1, waiting for transfers between devices, body(): lax.all_to_all(expert_out.reshape(-1, capacity, model_width), 'req', 0, 0...  33.7 us
    all_to_all x1, starting transfers between devices, body(): lax.all_to_all(send_rows.reshape(expert_count, capacity, model_width), 'r...  16.4 us
    pallas_call x1, Pallas kernels, attention(): pl.pallas_call(functools.partial(attention_kernel, token_count), out_shap...  15.4 us
    ppermute x3, waiting for transfers between devices, ring_neighbours(): lax.ppermute(shard, axis_name, down)  12.8 us
    ppermute x3, waiting for transfers between devices, ring_far(): lax.ppermute(lax.slice_in_dim(from_above, half, extent, axis=split_axis),...  12.4 us
    dot_general x1, matrix products, body(): jnp.einsum('hnf,hdf->hnd', activation, all_weights[:, 2], preferred_eleme...  12 us
    ppermute x3, starting transfers between devices, ring_far(): lax.ppermute(lax.slice_in_dim(from_above, half, extent, axis=split_axis),...  11.5 us
    ppermute x3, waiting for transfers between devices, ring_far(): lax.ppermute(lax.slice_in_dim(from_below, 0, half, axis=split_axis), axis...  10.2 us
  transfers between devices with their start and end apart: 17, of which 6 were waited for; matrix products, arithmetic and copies ran while one was open for 19% of the time, Pallas kernels for 7%

profile of v11, /device:TPU:1, one launch (start us, length us, event | category | flops | bytes accessed | tf_op | source)
XLA Modules:
  0.0 207.7 jit_solution(13487509167842443424)
XLA Ops:
  2.0 3.4 %collective-permute-start.2 = (bf16[1024,512]{1,0:T(8,128)(2,1)S(1)}, bf16[1024,512]{1,0:T(8,128)(2,1)}, u32[]{:S(2)}, u32[]{:S(2)}) collective-permute-start(bf16[1024,512]{1,0:T(8,128)(2,1)S(1)} %pad_maximum_fusion.2.k0_ref.v0_ref), channel_id=1, source_target_pairs={{0,3},{1,0},{2,1},{3,2},{4,7},{5,4},{6,5},{7,6},{8,11},{9,8},{10,9... | collective-permute-start | bytes 3145736 | tf_op jit(solution)/shard_map/ppermute | solution.py:208
  6.5 2.6 %fusion.16 = bf16[128,512]{1,0:T(8,128)(2,1)} fusion(bf16[1536,256]{1,0:T(8,128)(2,1)} %param.22, bf16[1536,256]{1,0:T(8,128)(2,1)} %param.21, bf16[1,128,1536]{2,1,0:T(8,128)(2,1)} %param.14, f32[1536]{0:T(1024)} %param.20, f32[128]{0:T(128)S(1)} %add_rsqrt_fusion.1), kind=kOutput, calls=%fused_computation.31 | convolution fusion | flops 205324288 | bytes 2103808 | tf_op jit(solution)/shard_map/dot_general | solution.py:260
  9.1 5.2 %collective-permute-start.6 = (bf16[128,512]{1,0:T(8,128)(2,1)}, bf16[128,512]{1,0:T(8,128)(2,1)}, u32[]{:S(2)}, u32[]{:S(2)}) collective-permute-start(bf16[128,512]{1,0:T(8,128)(2,1)} %fusion.16), channel_id=1, source_target_pairs={{0,3},{4,7},{8,11},{12,15},{16,19},{20,23},{24,27},{28,31},{32,35}... | collective-permute-start | bytes 393224 | tf_op jit(solution)/shard_map/ppermute | solution.py:271
  14.4 1.9 collective-permute-start.5
  16.3 2.5 %collective-permute-start.4 = (bf16[128,512]{1,0:T(8,128)(2,1)}, bf16[128,512]{1,0:T(8,128)(2,1)}, u32[]{:S(2)}, u32[]{:S(2)}) collective-permute-start(bf16[128,512]{1,0:T(8,128)(2,1)} %fusion.16), channel_id=1, source_target_pairs={{0,1},{1,2},{2,3},{4,5},{5,6},{6,7},{8,9},{9,10},{10,11},{12,13},{... | collective-permute-start | bytes 393224 | tf_op jit(solution)/shard_map/ppermute | solution.py:271
  21.5 1.4 pad_maximum_fusion.1
  23.0 5.4 %collective-permute-done.2.k3_ref.v3_ref = bf16[1024,512]{1,0:T(8,128)(2,1)} collective-permute-done((bf16[1024,512]{1,0:T(8,128)(2,1)S(1)}, bf16[1024,512]{1,0:T(8,128)(2,1)}, u32[]{:S(2)}, u32[]{:S(2)}) %collective-permute-start.2) | collective-permute-done | bytes 1048608 | tf_op jit(solution)/shard_map/ppermute | solution.py:208
  28.4 1.9 slice.65
  30.2 5.2 %collective-permute-start.3 = (bf16[512,512]{1,0:T(8,128)(2,1)}, bf16[512,512]{1,0:T(8,128)(2,1)S(1)}, u32[]{:S(2)}, u32[]{:S(2)}) collective-permute-start(bf16[512,512]{1,0:T(8,128)(2,1)} %slice.65), channel_id=1, source_target_pairs={{0,3},{1,0},{2,1},{3,2},{4,7},{5,4},{6,5},{7,6},{8,11},{9,8},{10,9... | collective-permute-start | bytes 1572872 | tf_op jit(solution)/shard_map/ppermute | solution.py:220
  41.5 7.0 %collective-permute-done.1 = bf16[512,512]{1,0:T(8,128)(2,1)} collective-permute-done((bf16[512,512]{1,0:T(8,128)(2,1)S(1)}, bf16[512,512]{1,0:T(8,128)(2,1)}, u32[]{:S(2)}, u32[]{:S(2)}) %collective-permute-start.1) | collective-permute-done | bytes 524320 | tf_op jit(solution)/shard_map/ppermute | solution.py:219
  50.8 1.5 collective-permute-start.7
  53.2 15.4 %shard_map.157 = bf16[2,768,128]{2,1,0:T(8,128)(2,1)} custom-call(s32[2]{0:T(128)} %pad_add_fusion.scalars, bf16[2,768,128]{2,1,0:T(8,128)(2,1)} %bitcast.118, bf16[1024,512]{1,0:T(8,128)(2,1)} %copy-done.1, bf16[1024,512]{1,0:T(8,128)(2,1)} %collective-permute-done.k1_ref.v1_ref, bf16[1024,512]{1,0:T(8,128)(2,1)} %copy-done.2, ...), custom_call_target="tpu_custom_call" | custom-call | tf_op jit(solution)/shard_map/pallas_call | solution.py:185
  68.6 1.9 copy.63
  70.5 3.4 %multiply_reduce_fusion = (f32[128]{0:T(128)S(1)}, f32[128,1536]{1,0:T(8,128)S(1)}) fusion(bf16[128,1536]{0,1:T(8,128)(2,1)} %bitcast.120, bf16[1536,1536]{1,0:T(8,128)(2,1)} %param.23, bf16[1,128,1536]{2,1,0:T(8,128)(2,1)S(1)} %copy-done.3), kind=kOutput, calls=%fused_computation.39 | convolution fusion | flops 605159296 | bytes 6291968 | tf_op jit(solution)/shard_map/dot_general | solution.py:298
  73.9 2.8 %convolution_convert_fusion.1 = bf16[1024,1536]{1,0:T(8,128)(2,1)} fusion(pred[1024,128]{1,0:T(8,128)(4,1)S(1)} %fusion.7, f32[128,1536]{1,0:T(8,128)S(1)} %get-tuple-element.20, f32[1536]{0:T(1024)S(1)} %copy-done.5, f32[128]{0:T(128)S(1)} %add_rsqrt_fusion), kind=kOutput, calls=%fused_computation.3 | convolution fusion | flops 404815872 | bytes 4069888 | tf_op jit(solution)/shard_map/dot_general | solution.py:315
  76.7 16.4 %all-to-all-start = ((bf16[32,32,1536]{2,1,0:T(8,128)(2,1)}), bf16[32,32,1536]{2,1,0:T(8,128)(2,1)}, u32[]{:S(2)}, u32[]{:S(2)}) async-start(bf16[32,32,1536]{2,1,0:T(8,128)(2,1)} %bitcast.116), calls=%async_computation | async-start | bytes 6291456 | tf_op jit(solution)/shard_map/all_to_all | solution.py:329
  93.2 4.7 %collective-permute-start.13 = (bf16[1,1536,192]{1,2,0:T(8,128)(2,1)S(1)}, bf16[1,1536,192]{1,2,0:T(8,128)(2,1)S(1)}, u32[]{:S(2)}, u32[]{:S(2)}) collective-permute-start(bf16[1,1536,192]{1,2,0:T(8,128)(2,1)S(1)} %slice.52), channel_id=1, source_target_pairs={{0,3},{1,0},{2,1},{3,2},{4,7},{5,4},{6,5},{7,6},{8,11},{9,8},{10,9... | collective-permute-start | bytes 1769480 | tf_op jit(solution)/shard_map/ppermute | solution.py:208
  100.1 2.7 %collective-permute-start.11 = (bf16[2,768,192]{1,2,0:T(8,128)(2,1)S(1)}, bf16[2,768,192]{1,2,0:T(8,128)(2,1)S(1)}, u32[]{:S(2)}, u32[]{:S(2)}) collective-permute-start(bf16[2,768,192]{1,2,0:T(8,128)(2,1)S(1)} %slice.54), channel_id=1, source_target_pairs={{0,3},{1,0},{2,1},{3,2},{4,7},{5,4},{6,5},{7,6},{8,11},{9,8},{10,9... | collective-permute-start | bytes 1769480 | tf_op jit(solution)/shard_map/ppermute | solution.py:220
  102.9 7.4 %collective-permute-done.13 = bf16[1,1536,192]{1,2,0:T(8,128)(2,1)S(1)} collective-permute-done((bf16[1,1536,192]{1,2,0:T(8,128)(2,1)S(1)}, bf16[1,1536,192]{1,2,0:T(8,128)(2,1)S(1)}, u32[]{:S(2)}, u32[]{:S(2)}) %collective-permute-start.13) | collective-permute-done | bytes 589856 | tf_op jit(solution)/shard_map/ppermute | solution.py:208
  110.3 3.6 %collective-permute-start.14 = (bf16[1,768,192]{1,2,0:T(8,128)(2,1)S(1)}, bf16[1,768,192]{1,2,0:T(8,128)(2,1)S(1)}, u32[]{:S(2)}, u32[]{:S(2)}) collective-permute-start(bf16[1,768,192]{1,2,0:T(8,128)(2,1)S(1)} %slice.68), channel_id=1, source_target_pairs={{0,3},{1,0},{2,1},{3,2},{4,7},{5,4},{6,5},{7,6},{8,11},{9,8},{10,9... | collective-permute-start | bytes 884744 | tf_op jit(solution)/shard_map/ppermute | solution.py:220
  114.0 1.4 maximum_bitcast_fusion
  115.5 1.4 maximum_bitcast_fusion.2
  116.9 12.4 %collective-permute-done.14 = bf16[1,768,192]{1,2,0:T(8,128)(2,1)S(1)} collective-permute-done((bf16[1,768,192]{1,2,0:T(8,128)(2,1)S(1)}, bf16[1,768,192]{1,2,0:T(8,128)(2,1)S(1)}, u32[]{:S(2)}, u32[]{:S(2)}) %collective-permute-start.14) | collective-permute-done | bytes 294944 | tf_op jit(solution)/shard_map/ppermute | solution.py:220
  129.3 3.2 %collective-permute-done.12 = bf16[1,768,192]{1,2,0:T(8,128)(2,1)S(1)} collective-permute-done((bf16[1,768,192]{1,2,0:T(8,128)(2,1)S(1)}, bf16[1,768,192]{1,2,0:T(8,128)(2,1)S(1)}, u32[]{:S(2)}, u32[]{:S(2)}) %collective-permute-start.12) | collective-permute-done | bytes 294944 | tf_op jit(solution)/shard_map/ppermute | solution.py:219
  132.7 3.5 %pad_maximum_fusion = bf16[4,3,1536,192]{2,3,0,1:T(8,128)(2,1)} fusion(bf16[1,3,1536,192]{2,3,0,1:T(8,128)(2,1)S(1)} %maximum_bitcast_fusion.2, bf16[1,3,1536,192]{2,3,0,1:T(8,128)(2,1)S(1)} %maximum_bitcast_fusion.1, bf16[1,3,1536,192]{2,3,0,1:T(8,128)(2,1)S(1)} %maximum_bitcast_fusion, bf16[1,3,1536,192]{2,3,0,1:T(8,128)(2,1)S(1)} %bitcast.115), kind=kLoop, calls=%fused_computation.2 | loop fusion | flops 10616832 | bytes 14155776 | tf_op jit(solution)/shard_map/stack | solution.py:326
  136.1 6.9 %fusion.4 = f32[4,192,1024]{2,1,0:T(8,128)} fusion(bf16[1024,1536,1]{1,0,2:T(8,128)(2,1)} %bitcast.33, bf16[4,3,1536,192]{2,3,0,1:T(8,128)(2,1)} %pad_maximum_fusion), kind=kOutput, calls=%fused_computation.14 | convolution fusion | flops 2415919104 | bytes 8650752 | tf_op jit(solution)/shard_map/nd,hdf->hnf/dot_general | solution.py:333
  143.0 12.0 %fusion = bf16[1024,1536]{1,0:T(8,128)(2,1)} fusion(bf16[4,3,1536,192]{2,3,0,1:T(8,128)(2,1)} %pad_maximum_fusion, f32[4,192,1024]{2,1,0:T(8,128)} %fusion.4, bf16[1024,1536,1]{1,0,2:T(8,128)(2,1)} %bitcast.33), kind=kOutput, calls=%fused_computation.6 | convolution fusion | flops 4845207552 | bytes 14155776 | tf_op jit(solution)/shard_map/hnf,hdf->hnd/dot_general | solution.py:340
  155.0 8.4 %all-to-all-start.1 = ((bf16[32,32,1536]{2,1,0:T(8,128)(2,1)}), bf16[32,32,1536]{2,1,0:T(8,128)(2,1)}, u32[]{:S(2)}, u32[]{:S(2)}) async-start(bf16[32,32,1536]{2,1,0:T(8,128)(2,1)} %bitcast.117), calls=%async_computation.1 | async-start | bytes 6291456 | tf_op jit(solution)/shard_map/all_to_all | solution.py:344
  163.6 1.5 slice_bitcast_fusion.10
  165.4 3.8 %gather_fusion = f32[512]{0:T(512)S(1)} fusion(f32[128,32]{0,1:T(8,128)S(1)} %fusion.37, s32[512]{0:T(512)S(1)} %reshape.190), kind=kCustom, calls=%fused_computation | custom fusion | bytes 8192 | tf_op jit(solution)/shard_map/jit(take_along_axis)/gather | solution.py:352
  169.4 33.7 %all-to-all-done.1 = bf16[32,32,1536]{2,1,0:T(8,128)(2,1)} async-done(((bf16[32,32,1536]{2,1,0:T(8,128)(2,1)}), bf16[32,32,1536]{2,1,0:T(8,128)(2,1)}, u32[]{:S(2)}, u32[]{:S(2)}) %all-to-all-start.1) | async-done | bytes 3145760 | tf_op jit(solution)/shard_map/all_to_all | solution.py:344
  203.1 3.8 %fusion.8 = f32[128,1536]{1,0:T(8,128)S(1)} fusion(bf16[1024,1536,1]{1,0,2:T(8,128)(2,1)} %bitcast.39, f32[128,4]{0,1:T(4,128)S(1)} %multiply_divide_fusion, s32[128,4]{0,1:T(4,128)S(1)} %fusion.34), kind=kOutput, calls=%fused_computation.23 | convolution fusion | flops 1612513280 | bytes 3936256 | tf_op jit(solution)/shard_map/dot_general | solution.py:347
  (70 shorter events, 17.9 us)
Async XLA Ops:
  0.6 164.5 %copy-start = (bf16[1536,32]{0,1:T(8,128)(2,1)S(1)}, bf16[1536,32]{0,1:T(8,128)(2,1)}, u32[]{:S(2)}) copy-start(bf16[1536,32]{0,1:T(8,128)(2,1)} %param.25) | copy-start | bytes 294916
  0.6 20.9 %copy-start.4 = (bf16[1,192,1536]{2,1,0:T(8,128)(2,1)S(1)}, bf16[1,192,1536]{2,1,0:T(8,128)(2,1)}, u32[]{:S(2)}) copy-start(bf16[1,192,1536]{2,1,0:T(8,128)(2,1)} %param.27) | copy-start | bytes 1769476
  2.0 21.0 %copy-start.1 = (bf16[1024,512]{1,0:T(8,128)(2,1)}, bf16[1024,512]{1,0:T(8,128)(2,1)S(1)}, u32[]{:S(2)}) copy-start(bf16[1024,512]{1,0:T(8,128)(2,1)S(1)} %pad_maximum_fusion.2.k0_ref.v0_ref) | copy-start | bytes 3145732
  2.0 26.3 %collective-permute-start.2 = (bf16[1024,512]{1,0:T(8,128)(2,1)S(1)}, bf16[1024,512]{1,0:T(8,128)(2,1)}, u32[]{:S(2)}, u32[]{:S(2)}) collective-permute-start(bf16[1024,512]{1,0:T(8,128)(2,1)S(1)} %pad_maximum_fusion.2.k0_ref.v0_ref), channel_id=1, source_target_pairs={{0,3},{1,0},{2,1},{3,2},{4,7},{5,4},{6,5},{7,6},{8,11},{9,8},{10,9... | collective-permute-start | bytes 3145736 | tf_op jit(solution)/shard_map/ppermute | solution.py:208
  5.4 30.0 %collective-permute-start = (bf16[1024,512]{1,0:T(8,128)(2,1)S(1)}, bf16[1024,512]{1,0:T(8,128)(2,1)}, u32[]{:S(2)}, u32[]{:S(2)}) collective-permute-start(bf16[1024,512]{1,0:T(8,128)(2,1)S(1)} %pad_maximum_fusion.2.k0_ref.v0_ref), channel_id=1, source_target_pairs={{0,1},{1,2},{2,3},{3,0},{4,5},{5,6},{6,7},{7,4},{8,9},{9,10},{10,1... | collective-permute-start | bytes 3145736 | tf_op jit(solution)/shard_map/ppermute | solution.py:208
  9.1 30.3 %collective-permute-start.6 = (bf16[128,512]{1,0:T(8,128)(2,1)}, bf16[128,512]{1,0:T(8,128)(2,1)}, u32[]{:S(2)}, u32[]{:S(2)}) collective-permute-start(bf16[128,512]{1,0:T(8,128)(2,1)} %fusion.16), channel_id=1, source_target_pairs={{0,3},{4,7},{8,11},{12,15},{16,19},{20,23},{24,27},{28,31},{32,35}... | collective-permute-start | bytes 393224 | tf_op jit(solution)/shard_map/ppermute | solution.py:271
  14.4 25.1 %collective-permute-start.5 = (bf16[128,512]{1,0:T(8,128)(2,1)}, bf16[128,512]{1,0:T(8,128)(2,1)}, u32[]{:S(2)}, u32[]{:S(2)}) collective-permute-start(bf16[128,512]{1,0:T(8,128)(2,1)} %fusion.16), channel_id=1, source_target_pairs={{0,2},{1,3},{4,6},{5,7},{8,10},{9,11},{12,14},{13,15},{16,18},{17,... | collective-permute-start | bytes 393224 | tf_op jit(solution)/shard_map/ppermute | solution.py:271
  16.3 23.1 %collective-permute-start.4 = (bf16[128,512]{1,0:T(8,128)(2,1)}, bf16[128,512]{1,0:T(8,128)(2,1)}, u32[]{:S(2)}, u32[]{:S(2)}) collective-permute-start(bf16[128,512]{1,0:T(8,128)(2,1)} %fusion.16), channel_id=1, source_target_pairs={{0,1},{1,2},{2,3},{4,5},{5,6},{6,7},{8,9},{9,10},{10,11},{12,13},{... | collective-permute-start | bytes 393224 | tf_op jit(solution)/shard_map/ppermute | solution.py:271
  30.2 19.3 %collective-permute-start.3 = (bf16[512,512]{1,0:T(8,128)(2,1)}, bf16[512,512]{1,0:T(8,128)(2,1)S(1)}, u32[]{:S(2)}, u32[]{:S(2)}) collective-permute-start(bf16[512,512]{1,0:T(8,128)(2,1)} %slice.65), channel_id=1, source_target_pairs={{0,3},{1,0},{2,1},{3,2},{4,7},{5,4},{6,5},{7,6},{8,11},{9,8},{10,9... | collective-permute-start | bytes 1572872 | tf_op jit(solution)/shard_map/ppermute | solution.py:220
  36.5 11.9 %collective-permute-start.1 = (bf16[512,512]{1,0:T(8,128)(2,1)S(1)}, bf16[512,512]{1,0:T(8,128)(2,1)}, u32[]{:S(2)}, u32[]{:S(2)}) collective-permute-start(bf16[512,512]{1,0:T(8,128)(2,1)S(1)} %slice.64), channel_id=1, source_target_pairs={{0,1},{1,2},{2,3},{3,0},{4,5},{5,6},{6,7},{7,4},{8,9},{9,10},{10,1... | collective-permute-start | bytes 1572872 | tf_op jit(solution)/shard_map/ppermute | solution.py:219
  49.6 3.6 %copy-start.2 = (bf16[1024,512]{1,0:T(8,128)(2,1)}, bf16[1024,512]{1,0:T(8,128)(2,1)S(1)}, u32[]{:S(2)}) copy-start(bf16[1024,512]{1,0:T(8,128)(2,1)S(1)} %constant_dynamic-update-slice_fusion.k2_ref.v2_ref) | copy-start | bytes 3145732
  50.8 25.9 %collective-permute-start.8 = (bf16[2,1536,192]{1,2,0:T(8,128)(2,1)}, bf16[2,1536,192]{1,2,0:T(8,128)(2,1)}, u32[]{:S(2)}, u32[]{:S(2)}) collective-permute-start(bf16[2,1536,192]{1,2,0:T(8,128)(2,1)} %slice.51), channel_id=1, source_target_pairs={{0,3},{1,0},{2,1},{3,2},{4,7},{5,4},{6,5},{7,6},{8,11},{9,8},{10,9... | collective-permute-start | bytes 3538952 | tf_op jit(solution)/shard_map/ppermute | solution.py:208
  50.8 25.9 %collective-permute-start.7 = (bf16[2,1536,192]{1,2,0:T(8,128)(2,1)}, bf16[2,1536,192]{1,2,0:T(8,128)(2,1)}, u32[]{:S(2)}, u32[]{:S(2)}) collective-permute-start(bf16[2,1536,192]{1,2,0:T(8,128)(2,1)} %slice.51), channel_id=1, source_target_pairs={{0,1},{1,2},{2,3},{3,0},{4,5},{5,6},{6,7},{7,4},{8,9},{9,10},{10,1... | collective-permute-start | bytes 3538952 | tf_op jit(solution)/shard_map/ppermute | solution.py:208
  53.2 17.3 %copy-start.3 = (bf16[1,128,1536]{2,1,0:T(8,128)(2,1)S(1)}, bf16[1,128,1536]{2,1,0:T(8,128)(2,1)}, u32[]{:S(2)}) copy-start(bf16[1,128,1536]{2,1,0:T(8,128)(2,1)} %param.14) | copy-start | bytes 1179652
  70.5 3.4 %copy-start.5 = (f32[1536]{0:T(1024)S(1)}, f32[1536]{0:T(1024)}, u32[]{:S(2)}) copy-start(f32[1536]{0:T(1024)} %param.24) | copy-start | bytes 18436
  76.7 59.5 %all-to-all-start = ((bf16[32,32,1536]{2,1,0:T(8,128)(2,1)}), bf16[32,32,1536]{2,1,0:T(8,128)(2,1)}, u32[]{:S(2)}, u32[]{:S(2)}) async-start(bf16[32,32,1536]{2,1,0:T(8,128)(2,1)} %bitcast.116), calls=%async_computation | async-start | bytes 6291456 | tf_op jit(solution)/shard_map/all_to_all | solution.py:329
  93.2 17.1 %collective-permute-start.13 = (bf16[1,1536,192]{1,2,0:T(8,128)(2,1)S(1)}, bf16[1,1536,192]{1,2,0:T(8,128)(2,1)S(1)}, u32[]{:S(2)}, u32[]{:S(2)}) collective-permute-start(bf16[1,1536,192]{1,2,0:T(8,128)(2,1)S(1)} %slice.52), channel_id=1, source_target_pairs={{0,3},{1,0},{2,1},{3,2},{4,7},{5,4},{6,5},{7,6},{8,11},{9,8},{10,9... | collective-permute-start | bytes 1769480 | tf_op jit(solution)/shard_map/ppermute | solution.py:208
  97.9 16.0 %collective-permute-start.9 = (bf16[1,1536,192]{1,2,0:T(8,128)(2,1)S(1)}, bf16[1,1536,192]{1,2,0:T(8,128)(2,1)S(1)}, u32[]{:S(2)}, u32[]{:S(2)}) collective-permute-start(bf16[1,1536,192]{1,2,0:T(8,128)(2,1)S(1)} %slice.52), channel_id=1, source_target_pairs={{0,1},{1,2},{2,3},{3,0},{4,5},{5,6},{6,7},{7,4},{8,9},{9,10},{10,1... | collective-permute-start | bytes 1769480 | tf_op jit(solution)/shard_map/ppermute | solution.py:208
  100.1 32.4 %collective-permute-start.11 = (bf16[2,768,192]{1,2,0:T(8,128)(2,1)S(1)}, bf16[2,768,192]{1,2,0:T(8,128)(2,1)S(1)}, u32[]{:S(2)}, u32[]{:S(2)}) collective-permute-start(bf16[2,768,192]{1,2,0:T(8,128)(2,1)S(1)} %slice.54), channel_id=1, source_target_pairs={{0,3},{1,0},{2,1},{3,2},{4,7},{5,4},{6,5},{7,6},{8,11},{9,8},{10,9... | collective-permute-start | bytes 1769480 | tf_op jit(solution)/shard_map/ppermute | solution.py:220
  102.9 29.6 %collective-permute-start.10 = (bf16[2,768,192]{1,2,0:T(8,128)(2,1)S(1)}, bf16[2,768,192]{1,2,0:T(8,128)(2,1)S(1)}, u32[]{:S(2)}, u32[]{:S(2)}) collective-permute-start(bf16[2,768,192]{1,2,0:T(8,128)(2,1)S(1)} %slice.53), channel_id=1, source_target_pairs={{0,1},{1,2},{2,3},{3,0},{4,5},{5,6},{6,7},{7,4},{8,9},{9,10},{10,1... | collective-permute-start | bytes 1769480 | tf_op jit(solution)/shard_map/ppermute | solution.py:219
  110.3 18.9 %collective-permute-start.14 = (bf16[1,768,192]{1,2,0:T(8,128)(2,1)S(1)}, bf16[1,768,192]{1,2,0:T(8,128)(2,1)S(1)}, u32[]{:S(2)}, u32[]{:S(2)}) collective-permute-start(bf16[1,768,192]{1,2,0:T(8,128)(2,1)S(1)} %slice.68), channel_id=1, source_target_pairs={{0,3},{1,0},{2,1},{3,2},{4,7},{5,4},{6,5},{7,6},{8,11},{9,8},{10,9... | collective-permute-start | bytes 884744 | tf_op jit(solution)/shard_map/ppermute | solution.py:220
  113.9 18.6 %collective-permute-start.12 = (bf16[1,768,192]{1,2,0:T(8,128)(2,1)S(1)}, bf16[1,768,192]{1,2,0:T(8,128)(2,1)S(1)}, u32[]{:S(2)}, u32[]{:S(2)}) collective-permute-start(bf16[1,768,192]{1,2,0:T(8,128)(2,1)S(1)} %slice.67), channel_id=1, source_target_pairs={{0,1},{1,2},{2,3},{3,0},{4,5},{5,6},{6,7},{7,4},{8,9},{9,10},{10,1... | collective-permute-start | bytes 884744 | tf_op jit(solution)/shard_map/ppermute | solution.py:219
  155.0 48.2 %all-to-all-start.1 = ((bf16[32,32,1536]{2,1,0:T(8,128)(2,1)}), bf16[32,32,1536]{2,1,0:T(8,128)(2,1)}, u32[]{:S(2)}, u32[]{:S(2)}) async-start(bf16[32,32,1536]{2,1,0:T(8,128)(2,1)} %bitcast.117), calls=%async_computation.1 | async-start | bytes 6291456 | tf_op jit(solution)/shard_map/all_to_all | solution.py:344

commit v12 on v11

--- a/solution.py
+++ b/solution.py
@@ -14,6 +14,7 @@
 EPS = 1e-06
 MASKED_SCORE = -1e30
 KEY_BLOCK = 512
+LANES = 128
 
 
 def normalize(row_data, gain_vector):
@@ -151,7 +152,10 @@
         if masked:
             s = jnp.where(visible(index, first, size, is_cache), s, MASKED_SCORE)
         s_ref[:, pl.ds(slot(index, first, is_cache), size)] = s
-        m_ref[...] = jnp.maximum(m_ref[...], jnp.max(s, axis=-1, keepdims=True))
+        tile_max = s[:, 0:LANES]
+        for lane in range(LANES, size, LANES):
+            tile_max = jnp.maximum(tile_max, s[:, lane : lane + LANES])
+        m_ref[...] = jnp.maximum(m_ref[...], tile_max)
 
     for index, first, size, is_cache in blocks:
         is_whole = whole(index, first, size, is_cache)
@@ -160,16 +164,21 @@
             functools.partial(first_pass, index, first, size, is_cache, True)
         )
 
+    row_max = jnp.max(m_ref[...], axis=-1, keepdims=True)
+
     for index, first, size, is_cache in blocks:
 
         @pl.when(live(index, first, size, is_cache))
         def _():
-            w = jnp.exp(s_ref[:, pl.ds(slot(index, first, is_cache), size)] - m_ref[...])
-            l_ref[...] += jnp.sum(w, axis=-1, keepdims=True)
+            w = jnp.exp(s_ref[:, pl.ds(slot(index, first, is_cache), size)] - row_max)
+            tile_sum = w[:, 0:LANES]
+            for lane in range(LANES, size, LANES):
+                tile_sum = tile_sum + w[:, lane : lane + LANES]
+            l_ref[...] += tile_sum
             v = v_refs[index][pl.ds(first, size), :] if is_cache else vn_ref[index]
             acc_ref[...] += jnp.dot(w.astype(jnp.bfloat16), v, preferred_element_type=jnp.float32)
 
-    o_ref[0] = (acc_ref[...] / l_ref[...]).astype(o_ref.dtype)
+    o_ref[0] = (acc_ref[...] / jnp.sum(l_ref[...], axis=-1, keepdims=True)).astype(o_ref.dtype)
 
 
 def attention(grouped, shifted_kv, new_kv, length, hid_index, token_count, interpret=False):
@@ -191,8 +200,8 @@
             in_specs=[row_spec] + [k_spec] * parts + [v_spec] * parts + [kn_spec, vn_spec],
             out_specs=row_spec,
             scratch_shapes=[
-                pltpu.VMEM((rows, 1), jnp.float32),
-                pltpu.VMEM((rows, 1), jnp.float32),
+                pltpu.VMEM((rows, LANES), jnp.float32),
+                pltpu.VMEM((rows, LANES), jnp.float32),
                 pltpu.VMEM((rows, head), jnp.float32),
                 pltpu.VMEM((rows, parts * (cache_rows + token_count)), jnp.float32),
             ],

time: 209 us -> 205 us (0.981)
  starting transfers between devices: 55.7 us -> 48.1 us
  Pallas kernels: 15.4 us -> 17.7 us
    all_to_all x1, starting transfers between devices: 16.4 us -> 10.1 us  [body(): lax.all_to_all(send_rows.reshape(expert_count, capacity, model_width), 'r...]
    pallas_call x1, Pallas kernels: 15.4 us -> 17.7 us  [attention(): pl.pallas_call(functools.partial(attention_kernel, token_count), out_shap...]
  transfers between devices with their start and end apart: 17 -> 17, of which waited for: 6 -> 6; matrix products, arithmetic and copies ran while one was open for 19% -> 20% of each run, Pallas kernels for 7% -> 9%
where the time goes in v12:
time: 205 us; the launch traced here: 202 us
  waiting for transfers between devices  69.1 us (34%)
  starting transfers between devices  48.1 us (23%)
  matrix products  31.6 us (15%)
  local copies, waits for them, and re-layouts  18 us (9%)
  Pallas kernels  17.7 us (9%)
  other arithmetic  16.3 us (8%)
    all_to_all x1, waiting for transfers between devices, body(): lax.all_to_all(expert_out.reshape(-1, capacity, model_width), 'req', 0, 0...  33.7 us
    pallas_call x1, Pallas kernels, attention(): pl.pallas_call(functools.partial(attention_kernel, token_count), out_shap...  17.7 us
    ppermute x3, waiting for transfers between devices, ring_neighbours(): lax.ppermute(shard, axis_name, down)  12.8 us
    ppermute x3, waiting for transfers between devices, ring_far(): lax.ppermute(lax.slice_in_dim(from_above, half, extent, axis=split_axis),...  12.4 us
    dot_general x1, matrix products, body(): jnp.einsum('hnf,hdf->hnd', activation, all_weights[:, 2], preferred_eleme...  12 us
    ppermute x3, starting transfers between devices, ring_far(): lax.ppermute(lax.slice_in_dim(from_above, half, extent, axis=split_axis),...  11.5 us
    ppermute x3, waiting for transfers between devices, ring_far(): lax.ppermute(lax.slice_in_dim(from_below, 0, half, axis=split_axis), axis...  10.2 us
    all_to_all x1, starting transfers between devices, body(): lax.all_to_all(send_rows.reshape(expert_count, capacity, model_width), 'r...  10.1 us
  transfers between devices with their start and end apart: 17, of which 6 were waited for; matrix products, arithmetic and copies ran while one was open for 20% of the time, Pallas kernels for 9%

profile of v12, /device:TPU:1, one launch (start us, length us, event | category | flops | bytes accessed | tf_op | source)
XLA Modules:
  0.0 202.3 jit_solution(6996588439927567221)
XLA Ops:
  2.0 3.4 %collective-permute-start.2 = (bf16[1024,512]{1,0:T(8,128)(2,1)S(1)}, bf16[1024,512]{1,0:T(8,128)(2,1)}, u32[]{:S(2)}, u32[]{:S(2)}) collective-permute-start(bf16[1024,512]{1,0:T(8,128)(2,1)S(1)} %pad_maximum_fusion.2.k0_ref.v0_ref), channel_id=1, source_target_pairs={{0,3},{1,0},{2,1},{3,2},{4,7},{5,4},{6,5},{7,6},{8,11},{9,8},{10,9... | collective-permute-start | bytes 3145736 | tf_op jit(solution)/shard_map/ppermute | solution.py:217
  6.5 2.6 %fusion.16 = bf16[128,512]{1,0:T(8,128)(2,1)} fusion(bf16[1536,256]{1,0:T(8,128)(2,1)} %param.22, bf16[1536,256]{1,0:T(8,128)(2,1)} %param.21, bf16[1,128,1536]{2,1,0:T(8,128)(2,1)} %param.14, f32[1536]{0:T(1024)} %param.20, f32[128]{0:T(128)S(1)} %add_rsqrt_fusion.1), kind=kOutput, calls=%fused_computation.31 | convolution fusion | flops 205324288 | bytes 2103808 | tf_op jit(solution)/shard_map/dot_general | solution.py:269
  9.1 5.2 %collective-permute-start.6 = (bf16[128,512]{1,0:T(8,128)(2,1)}, bf16[128,512]{1,0:T(8,128)(2,1)}, u32[]{:S(2)}, u32[]{:S(2)}) collective-permute-start(bf16[128,512]{1,0:T(8,128)(2,1)} %fusion.16), channel_id=1, source_target_pairs={{0,3},{4,7},{8,11},{12,15},{16,19},{20,23},{24,27},{28,31},{32,35}... | collective-permute-start | bytes 393224 | tf_op jit(solution)/shard_map/ppermute | solution.py:280
  14.4 1.9 collective-permute-start.5
  16.3 2.5 %collective-permute-start.4 = (bf16[128,512]{1,0:T(8,128)(2,1)}, bf16[128,512]{1,0:T(8,128)(2,1)}, u32[]{:S(2)}, u32[]{:S(2)}) collective-permute-start(bf16[128,512]{1,0:T(8,128)(2,1)} %fusion.16), channel_id=1, source_target_pairs={{0,1},{1,2},{2,3},{4,5},{5,6},{6,7},{8,9},{9,10},{10,11},{12,13},{... | collective-permute-start | bytes 393224 | tf_op jit(solution)/shard_map/ppermute | solution.py:280
  21.5 1.4 pad_maximum_fusion.1
  23.0 5.4 %collective-permute-done.2.k3_ref.v3_ref = bf16[1024,512]{1,0:T(8,128)(2,1)} collective-permute-done((bf16[1024,512]{1,0:T(8,128)(2,1)S(1)}, bf16[1024,512]{1,0:T(8,128)(2,1)}, u32[]{:S(2)}, u32[]{:S(2)}) %collective-permute-start.2) | collective-permute-done | bytes 1048608 | tf_op jit(solution)/shard_map/ppermute | solution.py:217
  28.4 1.9 slice.65
  30.2 5.2 %collective-permute-start.3 = (bf16[512,512]{1,0:T(8,128)(2,1)}, bf16[512,512]{1,0:T(8,128)(2,1)S(1)}, u32[]{:S(2)}, u32[]{:S(2)}) collective-permute-start(bf16[512,512]{1,0:T(8,128)(2,1)} %slice.65), channel_id=1, source_target_pairs={{0,3},{1,0},{2,1},{3,2},{4,7},{5,4},{6,5},{7,6},{8,11},{9,8},{10,9... | collective-permute-start | bytes 1572872 | tf_op jit(solution)/shard_map/ppermute | solution.py:229
  41.5 7.0 %collective-permute-done.1 = bf16[512,512]{1,0:T(8,128)(2,1)} collective-permute-done((bf16[512,512]{1,0:T(8,128)(2,1)S(1)}, bf16[512,512]{1,0:T(8,128)(2,1)}, u32[]{:S(2)}, u32[]{:S(2)}) %collective-permute-start.1) | collective-permute-done | bytes 524320 | tf_op jit(solution)/shard_map/ppermute | solution.py:228
  50.8 1.5 collective-permute-start.7
  53.2 17.7 %shard_map.157 = bf16[2,768,128]{2,1,0:T(8,128)(2,1)} custom-call(s32[2]{0:T(128)} %pad_add_fusion.scalars, bf16[2,768,128]{2,1,0:T(8,128)(2,1)} %bitcast.118, bf16[1024,512]{1,0:T(8,128)(2,1)} %copy-done.1, bf16[1024,512]{1,0:T(8,128)(2,1)} %collective-permute-done.k1_ref.v1_ref, bf16[1024,512]{1,0:T(8,128)(2,1)} %copy-done.2, ...), custom_call_target="tpu_custom_call" | custom-call | tf_op jit(solution)/shard_map/pallas_call | solution.py:194
  70.9 1.9 copy.63
  72.8 3.4 %multiply_reduce_fusion = (f32[128]{0:T(128)S(1)}, f32[128,1536]{1,0:T(8,128)S(1)}) fusion(bf16[128,1536]{0,1:T(8,128)(2,1)} %bitcast.120, bf16[1536,1536]{1,0:T(8,128)(2,1)} %param.23, bf16[1,128,1536]{2,1,0:T(8,128)(2,1)S(1)} %copy-done.3), kind=kOutput, calls=%fused_computation.39 | convolution fusion | flops 605159296 | bytes 6291968 | tf_op jit(solution)/shard_map/dot_general | solution.py:307
  76.2 2.8 %convolution_convert_fusion.1 = bf16[1024,1536]{1,0:T(8,128)(2,1)} fusion(pred[1024,128]{1,0:T(8,128)(4,1)S(1)} %fusion.7, f32[128,1536]{1,0:T(8,128)S(1)} %get-tuple-element.20, f32[1536]{0:T(1024)S(1)} %copy-done.5, f32[128]{0:T(128)S(1)} %add_rsqrt_fusion), kind=kOutput, calls=%fused_computation.3 | convolution fusion | flops 404815872 | bytes 4069888 | tf_op jit(solution)/shard_map/dot_general | solution.py:324
  79.0 10.1 %all-to-all-start = ((bf16[32,32,1536]{2,1,0:T(8,128)(2,1)}), bf16[32,32,1536]{2,1,0:T(8,128)(2,1)}, u32[]{:S(2)}, u32[]{:S(2)}) async-start(bf16[32,32,1536]{2,1,0:T(8,128)(2,1)} %bitcast.116), calls=%async_computation | async-start | bytes 6291456 | tf_op jit(solution)/shard_map/all_to_all | solution.py:338
  89.1 3.4 %collective-permute-start.13 = (bf16[1,1536,192]{1,2,0:T(8,128)(2,1)S(1)}, bf16[1,1536,192]{1,2,0:T(8,128)(2,1)S(1)}, u32[]{:S(2)}, u32[]{:S(2)}) collective-permute-start(bf16[1,1536,192]{1,2,0:T(8,128)(2,1)S(1)} %slice.52), channel_id=1, source_target_pairs={{0,3},{1,0},{2,1},{3,2},{4,7},{5,4},{6,5},{7,6},{8,11},{9,8},{10,9... | collective-permute-start | bytes 1769480 | tf_op jit(solution)/shard_map/ppermute | solution.py:217
  94.7 2.7 %collective-permute-start.11 = (bf16[2,768,192]{1,2,0:T(8,128)(2,1)S(1)}, bf16[2,768,192]{1,2,0:T(8,128)(2,1)S(1)}, u32[]{:S(2)}, u32[]{:S(2)}) collective-permute-start(bf16[2,768,192]{1,2,0:T(8,128)(2,1)S(1)} %slice.54), channel_id=1, source_target_pairs={{0,3},{1,0},{2,1},{3,2},{4,7},{5,4},{6,5},{7,6},{8,11},{9,8},{10,9... | collective-permute-start | bytes 1769480 | tf_op jit(solution)/shard_map/ppermute | solution.py:229
  97.5 7.4 %collective-permute-done.13 = bf16[1,1536,192]{1,2,0:T(8,128)(2,1)S(1)} collective-permute-done((bf16[1,1536,192]{1,2,0:T(8,128)(2,1)S(1)}, bf16[1,1536,192]{1,2,0:T(8,128)(2,1)S(1)}, u32[]{:S(2)}, u32[]{:S(2)}) %collective-permute-start.13) | collective-permute-done | bytes 589856 | tf_op jit(solution)/shard_map/ppermute | solution.py:217
  104.9 3.6 %collective-permute-start.14 = (bf16[1,768,192]{1,2,0:T(8,128)(2,1)S(1)}, bf16[1,768,192]{1,2,0:T(8,128)(2,1)S(1)}, u32[]{:S(2)}, u32[]{:S(2)}) collective-permute-start(bf16[1,768,192]{1,2,0:T(8,128)(2,1)S(1)} %slice.68), channel_id=1, source_target_pairs={{0,3},{1,0},{2,1},{3,2},{4,7},{5,4},{6,5},{7,6},{8,11},{9,8},{10,9... | collective-permute-start | bytes 884744 | tf_op jit(solution)/shard_map/ppermute | solution.py:229
  108.6 1.4 maximum_bitcast_fusion
  110.0 1.4 maximum_bitcast_fusion.2
  111.5 12.4 %collective-permute-done.14 = bf16[1,768,192]{1,2,0:T(8,128)(2,1)S(1)} collective-permute-done((bf16[1,768,192]{1,2,0:T(8,128)(2,1)S(1)}, bf16[1,768,192]{1,2,0:T(8,128)(2,1)S(1)}, u32[]{:S(2)}, u32[]{:S(2)}) %collective-permute-start.14) | collective-permute-done | bytes 294944 | tf_op jit(solution)/shard_map/ppermute | solution.py:229
  123.9 3.2 %collective-permute-done.12 = bf16[1,768,192]{1,2,0:T(8,128)(2,1)S(1)} collective-permute-done((bf16[1,768,192]{1,2,0:T(8,128)(2,1)S(1)}, bf16[1,768,192]{1,2,0:T(8,128)(2,1)S(1)}, u32[]{:S(2)}, u32[]{:S(2)}) %collective-permute-start.12) | collective-permute-done | bytes 294944 | tf_op jit(solution)/shard_map/ppermute | solution.py:228
  127.2 3.5 %pad_maximum_fusion = bf16[4,3,1536,192]{2,3,0,1:T(8,128)(2,1)} fusion(bf16[1,3,1536,192]{2,3,0,1:T(8,128)(2,1)S(1)} %maximum_bitcast_fusion.2, bf16[1,3,1536,192]{2,3,0,1:T(8,128)(2,1)S(1)} %maximum_bitcast_fusion.1, bf16[1,3,1536,192]{2,3,0,1:T(8,128)(2,1)S(1)} %maximum_bitcast_fusion, bf16[1,3,1536,192]{2,3,0,1:T(8,128)(2,1)S(1)} %bitcast.115), kind=kLoop, calls=%fused_computation.2 | loop fusion | flops 10616832 | bytes 14155776 | tf_op jit(solution)/shard_map/stack | solution.py:335
  130.7 6.9 %fusion.4 = f32[4,192,1024]{2,1,0:T(8,128)} fusion(bf16[1024,1536,1]{1,0,2:T(8,128)(2,1)} %bitcast.33, bf16[4,3,1536,192]{2,3,0,1:T(8,128)(2,1)} %pad_maximum_fusion), kind=kOutput, calls=%fused_computation.14 | convolution fusion | flops 2415919104 | bytes 8650752 | tf_op jit(solution)/shard_map/nd,hdf->hnf/dot_general | solution.py:342
  137.5 12.0 %fusion = bf16[1024,1536]{1,0:T(8,128)(2,1)} fusion(bf16[4,3,1536,192]{2,3,0,1:T(8,128)(2,1)} %pad_maximum_fusion, f32[4,192,1024]{2,1,0:T(8,128)} %fusion.4, bf16[1024,1536,1]{1,0,2:T(8,128)(2,1)} %bitcast.33), kind=kOutput, calls=%fused_computation.6 | convolution fusion | flops 4845207552 | bytes 14155776 | tf_op jit(solution)/shard_map/hnf,hdf->hnd/dot_general | solution.py:349
  149.5 8.4 %all-to-all-start.1 = ((bf16[32,32,1536]{2,1,0:T(8,128)(2,1)}), bf16[32,32,1536]{2,1,0:T(8,128)(2,1)}, u32[]{:S(2)}, u32[]{:S(2)}) async-start(bf16[32,32,1536]{2,1,0:T(8,128)(2,1)} %bitcast.117), calls=%async_computation.1 | async-start | bytes 6291456 | tf_op jit(solution)/shard_map/all_to_all | solution.py:353
  158.1 1.5 slice_bitcast_fusion.10
  160.0 3.8 %gather_fusion = f32[512]{0:T(512)S(1)} fusion(f32[128,32]{0,1:T(8,128)S(1)} %fusion.37, s32[512]{0:T(512)S(1)} %reshape.190), kind=kCustom, calls=%fused_computation | custom fusion | bytes 8192 | tf_op jit(solution)/shard_map/jit(take_along_axis)/gather | solution.py:361
  164.0 33.7 %all-to-all-done.1 = bf16[32,32,1536]{2,1,0:T(8,128)(2,1)} async-done(((bf16[32,32,1536]{2,1,0:T(8,128)(2,1)}), bf16[32,32,1536]{2,1,0:T(8,128)(2,1)}, u32[]{:S(2)}, u32[]{:S(2)}) %all-to-all-start.1) | async-done | bytes 3145760 | tf_op jit(solution)/shard_map/all_to_all | solution.py:353
  197.7 3.8 %fusion.8 = f32[128,1536]{1,0:T(8,128)S(1)} fusion(bf16[1024,1536,1]{1,0,2:T(8,128)(2,1)} %bitcast.39, f32[128,4]{0,1:T(4,128)S(1)} %multiply_divide_fusion, s32[128,4]{0,1:T(4,128)S(1)} %fusion.34), kind=kOutput, calls=%fused_computation.23 | convolution fusion | flops 1612513280 | bytes 3936256 | tf_op jit(solution)/shard_map/dot_general | solution.py:356
  (70 shorter events, 17.9 us)
Async XLA Ops:
  0.6 159.1 %copy-start = (bf16[1536,32]{0,1:T(8,128)(2,1)S(1)}, bf16[1536,32]{0,1:T(8,128)(2,1)}, u32[]{:S(2)}) copy-start(bf16[1536,32]{0,1:T(8,128)(2,1)} %param.25) | copy-start | bytes 294916
  0.6 20.9 %copy-start.4 = (bf16[1,192,1536]{2,1,0:T(8,128)(2,1)S(1)}, bf16[1,192,1536]{2,1,0:T(8,128)(2,1)}, u32[]{:S(2)}) copy-start(bf16[1,192,1536]{2,1,0:T(8,128)(2,1)} %param.27) | copy-start | bytes 1769476
  2.0 21.0 %copy-start.1 = (bf16[1024,512]{1,0:T(8,128)(2,1)}, bf16[1024,512]{1,0:T(8,128)(2,1)S(1)}, u32[]{:S(2)}) copy-start(bf16[1024,512]{1,0:T(8,128)(2,1)S(1)} %pad_maximum_fusion.2.k0_ref.v0_ref) | copy-start | bytes 3145732
  2.0 26.3 %collective-permute-start.2 = (bf16[1024,512]{1,0:T(8,128)(2,1)S(1)}, bf16[1024,512]{1,0:T(8,128)(2,1)}, u32[]{:S(2)}, u32[]{:S(2)}) collective-permute-start(bf16[1024,512]{1,0:T(8,128)(2,1)S(1)} %pad_maximum_fusion.2.k0_ref.v0_ref), channel_id=1, source_target_pairs={{0,3},{1,0},{2,1},{3,2},{4,7},{5,4},{6,5},{7,6},{8,11},{9,8},{10,9... | collective-permute-start | bytes 3145736 | tf_op jit(solution)/shard_map/ppermute | solution.py:217
  5.4 30.0 %collective-permute-start = (bf16[1024,512]{1,0:T(8,128)(2,1)S(1)}, bf16[1024,512]{1,0:T(8,128)(2,1)}, u32[]{:S(2)}, u32[]{:S(2)}) collective-permute-start(bf16[1024,512]{1,0:T(8,128)(2,1)S(1)} %pad_maximum_fusion.2.k0_ref.v0_ref), channel_id=1, source_target_pairs={{0,1},{1,2},{2,3},{3,0},{4,5},{5,6},{6,7},{7,4},{8,9},{9,10},{10,1... | collective-permute-start | bytes 3145736 | tf_op jit(solution)/shard_map/ppermute | solution.py:217
  9.1 30.3 %collective-permute-start.6 = (bf16[128,512]{1,0:T(8,128)(2,1)}, bf16[128,512]{1,0:T(8,128)(2,1)}, u32[]{:S(2)}, u32[]{:S(2)}) collective-permute-start(bf16[128,512]{1,0:T(8,128)(2,1)} %fusion.16), channel_id=1, source_target_pairs={{0,3},{4,7},{8,11},{12,15},{16,19},{20,23},{24,27},{28,31},{32,35}... | collective-permute-start | bytes 393224 | tf_op jit(solution)/shard_map/ppermute | solution.py:280
  14.4 25.1 %collective-permute-start.5 = (bf16[128,512]{1,0:T(8,128)(2,1)}, bf16[128,512]{1,0:T(8,128)(2,1)}, u32[]{:S(2)}, u32[]{:S(2)}) collective-permute-start(bf16[128,512]{1,0:T(8,128)(2,1)} %fusion.16), channel_id=1, source_target_pairs={{0,2},{1,3},{4,6},{5,7},{8,10},{9,11},{12,14},{13,15},{16,18},{17,... | collective-permute-start | bytes 393224 | tf_op jit(solution)/shard_map/ppermute | solution.py:280
  16.3 23.1 %collective-permute-start.4 = (bf16[128,512]{1,0:T(8,128)(2,1)}, bf16[128,512]{1,0:T(8,128)(2,1)}, u32[]{:S(2)}, u32[]{:S(2)}) collective-permute-start(bf16[128,512]{1,0:T(8,128)(2,1)} %fusion.16), channel_id=1, source_target_pairs={{0,1},{1,2},{2,3},{4,5},{5,6},{6,7},{8,9},{9,10},{10,11},{12,13},{... | collective-permute-start | bytes 393224 | tf_op jit(solution)/shard_map/ppermute | solution.py:280
  30.2 19.3 %collective-permute-start.3 = (bf16[512,512]{1,0:T(8,128)(2,1)}, bf16[512,512]{1,0:T(8,128)(2,1)S(1)}, u32[]{:S(2)}, u32[]{:S(2)}) collective-permute-start(bf16[512,512]{1,0:T(8,128)(2,1)} %slice.65), channel_id=1, source_target_pairs={{0,3},{1,0},{2,1},{3,2},{4,7},{5,4},{6,5},{7,6},{8,11},{9,8},{10,9... | collective-permute-start | bytes 1572872 | tf_op jit(solution)/shard_map/ppermute | solution.py:229
  36.5 11.9 %collective-permute-start.1 = (bf16[512,512]{1,0:T(8,128)(2,1)S(1)}, bf16[512,512]{1,0:T(8,128)(2,1)}, u32[]{:S(2)}, u32[]{:S(2)}) collective-permute-start(bf16[512,512]{1,0:T(8,128)(2,1)S(1)} %slice.64), channel_id=1, source_target_pairs={{0,1},{1,2},{2,3},{3,0},{4,5},{5,6},{6,7},{7,4},{8,9},{9,10},{10,1... | collective-permute-start | bytes 1572872 | tf_op jit(solution)/shard_map/ppermute | solution.py:228
  49.6 3.6 %copy-start.2 = (bf16[1024,512]{1,0:T(8,128)(2,1)}, bf16[1024,512]{1,0:T(8,128)(2,1)S(1)}, u32[]{:S(2)}) copy-start(bf16[1024,512]{1,0:T(8,128)(2,1)S(1)} %constant_dynamic-update-slice_fusion.k2_ref.v2_ref) | copy-start | bytes 3145732
  50.8 28.2 %collective-permute-start.8 = (bf16[2,1536,192]{1,2,0:T(8,128)(2,1)}, bf16[2,1536,192]{1,2,0:T(8,128)(2,1)}, u32[]{:S(2)}, u32[]{:S(2)}) collective-permute-start(bf16[2,1536,192]{1,2,0:T(8,128)(2,1)} %slice.51), channel_id=1, source_target_pairs={{0,3},{1,0},{2,1},{3,2},{4,7},{5,4},{6,5},{7,6},{8,11},{9,8},{10,9... | collective-permute-start | bytes 3538952 | tf_op jit(solution)/shard_map/ppermute | solution.py:217
  50.8 28.2 %collective-permute-start.7 = (bf16[2,1536,192]{1,2,0:T(8,128)(2,1)}, bf16[2,1536,192]{1,2,0:T(8,128)(2,1)}, u32[]{:S(2)}, u32[]{:S(2)}) collective-permute-start(bf16[2,1536,192]{1,2,0:T(8,128)(2,1)} %slice.51), channel_id=1, source_target_pairs={{0,1},{1,2},{2,3},{3,0},{4,5},{5,6},{6,7},{7,4},{8,9},{9,10},{10,1... | collective-permute-start | bytes 3538952 | tf_op jit(solution)/shard_map/ppermute | solution.py:217
  53.2 19.6 %copy-start.3 = (bf16[1,128,1536]{2,1,0:T(8,128)(2,1)S(1)}, bf16[1,128,1536]{2,1,0:T(8,128)(2,1)}, u32[]{:S(2)}) copy-start(bf16[1,128,1536]{2,1,0:T(8,128)(2,1)} %param.14) | copy-start | bytes 1179652
  72.8 3.4 %copy-start.5 = (f32[1536]{0:T(1024)S(1)}, f32[1536]{0:T(1024)}, u32[]{:S(2)}) copy-start(f32[1536]{0:T(1024)} %param.24) | copy-start | bytes 18436
  79.0 51.7 %all-to-all-start = ((bf16[32,32,1536]{2,1,0:T(8,128)(2,1)}), bf16[32,32,1536]{2,1,0:T(8,128)(2,1)}, u32[]{:S(2)}, u32[]{:S(2)}) async-start(bf16[32,32,1536]{2,1,0:T(8,128)(2,1)} %bitcast.116), calls=%async_computation | async-start | bytes 6291456 | tf_op jit(solution)/shard_map/all_to_all | solution.py:338
  89.1 15.8 %collective-permute-start.13 = (bf16[1,1536,192]{1,2,0:T(8,128)(2,1)S(1)}, bf16[1,1536,192]{1,2,0:T(8,128)(2,1)S(1)}, u32[]{:S(2)}, u32[]{:S(2)}) collective-permute-start(bf16[1,1536,192]{1,2,0:T(8,128)(2,1)S(1)} %slice.52), channel_id=1, source_target_pairs={{0,3},{1,0},{2,1},{3,2},{4,7},{5,4},{6,5},{7,6},{8,11},{9,8},{10,9... | collective-permute-start | bytes 1769480 | tf_op jit(solution)/shard_map/ppermute | solution.py:217
  92.5 16.0 %collective-permute-start.9 = (bf16[1,1536,192]{1,2,0:T(8,128)(2,1)S(1)}, bf16[1,1536,192]{1,2,0:T(8,128)(2,1)S(1)}, u32[]{:S(2)}, u32[]{:S(2)}) collective-permute-start(bf16[1,1536,192]{1,2,0:T(8,128)(2,1)S(1)} %slice.52), channel_id=1, source_target_pairs={{0,1},{1,2},{2,3},{3,0},{4,5},{5,6},{6,7},{7,4},{8,9},{9,10},{10,1... | collective-permute-start | bytes 1769480 | tf_op jit(solution)/shard_map/ppermute | solution.py:217
  94.7 32.3 %collective-permute-start.11 = (bf16[2,768,192]{1,2,0:T(8,128)(2,1)S(1)}, bf16[2,768,192]{1,2,0:T(8,128)(2,1)S(1)}, u32[]{:S(2)}, u32[]{:S(2)}) collective-permute-start(bf16[2,768,192]{1,2,0:T(8,128)(2,1)S(1)} %slice.54), channel_id=1, source_target_pairs={{0,3},{1,0},{2,1},{3,2},{4,7},{5,4},{6,5},{7,6},{8,11},{9,8},{10,9... | collective-permute-start | bytes 1769480 | tf_op jit(solution)/shard_map/ppermute | solution.py:229
  97.5 29.6 %collective-permute-start.10 = (bf16[2,768,192]{1,2,0:T(8,128)(2,1)S(1)}, bf16[2,768,192]{1,2,0:T(8,128)(2,1)S(1)}, u32[]{:S(2)}, u32[]{:S(2)}) collective-permute-start(bf16[2,768,192]{1,2,0:T(8,128)(2,1)S(1)} %slice.53), channel_id=1, source_target_pairs={{0,1},{1,2},{2,3},{3,0},{4,5},{5,6},{6,7},{7,4},{8,9},{9,10},{10,1... | collective-permute-start | bytes 1769480 | tf_op jit(solution)/shard_map/ppermute | solution.py:228
  104.9 18.9 %collective-permute-start.14 = (bf16[1,768,192]{1,2,0:T(8,128)(2,1)S(1)}, bf16[1,768,192]{1,2,0:T(8,128)(2,1)S(1)}, u32[]{:S(2)}, u32[]{:S(2)}) collective-permute-start(bf16[1,768,192]{1,2,0:T(8,128)(2,1)S(1)} %slice.68), channel_id=1, source_target_pairs={{0,3},{1,0},{2,1},{3,2},{4,7},{5,4},{6,5},{7,6},{8,11},{9,8},{10,9... | collective-permute-start | bytes 884744 | tf_op jit(solution)/shard_map/ppermute | solution.py:229
  108.5 18.5 %collective-permute-start.12 = (bf16[1,768,192]{1,2,0:T(8,128)(2,1)S(1)}, bf16[1,768,192]{1,2,0:T(8,128)(2,1)S(1)}, u32[]{:S(2)}, u32[]{:S(2)}) collective-permute-start(bf16[1,768,192]{1,2,0:T(8,128)(2,1)S(1)} %slice.67), channel_id=1, source_target_pairs={{0,1},{1,2},{2,3},{3,0},{4,5},{5,6},{6,7},{7,4},{8,9},{9,10},{10,1... | collective-permute-start | bytes 884744 | tf_op jit(solution)/shard_map/ppermute | solution.py:228
  149.5 48.2 %all-to-all-start.1 = ((bf16[32,32,1536]{2,1,0:T(8,128)(2,1)}), bf16[32,32,1536]{2,1,0:T(8,128)(2,1)}, u32[]{:S(2)}, u32[]{:S(2)}) async-start(bf16[32,32,1536]{2,1,0:T(8,128)(2,1)} %bitcast.117), calls=%async_computation.1 | async-start | bytes 6291456 | tf_op jit(solution)/shard_map/all_to_all | solution.py:353

commit v13 on v12

--- a/solution.py
+++ b/solution.py
@@ -13,7 +13,7 @@
 
 EPS = 1e-06
 MASKED_SCORE = -1e30
-KEY_BLOCK = 512
+KEY_BLOCK = 1024
 LANES = 128
 
 

time: 205 us -> 202 us (0.985); the launches traced: 202 us -> 202 us
  Pallas kernels: 17.7 us -> 15.2 us
  starting transfers between devices: 48.1 us -> 50.5 us
    pallas_call x1, Pallas kernels: 17.7 us -> 15.2 us  [attention(): pl.pallas_call(functools.partial(attention_kernel, token_count), out_shap...]
    all_to_all x1, starting transfers between devices: 10.1 us -> 12.3 us  [body(): lax.all_to_all(send_rows.reshape(expert_count, capacity, model_width), 'r...]
  transfers between devices with their start and end apart: 17 -> 17, of which waited for: 6 -> 6; matrix products, arithmetic and copies ran while one was open for 20% -> 20% of each run, Pallas kernels for 9% -> 8%
where the time goes in v13:
time: 202 us
  waiting for transfers between devices  69.1 us (34%)
  starting transfers between devices  50.5 us (25%)
  matrix products  31.6 us (16%)
  local copies, waits for them, and re-layouts  18 us (9%)
  other arithmetic  16.3 us (8%)
  Pallas kernels  15.2 us (8%)
    all_to_all x1, waiting for transfers between devices, body(): lax.all_to_all(expert_out.reshape(-1, capacity, model_width), 'req', 0, 0...  33.7 us
    pallas_call x1, Pallas kernels, attention(): pl.pallas_call(functools.partial(attention_kernel, token_count), out_shap...  15.2 us
    ppermute x3, waiting for transfers between devices, ring_neighbours(): lax.ppermute(shard, axis_name, down)  12.8 us
    ppermute x3, waiting for transfers between devices, ring_far(): lax.ppermute(lax.slice_in_dim(from_above, half, extent, axis=split_axis),...  12.4 us
    all_to_all x1, starting transfers between devices, body(): lax.all_to_all(send_rows.reshape(expert_count, capacity, model_width), 'r...  12.3 us
    dot_general x1, matrix products, body(): jnp.einsum('hnf,hdf->hnd', activation, all_weights[:, 2], preferred_eleme...  12 us
    ppermute x3, starting transfers between devices, ring_far(): lax.ppermute(lax.slice_in_dim(from_above, half, extent, axis=split_axis),...  11.5 us
    ppermute x3, waiting for transfers between devices, ring_far(): lax.ppermute(lax.slice_in_dim(from_below, 0, half, axis=split_axis), axis...  10.2 us
  transfers between devices with their start and end apart: 17, of which 6 were waited for; matrix products, arithmetic and copies ran while one was open for 20% of the time, Pallas kernels for 8%

profile of v13, /device:TPU:1, one launch (start us, length us, event | category | flops | bytes accessed | tf_op | source)
XLA Modules:
  0.0 202.3 jit_solution(7575847123839041211)
XLA Ops:
  2.0 3.4 %collective-permute-start.2 = (bf16[1024,512]{1,0:T(8,128)(2,1)S(1)}, bf16[1024,512]{1,0:T(8,128)(2,1)}, u32[]{:S(2)}, u32[]{:S(2)}) collective-permute-start(bf16[1024,512]{1,0:T(8,128)(2,1)S(1)} %pad_maximum_fusion.2.k0_ref.v0_ref), channel_id=1, source_target_pairs={{0,3},{1,0},{2,1},{3,2},{4,7},{5,4},{6,5},{7,6},{8,11},{9,8},{10,9... | collective-permute-start | bytes 3145736 | tf_op jit(solution)/shard_map/ppermute | solution.py:217
  6.5 2.6 %fusion.16 = bf16[128,512]{1,0:T(8,128)(2,1)} fusion(bf16[1536,256]{1,0:T(8,128)(2,1)} %param.22, bf16[1536,256]{1,0:T(8,128)(2,1)} %param.21, bf16[1,128,1536]{2,1,0:T(8,128)(2,1)} %param.14, f32[1536]{0:T(1024)} %param.20, f32[128]{0:T(128)S(1)} %add_rsqrt_fusion.1), kind=kOutput, calls=%fused_computation.31 | convolution fusion | flops 205324288 | bytes 2103808 | tf_op jit(solution)/shard_map/dot_general | solution.py:269
  9.1 5.2 %collective-permute-start.6 = (bf16[128,512]{1,0:T(8,128)(2,1)}, bf16[128,512]{1,0:T(8,128)(2,1)}, u32[]{:S(2)}, u32[]{:S(2)}) collective-permute-start(bf16[128,512]{1,0:T(8,128)(2,1)} %fusion.16), channel_id=1, source_target_pairs={{0,3},{4,7},{8,11},{12,15},{16,19},{20,23},{24,27},{28,31},{32,35}... | collective-permute-start | bytes 393224 | tf_op jit(solution)/shard_map/ppermute | solution.py:280
  14.4 1.9 collective-permute-start.5
  16.3 2.5 %collective-permute-start.4 = (bf16[128,512]{1,0:T(8,128)(2,1)}, bf16[128,512]{1,0:T(8,128)(2,1)}, u32[]{:S(2)}, u32[]{:S(2)}) collective-permute-start(bf16[128,512]{1,0:T(8,128)(2,1)} %fusion.16), channel_id=1, source_target_pairs={{0,1},{1,2},{2,3},{4,5},{5,6},{6,7},{8,9},{9,10},{10,11},{12,13},{... | collective-permute-start | bytes 393224 | tf_op jit(solution)/shard_map/ppermute | solution.py:280
  21.5 1.4 pad_maximum_fusion.1
  23.0 5.4 %collective-permute-done.2.k3_ref.v3_ref = bf16[1024,512]{1,0:T(8,128)(2,1)} collective-permute-done((bf16[1024,512]{1,0:T(8,128)(2,1)S(1)}, bf16[1024,512]{1,0:T(8,128)(2,1)}, u32[]{:S(2)}, u32[]{:S(2)}) %collective-permute-start.2) | collective-permute-done | bytes 1048608 | tf_op jit(solution)/shard_map/ppermute | solution.py:217
  28.4 1.9 slice.65
  30.2 5.2 %collective-permute-start.3 = (bf16[512,512]{1,0:T(8,128)(2,1)}, bf16[512,512]{1,0:T(8,128)(2,1)S(1)}, u32[]{:S(2)}, u32[]{:S(2)}) collective-permute-start(bf16[512,512]{1,0:T(8,128)(2,1)} %slice.65), channel_id=1, source_target_pairs={{0,3},{1,0},{2,1},{3,2},{4,7},{5,4},{6,5},{7,6},{8,11},{9,8},{10,9... | collective-permute-start | bytes 1572872 | tf_op jit(solution)/shard_map/ppermute | solution.py:229
  41.5 7.0 %collective-permute-done.1 = bf16[512,512]{1,0:T(8,128)(2,1)} collective-permute-done((bf16[512,512]{1,0:T(8,128)(2,1)S(1)}, bf16[512,512]{1,0:T(8,128)(2,1)}, u32[]{:S(2)}, u32[]{:S(2)}) %collective-permute-start.1) | collective-permute-done | bytes 524320 | tf_op jit(solution)/shard_map/ppermute | solution.py:228
  50.8 1.5 collective-permute-start.7
  53.2 15.2 %shard_map.157 = bf16[2,768,128]{2,1,0:T(8,128)(2,1)} custom-call(s32[2]{0:T(128)} %pad_add_fusion.scalars, bf16[2,768,128]{2,1,0:T(8,128)(2,1)} %bitcast.118, bf16[1024,512]{1,0:T(8,128)(2,1)} %copy-done.1, bf16[1024,512]{1,0:T(8,128)(2,1)} %collective-permute-done.k1_ref.v1_ref, bf16[1024,512]{1,0:T(8,128)(2,1)} %copy-done.2, ...), custom_call_target="tpu_custom_call" | custom-call | tf_op jit(solution)/shard_map/pallas_call | solution.py:194
  68.4 1.9 copy.63
  70.3 3.4 %multiply_reduce_fusion = (f32[128]{0:T(128)S(1)}, f32[128,1536]{1,0:T(8,128)S(1)}) fusion(bf16[128,1536]{0,1:T(8,128)(2,1)} %bitcast.120, bf16[1536,1536]{1,0:T(8,128)(2,1)} %param.23, bf16[1,128,1536]{2,1,0:T(8,128)(2,1)S(1)} %copy-done.3), kind=kOutput, calls=%fused_computation.39 | convolution fusion | flops 605159296 | bytes 6291968 | tf_op jit(solution)/shard_map/dot_general | solution.py:307
  73.7 2.8 %convolution_convert_fusion.1 = bf16[1024,1536]{1,0:T(8,128)(2,1)} fusion(pred[1024,128]{1,0:T(8,128)(4,1)S(1)} %fusion.7, f32[128,1536]{1,0:T(8,128)S(1)} %get-tuple-element.20, f32[1536]{0:T(1024)S(1)} %copy-done.5, f32[128]{0:T(128)S(1)} %add_rsqrt_fusion), kind=kOutput, calls=%fused_computation.3 | convolution fusion | flops 404815872 | bytes 4069888 | tf_op jit(solution)/shard_map/dot_general | solution.py:324
  76.5 12.3 %all-to-all-start = ((bf16[32,32,1536]{2,1,0:T(8,128)(2,1)}), bf16[32,32,1536]{2,1,0:T(8,128)(2,1)}, u32[]{:S(2)}, u32[]{:S(2)}) async-start(bf16[32,32,1536]{2,1,0:T(8,128)(2,1)} %bitcast.116), calls=%async_computation | async-start | bytes 6291456 | tf_op jit(solution)/shard_map/all_to_all | solution.py:338
  88.9 3.6 %collective-permute-start.13 = (bf16[1,1536,192]{1,2,0:T(8,128)(2,1)S(1)}, bf16[1,1536,192]{1,2,0:T(8,128)(2,1)S(1)}, u32[]{:S(2)}, u32[]{:S(2)}) collective-permute-start(bf16[1,1536,192]{1,2,0:T(8,128)(2,1)S(1)} %slice.52), channel_id=1, source_target_pairs={{0,3},{1,0},{2,1},{3,2},{4,7},{5,4},{6,5},{7,6},{8,11},{9,8},{10,9... | collective-permute-start | bytes 1769480 | tf_op jit(solution)/shard_map/ppermute | solution.py:217
  94.7 2.7 %collective-permute-start.11 = (bf16[2,768,192]{1,2,0:T(8,128)(2,1)S(1)}, bf16[2,768,192]{1,2,0:T(8,128)(2,1)S(1)}, u32[]{:S(2)}, u32[]{:S(2)}) collective-permute-start(bf16[2,768,192]{1,2,0:T(8,128)(2,1)S(1)} %slice.54), channel_id=1, source_target_pairs={{0,3},{1,0},{2,1},{3,2},{4,7},{5,4},{6,5},{7,6},{8,11},{9,8},{10,9... | collective-permute-start | bytes 1769480 | tf_op jit(solution)/shard_map/ppermute | solution.py:229
  97.4 7.4 %collective-permute-done.13 = bf16[1,1536,192]{1,2,0:T(8,128)(2,1)S(1)} collective-permute-done((bf16[1,1536,192]{1,2,0:T(8,128)(2,1)S(1)}, bf16[1,1536,192]{1,2,0:T(8,128)(2,1)S(1)}, u32[]{:S(2)}, u32[]{:S(2)}) %collective-permute-start.13) | collective-permute-done | bytes 589856 | tf_op jit(solution)/shard_map/ppermute | solution.py:217
  104.9 3.6 %collective-permute-start.14 = (bf16[1,768,192]{1,2,0:T(8,128)(2,1)S(1)}, bf16[1,768,192]{1,2,0:T(8,128)(2,1)S(1)}, u32[]{:S(2)}, u32[]{:S(2)}) collective-permute-start(bf16[1,768,192]{1,2,0:T(8,128)(2,1)S(1)} %slice.68), channel_id=1, source_target_pairs={{0,3},{1,0},{2,1},{3,2},{4,7},{5,4},{6,5},{7,6},{8,11},{9,8},{10,9... | collective-permute-start | bytes 884744 | tf_op jit(solution)/shard_map/ppermute | solution.py:229
  108.6 1.4 maximum_bitcast_fusion
  110.0 1.4 maximum_bitcast_fusion.2
  111.4 12.4 %collective-permute-done.14 = bf16[1,768,192]{1,2,0:T(8,128)(2,1)S(1)} collective-permute-done((bf16[1,768,192]{1,2,0:T(8,128)(2,1)S(1)}, bf16[1,768,192]{1,2,0:T(8,128)(2,1)S(1)}, u32[]{:S(2)}, u32[]{:S(2)}) %collective-permute-start.14) | collective-permute-done | bytes 294944 | tf_op jit(solution)/shard_map/ppermute | solution.py:229
  123.8 3.2 %collective-permute-done.12 = bf16[1,768,192]{1,2,0:T(8,128)(2,1)S(1)} collective-permute-done((bf16[1,768,192]{1,2,0:T(8,128)(2,1)S(1)}, bf16[1,768,192]{1,2,0:T(8,128)(2,1)S(1)}, u32[]{:S(2)}, u32[]{:S(2)}) %collective-permute-start.12) | collective-permute-done | bytes 294944 | tf_op jit(solution)/shard_map/ppermute | solution.py:228
  127.2 3.5 %pad_maximum_fusion = bf16[4,3,1536,192]{2,3,0,1:T(8,128)(2,1)} fusion(bf16[1,3,1536,192]{2,3,0,1:T(8,128)(2,1)S(1)} %maximum_bitcast_fusion.2, bf16[1,3,1536,192]{2,3,0,1:T(8,128)(2,1)S(1)} %maximum_bitcast_fusion.1, bf16[1,3,1536,192]{2,3,0,1:T(8,128)(2,1)S(1)} %maximum_bitcast_fusion, bf16[1,3,1536,192]{2,3,0,1:T(8,128)(2,1)S(1)} %bitcast.115), kind=kLoop, calls=%fused_computation.2 | loop fusion | flops 10616832 | bytes 14155776 | tf_op jit(solution)/shard_map/stack | solution.py:335
  130.7 6.9 %fusion.4 = f32[4,192,1024]{2,1,0:T(8,128)} fusion(bf16[1024,1536,1]{1,0,2:T(8,128)(2,1)} %bitcast.33, bf16[4,3,1536,192]{2,3,0,1:T(8,128)(2,1)} %pad_maximum_fusion), kind=kOutput, calls=%fused_computation.14 | convolution fusion | flops 2415919104 | bytes 8650752 | tf_op jit(solution)/shard_map/nd,hdf->hnf/dot_general | solution.py:342
  137.6 12.0 %fusion = bf16[1024,1536]{1,0:T(8,128)(2,1)} fusion(bf16[4,3,1536,192]{2,3,0,1:T(8,128)(2,1)} %pad_maximum_fusion, f32[4,192,1024]{2,1,0:T(8,128)} %fusion.4, bf16[1024,1536,1]{1,0,2:T(8,128)(2,1)} %bitcast.33), kind=kOutput, calls=%fused_computation.6 | convolution fusion | flops 4845207552 | bytes 14155776 | tf_op jit(solution)/shard_map/hnf,hdf->hnd/dot_general | solution.py:349
  149.5 8.4 %all-to-all-start.1 = ((bf16[32,32,1536]{2,1,0:T(8,128)(2,1)}), bf16[32,32,1536]{2,1,0:T(8,128)(2,1)}, u32[]{:S(2)}, u32[]{:S(2)}) async-start(bf16[32,32,1536]{2,1,0:T(8,128)(2,1)} %bitcast.117), calls=%async_computation.1 | async-start | bytes 6291456 | tf_op jit(solution)/shard_map/all_to_all | solution.py:353
  158.1 1.5 slice_bitcast_fusion.10
  159.9 3.8 %gather_fusion = f32[512]{0:T(512)S(1)} fusion(f32[128,32]{0,1:T(8,128)S(1)} %fusion.37, s32[512]{0:T(512)S(1)} %reshape.190), kind=kCustom, calls=%fused_computation | custom fusion | bytes 8192 | tf_op jit(solution)/shard_map/jit(take_along_axis)/gather | solution.py:361
  164.0 33.7 %all-to-all-done.1 = bf16[32,32,1536]{2,1,0:T(8,128)(2,1)} async-done(((bf16[32,32,1536]{2,1,0:T(8,128)(2,1)}), bf16[32,32,1536]{2,1,0:T(8,128)(2,1)}, u32[]{:S(2)}, u32[]{:S(2)}) %all-to-all-start.1) | async-done | bytes 3145760 | tf_op jit(solution)/shard_map/all_to_all | solution.py:353
  197.7 3.8 %fusion.8 = f32[128,1536]{1,0:T(8,128)S(1)} fusion(bf16[1024,1536,1]{1,0,2:T(8,128)(2,1)} %bitcast.39, f32[128,4]{0,1:T(4,128)S(1)} %multiply_divide_fusion, s32[128,4]{0,1:T(4,128)S(1)} %fusion.34), kind=kOutput, calls=%fused_computation.23 | convolution fusion | flops 1612513280 | bytes 3936256 | tf_op jit(solution)/shard_map/dot_general | solution.py:356
  (70 shorter events, 17.9 us)
Async XLA Ops:
  0.6 159.0 %copy-start = (bf16[1536,32]{0,1:T(8,128)(2,1)S(1)}, bf16[1536,32]{0,1:T(8,128)(2,1)}, u32[]{:S(2)}) copy-start(bf16[1536,32]{0,1:T(8,128)(2,1)} %param.25) | copy-start | bytes 294916
  0.6 20.9 %copy-start.4 = (bf16[1,192,1536]{2,1,0:T(8,128)(2,1)S(1)}, bf16[1,192,1536]{2,1,0:T(8,128)(2,1)}, u32[]{:S(2)}) copy-start(bf16[1,192,1536]{2,1,0:T(8,128)(2,1)} %param.27) | copy-start | bytes 1769476
  2.0 21.0 %copy-start.1 = (bf16[1024,512]{1,0:T(8,128)(2,1)}, bf16[1024,512]{1,0:T(8,128)(2,1)S(1)}, u32[]{:S(2)}) copy-start(bf16[1024,512]{1,0:T(8,128)(2,1)S(1)} %pad_maximum_fusion.2.k0_ref.v0_ref) | copy-start | bytes 3145732
  2.0 26.3 %collective-permute-start.2 = (bf16[1024,512]{1,0:T(8,128)(2,1)S(1)}, bf16[1024,512]{1,0:T(8,128)(2,1)}, u32[]{:S(2)}, u32[]{:S(2)}) collective-permute-start(bf16[1024,512]{1,0:T(8,128)(2,1)S(1)} %pad_maximum_fusion.2.k0_ref.v0_ref), channel_id=1, source_target_pairs={{0,3},{1,0},{2,1},{3,2},{4,7},{5,4},{6,5},{7,6},{8,11},{9,8},{10,9... | collective-permute-start | bytes 3145736 | tf_op jit(solution)/shard_map/ppermute | solution.py:217
  5.4 30.0 %collective-permute-start = (bf16[1024,512]{1,0:T(8,128)(2,1)S(1)}, bf16[1024,512]{1,0:T(8,128)(2,1)}, u32[]{:S(2)}, u32[]{:S(2)}) collective-permute-start(bf16[1024,512]{1,0:T(8,128)(2,1)S(1)} %pad_maximum_fusion.2.k0_ref.v0_ref), channel_id=1, source_target_pairs={{0,1},{1,2},{2,3},{3,0},{4,5},{5,6},{6,7},{7,4},{8,9},{9,10},{10,1... | collective-permute-start | bytes 3145736 | tf_op jit(solution)/shard_map/ppermute | solution.py:217
  9.1 30.3 %collective-permute-start.6 = (bf16[128,512]{1,0:T(8,128)(2,1)}, bf16[128,512]{1,0:T(8,128)(2,1)}, u32[]{:S(2)}, u32[]{:S(2)}) collective-permute-start(bf16[128,512]{1,0:T(8,128)(2,1)} %fusion.16), channel_id=1, source_target_pairs={{0,3},{4,7},{8,11},{12,15},{16,19},{20,23},{24,27},{28,31},{32,35}... | collective-permute-start | bytes 393224 | tf_op jit(solution)/shard_map/ppermute | solution.py:280
  14.4 25.1 %collective-permute-start.5 = (bf16[128,512]{1,0:T(8,128)(2,1)}, bf16[128,512]{1,0:T(8,128)(2,1)}, u32[]{:S(2)}, u32[]{:S(2)}) collective-permute-start(bf16[128,512]{1,0:T(8,128)(2,1)} %fusion.16), channel_id=1, source_target_pairs={{0,2},{1,3},{4,6},{5,7},{8,10},{9,11},{12,14},{13,15},{16,18},{17,... | collective-permute-start | bytes 393224 | tf_op jit(solution)/shard_map/ppermute | solution.py:280
  16.3 23.1 %collective-permute-start.4 = (bf16[128,512]{1,0:T(8,128)(2,1)}, bf16[128,512]{1,0:T(8,128)(2,1)}, u32[]{:S(2)}, u32[]{:S(2)}) collective-permute-start(bf16[128,512]{1,0:T(8,128)(2,1)} %fusion.16), channel_id=1, source_target_pairs={{0,1},{1,2},{2,3},{4,5},{5,6},{6,7},{8,9},{9,10},{10,11},{12,13},{... | collective-permute-start | bytes 393224 | tf_op jit(solution)/shard_map/ppermute | solution.py:280
  30.2 19.3 %collective-permute-start.3 = (bf16[512,512]{1,0:T(8,128)(2,1)}, bf16[512,512]{1,0:T(8,128)(2,1)S(1)}, u32[]{:S(2)}, u32[]{:S(2)}) collective-permute-start(bf16[512,512]{1,0:T(8,128)(2,1)} %slice.65), channel_id=1, source_target_pairs={{0,3},{1,0},{2,1},{3,2},{4,7},{5,4},{6,5},{7,6},{8,11},{9,8},{10,9... | collective-permute-start | bytes 1572872 | tf_op jit(solution)/shard_map/ppermute | solution.py:229
  36.5 11.9 %collective-permute-start.1 = (bf16[512,512]{1,0:T(8,128)(2,1)S(1)}, bf16[512,512]{1,0:T(8,128)(2,1)}, u32[]{:S(2)}, u32[]{:S(2)}) collective-permute-start(bf16[512,512]{1,0:T(8,128)(2,1)S(1)} %slice.64), channel_id=1, source_target_pairs={{0,1},{1,2},{2,3},{3,0},{4,5},{5,6},{6,7},{7,4},{8,9},{9,10},{10,1... | collective-permute-start | bytes 1572872 | tf_op jit(solution)/shard_map/ppermute | solution.py:228
  49.6 3.6 %copy-start.2 = (bf16[1024,512]{1,0:T(8,128)(2,1)}, bf16[1024,512]{1,0:T(8,128)(2,1)S(1)}, u32[]{:S(2)}) copy-start(bf16[1024,512]{1,0:T(8,128)(2,1)S(1)} %constant_dynamic-update-slice_fusion.k2_ref.v2_ref) | copy-start | bytes 3145732
  50.8 25.7 %collective-permute-start.8 = (bf16[2,1536,192]{1,2,0:T(8,128)(2,1)}, bf16[2,1536,192]{1,2,0:T(8,128)(2,1)}, u32[]{:S(2)}, u32[]{:S(2)}) collective-permute-start(bf16[2,1536,192]{1,2,0:T(8,128)(2,1)} %slice.51), channel_id=1, source_target_pairs={{0,3},{1,0},{2,1},{3,2},{4,7},{5,4},{6,5},{7,6},{8,11},{9,8},{10,9... | collective-permute-start | bytes 3538952 | tf_op jit(solution)/shard_map/ppermute | solution.py:217
  50.8 25.7 %collective-permute-start.7 = (bf16[2,1536,192]{1,2,0:T(8,128)(2,1)}, bf16[2,1536,192]{1,2,0:T(8,128)(2,1)}, u32[]{:S(2)}, u32[]{:S(2)}) collective-permute-start(bf16[2,1536,192]{1,2,0:T(8,128)(2,1)} %slice.51), channel_id=1, source_target_pairs={{0,1},{1,2},{2,3},{3,0},{4,5},{5,6},{6,7},{7,4},{8,9},{9,10},{10,1... | collective-permute-start | bytes 3538952 | tf_op jit(solution)/shard_map/ppermute | solution.py:217
  53.2 17.1 %copy-start.3 = (bf16[1,128,1536]{2,1,0:T(8,128)(2,1)S(1)}, bf16[1,128,1536]{2,1,0:T(8,128)(2,1)}, u32[]{:S(2)}) copy-start(bf16[1,128,1536]{2,1,0:T(8,128)(2,1)} %param.14) | copy-start | bytes 1179652
  70.3 3.4 %copy-start.5 = (f32[1536]{0:T(1024)S(1)}, f32[1536]{0:T(1024)}, u32[]{:S(2)}) copy-start(f32[1536]{0:T(1024)} %param.24) | copy-start | bytes 18436
  76.5 54.2 %all-to-all-start = ((bf16[32,32,1536]{2,1,0:T(8,128)(2,1)}), bf16[32,32,1536]{2,1,0:T(8,128)(2,1)}, u32[]{:S(2)}, u32[]{:S(2)}) async-start(bf16[32,32,1536]{2,1,0:T(8,128)(2,1)} %bitcast.116), calls=%async_computation | async-start | bytes 6291456 | tf_op jit(solution)/shard_map/all_to_all | solution.py:338
  88.9 16.0 %collective-permute-start.13 = (bf16[1,1536,192]{1,2,0:T(8,128)(2,1)S(1)}, bf16[1,1536,192]{1,2,0:T(8,128)(2,1)S(1)}, u32[]{:S(2)}, u32[]{:S(2)}) collective-permute-start(bf16[1,1536,192]{1,2,0:T(8,128)(2,1)S(1)} %slice.52), channel_id=1, source_target_pairs={{0,3},{1,0},{2,1},{3,2},{4,7},{5,4},{6,5},{7,6},{8,11},{9,8},{10,9... | collective-permute-start | bytes 1769480 | tf_op jit(solution)/shard_map/ppermute | solution.py:217
  92.5 16.0 %collective-permute-start.9 = (bf16[1,1536,192]{1,2,0:T(8,128)(2,1)S(1)}, bf16[1,1536,192]{1,2,0:T(8,128)(2,1)S(1)}, u32[]{:S(2)}, u32[]{:S(2)}) collective-permute-start(bf16[1,1536,192]{1,2,0:T(8,128)(2,1)S(1)} %slice.52), channel_id=1, source_target_pairs={{0,1},{1,2},{2,3},{3,0},{4,5},{5,6},{6,7},{7,4},{8,9},{9,10},{10,1... | collective-permute-start | bytes 1769480 | tf_op jit(solution)/shard_map/ppermute | solution.py:217
  94.7 32.4 %collective-permute-start.11 = (bf16[2,768,192]{1,2,0:T(8,128)(2,1)S(1)}, bf16[2,768,192]{1,2,0:T(8,128)(2,1)S(1)}, u32[]{:S(2)}, u32[]{:S(2)}) collective-permute-start(bf16[2,768,192]{1,2,0:T(8,128)(2,1)S(1)} %slice.54), channel_id=1, source_target_pairs={{0,3},{1,0},{2,1},{3,2},{4,7},{5,4},{6,5},{7,6},{8,11},{9,8},{10,9... | collective-permute-start | bytes 1769480 | tf_op jit(solution)/shard_map/ppermute | solution.py:229
  97.4 29.6 %collective-permute-start.10 = (bf16[2,768,192]{1,2,0:T(8,128)(2,1)S(1)}, bf16[2,768,192]{1,2,0:T(8,128)(2,1)S(1)}, u32[]{:S(2)}, u32[]{:S(2)}) collective-permute-start(bf16[2,768,192]{1,2,0:T(8,128)(2,1)S(1)} %slice.53), channel_id=1, source_target_pairs={{0,1},{1,2},{2,3},{3,0},{4,5},{5,6},{6,7},{7,4},{8,9},{9,10},{10,1... | collective-permute-start | bytes 1769480 | tf_op jit(solution)/shard_map/ppermute | solution.py:228
  104.9 18.9 %collective-permute-start.14 = (bf16[1,768,192]{1,2,0:T(8,128)(2,1)S(1)}, bf16[1,768,192]{1,2,0:T(8,128)(2,1)S(1)}, u32[]{:S(2)}, u32[]{:S(2)}) collective-permute-start(bf16[1,768,192]{1,2,0:T(8,128)(2,1)S(1)} %slice.68), channel_id=1, source_target_pairs={{0,3},{1,0},{2,1},{3,2},{4,7},{5,4},{6,5},{7,6},{8,11},{9,8},{10,9... | collective-permute-start | bytes 884744 | tf_op jit(solution)/shard_map/ppermute | solution.py:229
  108.5 18.6 %collective-permute-start.12 = (bf16[1,768,192]{1,2,0:T(8,128)(2,1)S(1)}, bf16[1,768,192]{1,2,0:T(8,128)(2,1)S(1)}, u32[]{:S(2)}, u32[]{:S(2)}) collective-permute-start(bf16[1,768,192]{1,2,0:T(8,128)(2,1)S(1)} %slice.67), channel_id=1, source_target_pairs={{0,1},{1,2},{2,3},{3,0},{4,5},{5,6},{6,7},{7,4},{8,9},{9,10},{10,1... | collective-permute-start | bytes 884744 | tf_op jit(solution)/shard_map/ppermute | solution.py:228
  149.5 48.2 %all-to-all-start.1 = ((bf16[32,32,1536]{2,1,0:T(8,128)(2,1)}), bf16[32,32,1536]{2,1,0:T(8,128)(2,1)}, u32[]{:S(2)}, u32[]{:S(2)}) async-start(bf16[32,32,1536]{2,1,0:T(8,128)(2,1)} %bitcast.117), calls=%async_computation.1 | async-start | bytes 6291456 | tf_op jit(solution)/shard_map/all_to_all | solution.py:353
